TPU v7x, 256 devices: a whole 4x4x8 slice. The times are simulated.
256 devices in a mesh: pipe: 16 (over y, z_hi, core), expert: 16 (over z_lo, x).
Axes of the slice: x: 4, y: 4, z: 8 (z_hi: 2, z_lo: 4; z = z_hi * 4 + z_lo), core: 2. Of those that a mesh axis runs over, the one named last changes fastest.
Arguments:
- tokens_a: bfloat16 [16, 2048, 2048], P('pipe', 'expert'), may hold values from -6 to 6
- cotangent_a: bfloat16 [16, 2048, 2048], P('pipe', 'expert'), may hold values from -6 to 6
- tokens_b: bfloat16 [16, 2048, 2048], P('pipe', 'expert'), may hold values from -6 to 6
- routes_a: int32 [16, 2048, 2], P('pipe', 'expert'), may hold values from 0 to 15, as said below
- routes_b: int32 [16, 2048, 2], P('pipe', 'expert'), may hold values from 0 to 15, as said below
- probs_a: float32 [16, 2048, 2], P('pipe', 'expert'), may hold values from 0.1 to 0.9
- probs_b: float32 [16, 2048, 2], P('pipe', 'expert'), may hold values from 0.1 to 0.9
- w_gate: bfloat16 [16, 16, 2048, 768], P('pipe', 'expert'), may hold values from -0.125 to 0.125
- w_up: bfloat16 [16, 16, 2048, 768], P('pipe', 'expert'), may hold values from -0.125 to 0.125
- w_down: bfloat16 [16, 16, 768, 2048], P('pipe', 'expert'), may hold values from -0.21875 to 0.21875
Outputs:
- grad_a: bfloat16 [16, 2048, 2048], P('pipe', 'expert')
- grad_b: bfloat16 [16, 2048, 2048], P('pipe', 'expert')
Inputs may be any that keep to these rules, and one draw needn't show every extreme that they name: `routes_a`: in every section one expert, drawn per section, is named exactly 28 times by the 128 tokens of every aligned block of 128 tokens; no block names any expert more than 28 times; the two experts of a token differ. `routes_b`: in every section one expert, drawn per section, is named exactly 28 times by the 128 tokens of every aligned block of 128 tokens; no block names any expert more than 28 times; the two experts of a token differ.
All inputs are finite; a program needn't handle non-finite values.
Results may differ from a plain program's by a relative error of at most 0.0062.
Values may be sent and summed in bfloat16 or wider, within the bound.
No kernel may reach another device: no remote copies, remote signals or barrier semaphores. Data moves between devices by JAX's collectives and lax.ppermute only.
A program may use at most 64 MiB of HBM per device.

v0:
```python
import jax
import jax.numpy as jnp
from jax import lax
from jax.sharding import PartitionSpec as P


def shifted(block, axis, distance):
    devices = range(lax.axis_size(axis))
    route = [((i - distance) % len(devices), i) for i in devices]
    return lax.ppermute(block, axis, route)


def slot_table(routes, experts):
    route_hits = (routes[:, :, None] == jnp.arange(experts, dtype=jnp.int32)[None, None, :]).astype(
        jnp.int32
    )
    per_token = jnp.sum(route_hits, axis=1)
    before = jnp.cumsum(per_token, axis=0) - per_token
    return jnp.sum(route_hits * before[:, None, :], axis=2)


def slot_hits(routes, experts, capacity):
    slot_index = slot_table(routes, experts)
    flat_ids = routes * capacity + slot_index
    targets = jnp.arange(experts * capacity, dtype=jnp.int32)
    hits = (flat_ids[:, :, None] == targets[None, None, :]).astype(jnp.bfloat16)
    return hits.reshape(routes.shape[0], 2, experts, capacity)


def scaled_rows(cotangent, probs):
    return (probs[:, :, None] * cotangent[:, None, :].astype(jnp.float32)).astype(jnp.bfloat16)


def place(hits, rows):
    packed = lax.dot_general(
        hits, rows, (((0, 1), (0, 1)), ((), ())), preferred_element_type=jnp.float32
    )
    return packed.astype(jnp.bfloat16)


def place_tokens(tokens, hits):
    table = jnp.sum(hits, axis=1)
    packed = lax.dot_general(
        table, tokens, (((0,), (0,)), ((), ())), preferred_element_type=jnp.float32
    )
    return packed.astype(jnp.bfloat16)


def recompute(rows, gate_mat, up_mat):
    contract = (((2,), (0,)), ((), ()))
    gate_pre = lax.dot_general(rows, gate_mat, contract, preferred_element_type=jnp.float32)
    up_pre = lax.dot_general(rows, up_mat, contract, preferred_element_type=jnp.float32)
    return (gate_pre, up_pre)


def backprop(gate_pre, up_pre, scaled, gate_mat, up_mat, down_mat):
    contract = (((2,), (1,)), ((), ()))
    d_hidden = lax.dot_general(scaled, down_mat, contract, preferred_element_type=jnp.float32)
    gate_sig = jax.nn.sigmoid(gate_pre)
    active = gate_pre * gate_sig
    slope = gate_sig * (1.0 + gate_pre * (1.0 - gate_sig))
    d_gate = (d_hidden * up_pre * slope).astype(jnp.bfloat16)
    d_up = (d_hidden * active).astype(jnp.bfloat16)
    back = lax.dot_general(d_gate, gate_mat, contract, preferred_element_type=jnp.float32)
    back = back + lax.dot_general(d_up, up_mat, contract, preferred_element_type=jnp.float32)
    return back.astype(jnp.bfloat16)


def exchange(block):
    return lax.all_to_all(block, "expert", split_axis=0, concat_axis=0, tiled=True)


def pick(returned, hits, cotangent):
    table = jnp.sum(hits, axis=1)
    picked = lax.dot_general(
        table, returned, (((1, 2), (0, 1)), ((), ())), preferred_element_type=jnp.float32
    )
    summed = cotangent.astype(jnp.float32) + picked
    return summed.astype(jnp.bfloat16)


def on_device(
    tokens_a, cotangent_a, tokens_b, routes_a, routes_b, probs_a, probs_b, w_gate, w_up, w_down
):
    experts = lax.axis_size("expert")
    tok_count = tokens_a.shape[1]
    width = tokens_a.shape[2]
    capacity = 7 * tok_count // (2 * experts)
    gate_mat = w_gate[0, 0]
    up_mat = w_up[0, 0]
    down_mat = w_down[0, 0]
    first_hits = slot_hits(routes_a[0], experts, capacity)
    second_hits = slot_hits(routes_b[0], experts, capacity)
    first_cot = cotangent_a[0]

    first_rows = jnp.concatenate(
        [
            jnp.broadcast_to(tokens_a[0][:, None, :], (tok_count, 2, width)),
            scaled_rows(first_cot, probs_a[0]),
        ],
        axis=2,
    )
    first_arrived = exchange(place(first_hits, first_rows))
    gate_pre, up_pre = recompute(first_arrived[:, :, :width], gate_mat, up_mat)
    first_back = backprop(
        gate_pre, up_pre, first_arrived[:, :, width:], gate_mat, up_mat, down_mat
    )
    second_tokens = place_tokens(tokens_b[0], second_hits)
    mixed = exchange(jnp.concatenate([first_back, second_tokens], axis=2))
    grad_a = pick(mixed[:, :, :width], first_hits, first_cot)

    second_cot = shifted(grad_a, "pipe", -1)
    second_gate_pre, second_up_pre = recompute(mixed[:, :, width:], gate_mat, up_mat)
    second_scaled = exchange(place(second_hits, scaled_rows(second_cot, probs_b[0])))
    second_back = backprop(
        second_gate_pre, second_up_pre, second_scaled, gate_mat, up_mat, down_mat
    )
    grad_b = pick(exchange(second_back), second_hits, second_cot)
    return (grad_a[None], grad_b[None])


def solution(mesh):
    in_specs = (
        P("pipe", "expert", None),
        P("pipe", "expert", None),
        P("pipe", "expert", None),
        P("pipe", "expert", None),
        P("pipe", "expert", None),
        P("pipe", "expert", None),
        P("pipe", "expert", None),
        P("pipe", "expert", None, None),
        P("pipe", "expert", None, None),
        P("pipe", "expert", None, None),
    )
    out_specs = (P("pipe", "expert", None), P("pipe", "expert", None))
    return jax.shard_map(
        on_device, mesh=mesh, in_specs=in_specs, out_specs=out_specs, check_vma=False
    )
```

profile of v0, /device:TPU:64, one launch (start us, length us, event | category | flops | bytes accessed | tf_op | source)
XLA Modules:
  0.0 386.9 jit_solution(208457819205797592)
XLA Ops:
  0.7 0.8 convert_reduce_fusion.1
  1.5 0.8 convert_reduce_fusion
  2.5 0.2 reduce_window_sum.17
  2.8 0.7 select_reduce_fusion.1
  3.7 0.8 select_reduce_fusion
  4.5 1.1 bitcast_convert_fusion.2
  5.7 0.2 multiply_convert_fusion.1
  6.0 3.3 bitcast_convert_fusion
  9.3 8.0 %all-to-all-start = ((bf16[16,28,4096]{2,1,0:T(8,128)(2,1)}), bf16[16,28,4096]{2,1,0:T(8,128)(2,1)}, u32[]{:S(2)}, u32[]{:S(2)}) async-start(bf16[16,28,4096]{2,1,0:T(8,128)(2,1)} %bitcast_convert_fusion), calls=%async_computation | async-start | bytes 8388608 | tf_op jit(solution)/shard_map/all_to_all | solution.py:70
  17.5 3.1 convolution_convert_fusion
  20.6 90.0 %all-to-all-done = bf16[16,28,4096]{2,1,0:T(8,128)(2,1)} async-done(((bf16[16,28,4096]{2,1,0:T(8,128)(2,1)}), bf16[16,28,4096]{2,1,0:T(8,128)(2,1)}, u32[]{:S(2)}, u32[]{:S(2)}) %all-to-all-start) | async-done | bytes 3670048 | tf_op jit(solution)/shard_map/all_to_all | solution.py:70
  110.6 5.6 %fusion.6 = f32[16,28,768]{2,1,0:T(8,128)} fusion(bf16[1,1,2048,768]{3,2,1,0:T(8,128)(2,1)} %param.17, bf16[16,28,4096]{2,1,0:T(8,128)(2,1)} %all-to-all-done), kind=kOutput, calls=%fused_computation.11 | convolution fusion | flops 1409286144 | bytes 6619136 | tf_op jit(solution)/shard_map/dot_general | solution.py:51
  116.2 4.7 %fusion.10 = f32[16,28,768]{2,1,0:T(8,128)} fusion(bf16[1,1,768,2048]{3,2,1,0:T(8,128)(2,1)S(1)} %copy-done.9, bf16[16,28,4096]{2,1,0:T(8,128)(2,1)} %all-to-all-done), kind=kOutput, calls=%fused_computation.15 | convolution fusion | flops 1409286144 | bytes 6619136 | tf_op jit(solution)/shard_map/dot_general | solution.py:58
  120.9 9.4 %fusion.4 = f32[16,28,2048]{2,1,0:T(8,128)} fusion(bf16[1,1,2048,768]{3,2,1,0:T(8,128)(2,1)} %param.17, f32[16,28,768]{2,1,0:T(8,128)} %fusion.6, f32[16,28,768]{2,1,0:T(8,128)} %fusion.10, bf16[1,1,2048,768]{3,2,1,0:T(8,128)(2,1)S(1)} %copy-done, bf16[16,28,4096]{2,1,0:T(8,128)(2,1)} %all-to-all-done), kind=kOutput, calls=%fused_computation.9 | convolution fusion | flops 2822012928 | bytes 15204352 | tf_op jit(solution)/shard_map/dot_general | solution.py:64
  130.3 5.1 %add_convert_fusion.1 = bf16[16,28,2048]{2,1,0:T(8,128)(2,1)S(1)} fusion(f32[16,28,2048]{2,1,0:T(8,128)} %fusion.4, bf16[1,1,2048,768]{3,2,1,0:T(8,128)(2,1)S(1)} %copy-done, f32[16,28,768]{2,1,0:T(8,128)} %fusion.10, f32[16,28,768]{2,1,0:T(8,128)} %fusion.6), kind=kOutput, calls=%fused_computation.4 | convolution fusion | flops 1413185536 | bytes 11403264 | tf_op jit(solution)/shard_map/dot_general | solution.py:65
  135.5 0.6 pad_maximum_fusion
  136.1 97.9 %all_to_all.20 = bf16[16,28,4096]{2,1,0:T(8,128)(2,1)S(1)} all-to-all(bf16[16,28,4096]{2,1,0:T(8,128)(2,1)S(1)} %pad_maximum_fusion), channel_id=1, replica_groups=mesh['pipe'=16,'expert'=16] {'expert'}, dimensions={0} | all-to-all | bytes 7340032 | tf_op jit(solution)/shard_map/all_to_all | solution.py:70
  234.0 1.9 copy-done.1
  236.0 1.3 fusion.27
  237.2 5.5 %collective-permute-start = (bf16[128,2048]{1,0:T(8,128)(2,1)}, bf16[128,2048]{1,0:T(8,128)(2,1)}, u32[]{:S(2)}, u32[]{:S(2)}) collective-permute-start(bf16[128,2048]{1,0:T(8,128)(2,1)} %fusion.27), channel_id=1, source_target_pairs={{16,0},{32,16},{48,32},{64,48},{80,64},{96,80},{112,96},{128,112},... | collective-permute-start | bytes 1572872 | tf_op jit(solution)/shard_map/ppermute | solution.py:10
  242.9 11.4 %collective-permute-done = bf16[128,2048]{1,0:T(8,128)(2,1)} collective-permute-done((bf16[128,2048]{1,0:T(8,128)(2,1)}, bf16[128,2048]{1,0:T(8,128)(2,1)}, u32[]{:S(2)}, u32[]{:S(2)}) %collective-permute-start) | collective-permute-done | bytes 524320 | tf_op jit(solution)/shard_map/ppermute | solution.py:10
  254.3 1.1 convert_element_type.89
  255.4 0.9 fusion.53
  256.3 2.4 bitcast_convert_fusion.1
  258.7 5.3 %all-to-all-start.2 = ((bf16[16,28,2048]{2,1,0:T(8,128)(2,1)}), bf16[16,28,2048]{2,1,0:T(8,128)(2,1)}, u32[]{:S(2)}, u32[]{:S(2)}) async-start(bf16[16,28,2048]{2,1,0:T(8,128)(2,1)} %bitcast_convert_fusion.1), calls=%async_computation.2 | async-start | bytes 4194304 | tf_op jit(solution)/shard_map/all_to_all | solution.py:70
  264.0 5.5 %fusion.2 = f32[16,28,768]{2,1,0:T(8,128)} fusion(bf16[1,1,2048,768]{3,2,1,0:T(8,128)(2,1)} %param.17, bf16[16,28,4096]{2,1,0:T(8,128)(2,1)} %copy-done.1), kind=kOutput, calls=%fused_computation.7 | convolution fusion | flops 1409286144 | bytes 6619136 | tf_op jit(solution)/shard_map/dot_general | solution.py:51
  269.5 42.7 %all-to-all-done.2 = bf16[16,28,2048]{2,1,0:T(8,128)(2,1)} async-done(((bf16[16,28,2048]{2,1,0:T(8,128)(2,1)}), bf16[16,28,2048]{2,1,0:T(8,128)(2,1)}, u32[]{:S(2)}, u32[]{:S(2)}) %all-to-all-start.2) | async-done | bytes 1835040 | tf_op jit(solution)/shard_map/all_to_all | solution.py:70
  312.2 5.5 %fusion.8 = f32[16,28,768]{2,1,0:T(8,128)} fusion(bf16[16,28,2048]{2,1,0:T(8,128)(2,1)} %all-to-all-done.2, bf16[1,1,768,2048]{3,2,1,0:T(8,128)(2,1)} %param.19), kind=kOutput, calls=%fused_computation.13 | convolution fusion | flops 1409286144 | bytes 6356992 | tf_op jit(solution)/shard_map/dot_general | solution.py:58
  317.7 9.4 %fusion = f32[16,28,2048]{2,1,0:T(8,128)} fusion(bf16[1,1,2048,768]{3,2,1,0:T(8,128)(2,1)} %param.17, f32[16,28,768]{2,1,0:T(8,128)} %fusion.2, f32[16,28,768]{2,1,0:T(8,128)} %fusion.8, bf16[1,1,2048,768]{3,2,1,0:T(8,128)(2,1)S(1)} %copy-done, bf16[16,28,4096]{2,1,0:T(8,128)(2,1)} %copy-done.1), kind=kOutput, calls=%fused_computation.5 | convolution fusion | flops 2822012928 | bytes 15204352 | tf_op jit(solution)/shard_map/dot_general | solution.py:64
  327.1 5.0 %add_convert_fusion = bf16[16,28,2048]{2,1,0:T(8,128)(2,1)S(1)} fusion(f32[16,28,2048]{2,1,0:T(8,128)} %fusion, bf16[1,1,2048,768]{3,2,1,0:T(8,128)(2,1)S(1)} %copy-done, f32[16,28,768]{2,1,0:T(8,128)} %fusion.8, f32[16,28,768]{2,1,0:T(8,128)} %fusion.2), kind=kOutput, calls=%fused_computation.3 | convolution fusion | flops 1413185536 | bytes 11403264 | tf_op jit(solution)/shard_map/dot_general | solution.py:65
  332.1 52.4 %all_to_all.21 = bf16[16,28,2048]{2,1,0:T(8,128)(2,1)S(1)} all-to-all(bf16[16,28,2048]{2,1,0:T(8,128)(2,1)S(1)} %add_convert_fusion), channel_id=1, replica_groups=mesh['pipe'=16,'expert'=16] {'expert'}, dimensions={0} | all-to-all | bytes 3670016 | tf_op jit(solution)/shard_map/all_to_all | solution.py:70
  384.5 2.3 fusion.28
  (31 shorter events, 1.0 us)
Async XLA Ops:
  0.6 120.3 %copy-start = (bf16[1,1,2048,768]{3,2,1,0:T(8,128)(2,1)S(1)}, bf16[1,1,2048,768]{3,2,1,0:T(8,128)(2,1)}, u32[]{:S(2)}) copy-start(bf16[1,1,2048,768]{3,2,1,0:T(8,128)(2,1)} %param.18) | copy-start | bytes 9437188
  0.6 5.0 %copy-start.6 = (s32[1,128,2]{1,2,0:T(2,128)S(1)}, s32[1,128,2]{1,2,0:T(2,128)}, u32[]{:S(2)}) copy-start(s32[1,128,2]{1,2,0:T(2,128)} %param.13) | copy-start | bytes 3076
  0.7 5.0 %copy-start.5 = (s32[1,128,2]{1,2,0:T(2,128)S(1)}, s32[1,128,2]{1,2,0:T(2,128)}, u32[]{:S(2)}) copy-start(s32[1,128,2]{1,2,0:T(2,128)} %param.14) | copy-start | bytes 3076
  0.7 5.0 %copy-start.7 = (f32[1,128,2]{1,2,0:T(2,128)S(1)}, f32[1,128,2]{1,2,0:T(2,128)}, u32[]{:S(2)}) copy-start(f32[1,128,2]{1,2,0:T(2,128)} %param.15) | copy-start | bytes 3076
  3.7 2.2 copy-start.4
  9.3 101.4 %all-to-all-start = ((bf16[16,28,4096]{2,1,0:T(8,128)(2,1)}), bf16[16,28,4096]{2,1,0:T(8,128)(2,1)}, u32[]{:S(2)}, u32[]{:S(2)}) async-start(bf16[16,28,4096]{2,1,0:T(8,128)(2,1)} %bitcast_convert_fusion), calls=%async_computation | async-start | bytes 8388608 | tf_op jit(solution)/shard_map/all_to_all | solution.py:70
  110.6 5.6 %copy-start.9 = (bf16[1,1,768,2048]{3,2,1,0:T(8,128)(2,1)S(1)}, bf16[1,1,768,2048]{3,2,1,0:T(8,128)(2,1)}, u32[]{:S(2)}) copy-start(bf16[1,1,768,2048]{3,2,1,0:T(8,128)(2,1)} %param.19) | copy-start | bytes 9437188
  130.3 5.1 %copy-start.2 = (bf16[16,28,2048]{2,1,0:T(8,128)(2,1)S(1)}, bf16[16,28,2048]{2,1,0:T(8,128)(2,1)}, u32[]{:S(2)}) copy-start(bf16[16,28,2048]{2,1,0:T(8,128)(2,1)} %convolution_convert_fusion) | copy-start | bytes 5505028
  136.1 99.9 %copy-start.3 = (bf16[1,128,2048]{2,1,0:T(8,128)(2,1)S(1)}, bf16[1,128,2048]{2,1,0:T(8,128)(2,1)}, u32[]{:S(2)}) copy-start(bf16[1,128,2048]{2,1,0:T(8,128)(2,1)} %param.11) | copy-start | bytes 1572868
  234.0 1.9 copy-start.1
  234.0 8.7 %copy-start.8 = (f32[1,128,2]{1,2,0:T(2,128)S(1)}, f32[1,128,2]{1,2,0:T(2,128)}, u32[]{:S(2)}) copy-start(f32[1,128,2]{1,2,0:T(2,128)} %param.16) | copy-start | bytes 3076
  237.2 17.1 %collective-permute-start = (bf16[128,2048]{1,0:T(8,128)(2,1)}, bf16[128,2048]{1,0:T(8,128)(2,1)}, u32[]{:S(2)}, u32[]{:S(2)}) collective-permute-start(bf16[128,2048]{1,0:T(8,128)(2,1)} %fusion.27), channel_id=1, source_target_pairs={{16,0},{32,16},{48,32},{64,48},{80,64},{96,80},{112,96},{128,112},... | collective-permute-start | bytes 1572872 | tf_op jit(solution)/shard_map/ppermute | solution.py:10
  258.7 53.5 %all-to-all-start.2 = ((bf16[16,28,2048]{2,1,0:T(8,128)(2,1)}), bf16[16,28,2048]{2,1,0:T(8,128)(2,1)}, u32[]{:S(2)}, u32[]{:S(2)}) async-start(bf16[16,28,2048]{2,1,0:T(8,128)(2,1)} %bitcast_convert_fusion.1), calls=%async_computation.2 | async-start | bytes 4194304 | tf_op jit(solution)/shard_map/all_to_all | solution.py:70
where the time goes:
time: 389 us; the launch traced here: 387 us
  blocking collectives  150 us (39%)
  waiting for transfers between devices  144 us (37%)
  matrix products  62.6 us (16%)
  starting transfers between devices  18.9 us (5%)
  other arithmetic  7.63 us (2%)
    all_to_all x2, blocking collectives, exchange(): lax.all_to_all(block, 'expert', split_axis=0, concat_axis=0, tiled=True)  150 us
    all_to_all x2, waiting for transfers between devices, exchange(): lax.all_to_all(block, 'expert', split_axis=0, concat_axis=0, tiled=True)  133 us
    dot_general x2, matrix products, backprop(): lax.dot_general(d_gate, gate_mat, contract, preferred_element_type=jnp.fl...  18.8 us
    all_to_all x2, starting transfers between devices, exchange(): lax.all_to_all(block, 'expert', split_axis=0, concat_axis=0, tiled=True)  13.3 us
    ppermute x1, waiting for transfers between devices, shifted(): return lax.ppermute(block, axis, route)  11.4 us
    dot_general x2, matrix products, recompute(): lax.dot_general(rows, gate_mat, contract, preferred_element_type=jnp.floa...  11.1 us
    dot_general x2, matrix products, backprop(): lax.dot_general(scaled, down_mat, contract, preferred_element_type=jnp.fl...  10.2 us
    dot_general x2, matrix products, backprop(): lax.dot_general(d_up, up_mat, contract, preferred_element_type=jnp.float32)  10.1 us
  transfers between devices with their start and end apart: 3, of which 3 were waited for; matrix products, arithmetic and copies ran while one was open for 2% of the time, Pallas kernels for 0%

commit v1 on v0

--- a/solution.py
+++ b/solution.py
@@ -79,43 +79,71 @@
     return summed.astype(jnp.bfloat16)
 
 
+def back_half(d_gate, d_up, gate_mat, up_mat):
+    contract = (((2,), (1,)), ((), ()))
+    back = lax.dot_general(d_gate, gate_mat, contract, preferred_element_type=jnp.float32)
+    back = back + lax.dot_general(d_up, up_mat, contract, preferred_element_type=jnp.float32)
+    return back.astype(jnp.bfloat16)
+
+
+def hidden_grads(gate_pre, up_pre, scaled, down_mat):
+    contract = (((2,), (1,)), ((), ()))
+    d_hidden = lax.dot_general(scaled, down_mat, contract, preferred_element_type=jnp.float32)
+    gate_sig = jax.nn.sigmoid(gate_pre)
+    active = gate_pre * gate_sig
+    slope = gate_sig * (1.0 + gate_pre * (1.0 - gate_sig))
+    d_gate = (d_hidden * up_pre * slope).astype(jnp.bfloat16)
+    d_up = (d_hidden * active).astype(jnp.bfloat16)
+    return d_gate, d_up
+
+
+def pick_cols(returned, table):
+    return lax.dot_general(
+        table, returned, (((1, 2), (0, 1)), ((), ())), preferred_element_type=jnp.float32
+    )
+
+
 def on_device(
     tokens_a, cotangent_a, tokens_b, routes_a, routes_b, probs_a, probs_b, w_gate, w_up, w_down
 ):
     experts = lax.axis_size("expert")
     tok_count = tokens_a.shape[1]
     width = tokens_a.shape[2]
+    half = width // 2
     capacity = 7 * tok_count // (2 * experts)
     gate_mat = w_gate[0, 0]
     up_mat = w_up[0, 0]
     down_mat = w_down[0, 0]
     first_hits = slot_hits(routes_a[0], experts, capacity)
     second_hits = slot_hits(routes_b[0], experts, capacity)
+    first_table = jnp.sum(first_hits, axis=1)
+    second_table = jnp.sum(second_hits, axis=1)
     first_cot = cotangent_a[0]
 
-    first_rows = jnp.concatenate(
-        [
-            jnp.broadcast_to(tokens_a[0][:, None, :], (tok_count, 2, width)),
-            scaled_rows(first_cot, probs_a[0]),
-        ],
-        axis=2,
+    first_tokens = exchange(place_tokens(tokens_a[0], first_hits))
+    first_scaled = exchange(place(first_hits, scaled_rows(first_cot, probs_a[0])))
+    gate_pre, up_pre = recompute(first_tokens, gate_mat, up_mat)
+    d_gate, d_up = hidden_grads(gate_pre, up_pre, first_scaled, down_mat)
+    lead = exchange(back_half(d_gate, d_up, gate_mat[:half], up_mat[:half]))
+    second_tokens = place_tokens(tokens_b[0], second_hits)
+    mixed = exchange(
+        jnp.concatenate([back_half(d_gate, d_up, gate_mat[half:], up_mat[half:]), second_tokens], axis=2)
     )
-    first_arrived = exchange(place(first_hits, first_rows))
-    gate_pre, up_pre = recompute(first_arrived[:, :, :width], gate_mat, up_mat)
-    first_back = backprop(
-        gate_pre, up_pre, first_arrived[:, :, width:], gate_mat, up_mat, down_mat
+    picked = jnp.concatenate(
+        [pick_cols(lead, first_table), pick_cols(mixed[:, :, :half], first_table)], axis=1
     )
-    second_tokens = place_tokens(tokens_b[0], second_hits)
-    mixed = exchange(jnp.concatenate([first_back, second_tokens], axis=2))
-    grad_a = pick(mixed[:, :, :width], first_hits, first_cot)
+    grad_a = (first_cot.astype(jnp.float32) + picked).astype(jnp.bfloat16)
 
     second_cot = shifted(grad_a, "pipe", -1)
-    second_gate_pre, second_up_pre = recompute(mixed[:, :, width:], gate_mat, up_mat)
+    gate_pre, up_pre = recompute(mixed[:, :, half:], gate_mat, up_mat)
     second_scaled = exchange(place(second_hits, scaled_rows(second_cot, probs_b[0])))
-    second_back = backprop(
-        second_gate_pre, second_up_pre, second_scaled, gate_mat, up_mat, down_mat
+    d_gate, d_up = hidden_grads(gate_pre, up_pre, second_scaled, down_mat)
+    lead = exchange(back_half(d_gate, d_up, gate_mat[:half], up_mat[:half]))
+    trail = exchange(back_half(d_gate, d_up, gate_mat[half:], up_mat[half:]))
+    picked = jnp.concatenate(
+        [pick_cols(lead, second_table), pick_cols(trail, second_table)], axis=1
     )
-    grad_b = pick(exchange(second_back), second_hits, second_cot)
+    grad_b = (second_cot.astype(jnp.float32) + picked).astype(jnp.bfloat16)
     return (grad_a[None], grad_b[None])
 
 

time: 389 us -> 393 us (1.010)
  blocking collectives: 150 us -> 0 us
  waiting for transfers between devices: 144 us -> 262 us
  starting transfers between devices: 18.9 us -> 50.4 us
  other arithmetic: 7.63 us -> 16.5 us
    all_to_all x2 -> x0, blocking collectives: 150 us -> none  [exchange(): lax.all_to_all(block, 'expert', split_axis=0, concat_axis=0, tiled=True)]
    all_to_all x2 -> x7, waiting for transfers between devices: 133 us -> 255 us  [exchange(): lax.all_to_all(block, 'expert', split_axis=0, concat_axis=0, tiled=True)]
    all_to_all x2 -> x7, starting transfers between devices: 13.3 us -> 46.3 us  [exchange(): lax.all_to_all(block, 'expert', split_axis=0, concat_axis=0, tiled=True)]
    ppermute x1, waiting for transfers between devices: 11.4 us -> 6.9 us  [shifted(): return lax.ppermute(block, axis, route)]
    dot_general x8 -> x16, matrix products: 42.7 us -> 38.4 us  [the longest x2 8.2 us: hidden_grads(): lax.dot_general(scaled, down_mat, contract, preferred_element_type=jnp.fl...]
  transfers between devices with their start and end apart: 3 -> 8, of which waited for: 3 -> 8; matrix products, arithmetic and copies ran while one was open for 2% -> 9% of each run, Pallas kernels for 0% -> 0%
where the time goes in v1:
time: 393 us; the launch traced here: 392 us
  waiting for transfers between devices  262 us (67%)
  matrix products  59.1 us (15%)
  starting transfers between devices  50.4 us (13%)
  other arithmetic  16.5 us (4%)
    all_to_all x7, waiting for transfers between devices, exchange(): lax.all_to_all(block, 'expert', split_axis=0, concat_axis=0, tiled=True)  255 us
    all_to_all x7, starting transfers between devices, exchange(): lax.all_to_all(block, 'expert', split_axis=0, concat_axis=0, tiled=True)  46.3 us
    dot_general x2, matrix products, recompute(): lax.dot_general(rows, gate_mat, contract, preferred_element_type=jnp.floa...  11 us
    dot_general x2, matrix products, hidden_grads(): lax.dot_general(scaled, down_mat, contract, preferred_element_type=jnp.fl...  8.2 us
    dot_general x4, matrix products, pick_cols(): lax.dot_general(table, returned, (((1, 2), (0, 1)), ((), ())), preferred_...  8.03 us
  transfers between devices with their start and end apart: 8, of which 8 were waited for; matrix products, arithmetic and copies ran while one was open for 9% of the time, Pallas kernels for 0%

profile of v1, /device:TPU:64, one launch (start us, length us, event | category | flops | bytes accessed | tf_op | source)
XLA Modules:
  0.0 392.0 jit_solution(1369849794791764823)
XLA Ops:
  5.7 3.0 convolution_convert_fusion.1
  8.8 8.2 %all-to-all-start.1 = ((bf16[16,28,2048]{2,1,0:T(8,128)(2,1)}), bf16[16,28,2048]{2,1,0:T(8,128)(2,1)}, u32[]{:S(2)}, u32[]{:S(2)}) async-start(bf16[16,28,2048]{2,1,0:T(8,128)(2,1)} %convolution_convert_fusion.1), calls=%async_computation.1 | async-start | bytes 4194304 | tf_op jit(solution)/shard_map/all_to_all | solution.py:70
  20.0 2.4 bitcast_convert_fusion.1
  22.4 42.9 %all-to-all-done.1 = bf16[16,28,2048]{2,1,0:T(8,128)(2,1)} async-done(((bf16[16,28,2048]{2,1,0:T(8,128)(2,1)}), bf16[16,28,2048]{2,1,0:T(8,128)(2,1)}, u32[]{:S(2)}, u32[]{:S(2)}) %all-to-all-start.1) | async-done | bytes 1835040 | tf_op jit(solution)/shard_map/all_to_all | solution.py:70
  65.3 5.1 %all-to-all-start = ((bf16[16,28,2048]{2,1,0:T(8,128)(2,1)}), bf16[16,28,2048]{2,1,0:T(8,128)(2,1)}, u32[]{:S(2)}, u32[]{:S(2)}) async-start(bf16[16,28,2048]{2,1,0:T(8,128)(2,1)} %bitcast_convert_fusion.1), calls=%async_computation | async-start | bytes 4194304 | tf_op jit(solution)/shard_map/all_to_all | solution.py:70
  70.4 5.5 %fusion.2 = f32[16,28,768]{2,1,0:T(8,128)} fusion(bf16[16,28,2048]{2,1,0:T(8,128)(2,1)} %all-to-all-done.1, bf16[1,1,2048,768]{3,2,1,0:T(8,128)(2,1)} %param.17), kind=kOutput, calls=%fused_computation.5 | convolution fusion | flops 1409286144 | bytes 6356992 | tf_op jit(solution)/shard_map/dot_general | solution.py:51
  75.9 42.0 %all-to-all-done = bf16[16,28,2048]{2,1,0:T(8,128)(2,1)} async-done(((bf16[16,28,2048]{2,1,0:T(8,128)(2,1)}), bf16[16,28,2048]{2,1,0:T(8,128)(2,1)}, u32[]{:S(2)}, u32[]{:S(2)}) %all-to-all-start) | async-done | bytes 1835040 | tf_op jit(solution)/shard_map/all_to_all | solution.py:70
  118.0 4.1 %multiply_convert_fusion.4 = (bf16[16,28,768]{2,1,0:T(8,128)(2,1)S(1)}, f32[16,28,768]{2,1,0:T(8,128)S(1)}) fusion(f32[16,28,768]{2,1,0:T(8,128)} %fusion.2, bf16[16,28,2048]{2,1,0:T(8,128)(2,1)} %all-to-all-done, bf16[1,1,768,2048]{3,2,1,0:T(8,128)(2,1)S(1)} %copy-done), kind=kOutput, calls=%fused_computation.40 | convolution fusion | flops 1411350528 | bytes 8421376 | tf_op jit(solution)/shard_map/dot_general | solution.py:91
  122.1 3.9 multiply_convert_fusion.5
  129.1 5.1 %all-to-all-start.2 = ((bf16[16,28,1024]{2,1,0:T(8,128)(2,1)}), bf16[16,28,1024]{2,1,0:T(8,128)(2,1)}, u32[]{:S(2)}, u32[]{:S(2)}) async-start(bf16[16,28,1024]{2,1,0:T(8,128)(2,1)} %add_convert_fusion.3), calls=%async_computation.2 | async-start | bytes 2097152 | tf_op jit(solution)/shard_map/all_to_all | solution.py:70
  136.1 2.6 fusion.18
  139.7 2.1 pad_maximum_fusion
  141.8 17.4 %all-to-all-done.2 = bf16[16,28,1024]{2,1,0:T(8,128)(2,1)} async-done(((bf16[16,28,1024]{2,1,0:T(8,128)(2,1)}), bf16[16,28,1024]{2,1,0:T(8,128)(2,1)}, u32[]{:S(2)}, u32[]{:S(2)}) %all-to-all-start.2) | async-done | bytes 917536 | tf_op jit(solution)/shard_map/all_to_all | solution.py:70
  159.2 5.1 %all-to-all-start.3 = ((bf16[16,28,3072]{2,1,0:T(8,128)(2,1)}), bf16[16,28,3072]{2,1,0:T(8,128)(2,1)}, u32[]{:S(2)}, u32[]{:S(2)}) async-start(bf16[16,28,3072]{2,1,0:T(8,128)(2,1)} %pad_maximum_fusion), calls=%async_computation.3 | async-start | bytes 6291456 | tf_op jit(solution)/shard_map/all_to_all | solution.py:70
  164.3 2.7 fusion.51
  167.0 67.2 %all-to-all-done.3 = bf16[16,28,3072]{2,1,0:T(8,128)(2,1)} async-done(((bf16[16,28,3072]{2,1,0:T(8,128)(2,1)}), bf16[16,28,3072]{2,1,0:T(8,128)(2,1)}, u32[]{:S(2)}, u32[]{:S(2)}) %all-to-all-start.3) | async-done | bytes 2752544 | tf_op jit(solution)/shard_map/all_to_all | solution.py:70
  237.3 4.1 %collective-permute-start = (bf16[128,2048]{1,0:T(8,128)(2,1)}, bf16[128,2048]{1,0:T(8,128)(2,1)}, u32[]{:S(2)}, u32[]{:S(2)}) collective-permute-start(bf16[128,2048]{1,0:T(8,128)(2,1)} %fusion.43), channel_id=1, source_target_pairs={{16,0},{32,16},{48,32},{64,48},{80,64},{96,80},{112,96},{128,112},... | collective-permute-start | bytes 1572872 | tf_op jit(solution)/shard_map/ppermute | solution.py:10
  241.5 6.9 %collective-permute-done = bf16[128,2048]{1,0:T(8,128)(2,1)} collective-permute-done((bf16[128,2048]{1,0:T(8,128)(2,1)}, bf16[128,2048]{1,0:T(8,128)(2,1)}, u32[]{:S(2)}, u32[]{:S(2)}) %collective-permute-start) | collective-permute-done | bytes 524320 | tf_op jit(solution)/shard_map/ppermute | solution.py:10
  250.5 2.4 bitcast_convert_fusion
  252.8 12.2 %all-to-all-start.4 = ((bf16[16,28,2048]{2,1,0:T(8,128)(2,1)}), bf16[16,28,2048]{2,1,0:T(8,128)(2,1)}, u32[]{:S(2)}, u32[]{:S(2)}) async-start(bf16[16,28,2048]{2,1,0:T(8,128)(2,1)} %bitcast_convert_fusion), calls=%async_computation.4 | async-start | bytes 4194304 | tf_op jit(solution)/shard_map/all_to_all | solution.py:70
  265.1 5.6 %fusion = f32[16,28,768]{2,1,0:T(8,128)} fusion(bf16[1,1,2048,768]{3,2,1,0:T(8,128)(2,1)} %param.17, bf16[16,28,3072]{2,1,0:T(8,128)(2,1)} %all-to-all-done.3), kind=kOutput, calls=%fused_computation.3 | convolution fusion | flops 1409286144 | bytes 6619136 | tf_op jit(solution)/shard_map/dot_general | solution.py:51
  270.6 42.7 %all-to-all-done.4 = bf16[16,28,2048]{2,1,0:T(8,128)(2,1)} async-done(((bf16[16,28,2048]{2,1,0:T(8,128)(2,1)}), bf16[16,28,2048]{2,1,0:T(8,128)(2,1)}, u32[]{:S(2)}, u32[]{:S(2)}) %all-to-all-start.4) | async-done | bytes 1835040 | tf_op jit(solution)/shard_map/all_to_all | solution.py:70
  313.3 4.1 %multiply_convert_fusion.2 = (bf16[16,28,768]{2,1,0:T(8,128)(2,1)S(1)}, f32[16,28,768]{2,1,0:T(8,128)S(1)}) fusion(f32[16,28,768]{2,1,0:T(8,128)} %fusion, bf16[16,28,2048]{2,1,0:T(8,128)(2,1)} %all-to-all-done.4, bf16[1,1,768,2048]{3,2,1,0:T(8,128)(2,1)S(1)} %copy-done), kind=kOutput, calls=%fused_computation.37 | convolution fusion | flops 1411350528 | bytes 8421376 | tf_op jit(solution)/shard_map/dot_general | solution.py:91
  317.5 3.9 multiply_convert_fusion.3
  324.5 5.5 %all-to-all-start.6 = ((bf16[16,28,1024]{2,1,0:T(8,128)(2,1)}), bf16[16,28,1024]{2,1,0:T(8,128)(2,1)}, u32[]{:S(2)}, u32[]{:S(2)}) async-start(bf16[16,28,1024]{2,1,0:T(8,128)(2,1)} %add_convert_fusion), calls=%async_computation.6 | async-start | bytes 2097152 | tf_op jit(solution)/shard_map/all_to_all | solution.py:70
  330.0 2.8 fusion.22
  334.8 22.2 %all-to-all-done.6 = bf16[16,28,1024]{2,1,0:T(8,128)(2,1)} async-done(((bf16[16,28,1024]{2,1,0:T(8,128)(2,1)}), bf16[16,28,1024]{2,1,0:T(8,128)(2,1)}, u32[]{:S(2)}, u32[]{:S(2)}) %all-to-all-start.6) | async-done | bytes 917536 | tf_op jit(solution)/shard_map/all_to_all | solution.py:70
  357.0 5.1 %all-to-all-start.5 = ((bf16[16,28,1024]{2,1,0:T(8,128)(2,1)}), bf16[16,28,1024]{2,1,0:T(8,128)(2,1)}, u32[]{:S(2)}, u32[]{:S(2)}) async-start(bf16[16,28,1024]{2,1,0:T(8,128)(2,1)} %add_convert_fusion.1), calls=%async_computation.5 | async-start | bytes 2097152 | tf_op jit(solution)/shard_map/all_to_all | solution.py:70
  362.1 2.3 fusion.40
  364.4 2.7 convolution_bitcast_fusion
  367.1 20.9 %all-to-all-done.5 = bf16[16,28,1024]{2,1,0:T(8,128)(2,1)} async-done(((bf16[16,28,1024]{2,1,0:T(8,128)(2,1)}), bf16[16,28,1024]{2,1,0:T(8,128)(2,1)}, u32[]{:S(2)}, u32[]{:S(2)}) %all-to-all-start.5) | async-done | bytes 917536 | tf_op jit(solution)/shard_map/all_to_all | solution.py:70
  389.9 2.1 fusion.53
  (81 shorter events, 26.1 us)
Async XLA Ops:
  0.6 117.3 %copy-start = (bf16[1,1,768,2048]{3,2,1,0:T(8,128)(2,1)S(1)}, bf16[1,1,768,2048]{3,2,1,0:T(8,128)(2,1)}, u32[]{:S(2)}) copy-start(bf16[1,1,768,2048]{3,2,1,0:T(8,128)(2,1)} %param.19) | copy-start | bytes 9437188
  0.7 8.1 %copy-start.4 = (s32[16,28]{0,1:T(8,128)}, s32[16,28]{0,1:T(8,128)S(1)}, u32[]{:S(2)}) copy-start(s32[16,28]{0,1:T(8,128)S(1)} %multiply_add_fusion) | copy-start | bytes 5380
  5.0 0.6 copy-start.5
  5.0 0.7 copy-start.6
  8.8 8.2 %copy-start.7 = (f32[1,128,2]{1,2,0:T(2,128)S(1)}, f32[1,128,2]{1,2,0:T(2,128)}, u32[]{:S(2)}) copy-start(f32[1,128,2]{1,2,0:T(2,128)} %param.15) | copy-start | bytes 3076
  8.8 56.5 %all-to-all-start.1 = ((bf16[16,28,2048]{2,1,0:T(8,128)(2,1)}), bf16[16,28,2048]{2,1,0:T(8,128)(2,1)}, u32[]{:S(2)}, u32[]{:S(2)}) async-start(bf16[16,28,2048]{2,1,0:T(8,128)(2,1)} %convolution_convert_fusion.1), calls=%async_computation.1 | async-start | bytes 4194304 | tf_op jit(solution)/shard_map/all_to_all | solution.py:70
  65.3 52.6 %all-to-all-start = ((bf16[16,28,2048]{2,1,0:T(8,128)(2,1)}), bf16[16,28,2048]{2,1,0:T(8,128)(2,1)}, u32[]{:S(2)}, u32[]{:S(2)}) async-start(bf16[16,28,2048]{2,1,0:T(8,128)(2,1)} %bitcast_convert_fusion.1), calls=%async_computation | async-start | bytes 4194304 | tf_op jit(solution)/shard_map/all_to_all | solution.py:70
  118.0 4.1 %copy-start.11 = (bf16[1,1,2048,768]{3,2,1,0:T(8,128)(2,1)S(1)}, bf16[1,1,2048,768]{3,2,1,0:T(8,128)(2,1)}, u32[]{:S(2)}) copy-start(bf16[1,1,2048,768]{3,2,1,0:T(8,128)(2,1)} %param.18) | copy-start | bytes 9437188
  118.0 4.1 %copy-start.23 = (f32[16,28,768]{2,1,0:T(8,128)S(1)}, f32[16,28,768]{2,1,0:T(8,128)}, u32[]{:S(2)}) copy-start(f32[16,28,768]{2,1,0:T(8,128)} %fusion.2) | copy-start | bytes 4128772
  122.1 5.0 %copy-start.15 = (bf16[16,28,768]{2,1,0:T(8,128)(2,1)}, bf16[16,28,768]{2,1,0:T(8,128)(2,1)S(1)}, u32[]{:S(2)}) copy-start(bf16[16,28,768]{2,1,0:T(8,128)(2,1)S(1)} %get-tuple-element.6) | copy-start | bytes 2064388
  122.1 3.9 copy-start.9
  126.0 1.0 copy-start.19
  129.1 30.1 %all-to-all-start.2 = ((bf16[16,28,1024]{2,1,0:T(8,128)(2,1)}), bf16[16,28,1024]{2,1,0:T(8,128)(2,1)}, u32[]{:S(2)}, u32[]{:S(2)}) async-start(bf16[16,28,1024]{2,1,0:T(8,128)(2,1)} %add_convert_fusion.3), calls=%async_computation.2 | async-start | bytes 2097152 | tf_op jit(solution)/shard_map/all_to_all | solution.py:70
  134.2 1.8 copy-start.20
  136.0 2.6 copy-start.12
  136.0 2.6 copy-start.16
  159.2 75.0 %all-to-all-start.3 = ((bf16[16,28,3072]{2,1,0:T(8,128)(2,1)}), bf16[16,28,3072]{2,1,0:T(8,128)(2,1)}, u32[]{:S(2)}, u32[]{:S(2)}) async-start(bf16[16,28,3072]{2,1,0:T(8,128)(2,1)} %pad_maximum_fusion), calls=%async_computation.3 | async-start | bytes 6291456 | tf_op jit(solution)/shard_map/all_to_all | solution.py:70
  234.2 2.1 copy-start.1
  234.2 2.1 copy-start.2
  235.6 5.8 %copy-start.8 = (f32[1,128,2]{1,2,0:T(2,128)S(1)}, f32[1,128,2]{1,2,0:T(2,128)}, u32[]{:S(2)}) copy-start(f32[1,128,2]{1,2,0:T(2,128)} %param.16) | copy-start | bytes 3076
  236.4 1.0 copy-start.3
  237.3 11.1 %collective-permute-start = (bf16[128,2048]{1,0:T(8,128)(2,1)}, bf16[128,2048]{1,0:T(8,128)(2,1)}, u32[]{:S(2)}, u32[]{:S(2)}) collective-permute-start(bf16[128,2048]{1,0:T(8,128)(2,1)} %fusion.43), channel_id=1, source_target_pairs={{16,0},{32,16},{48,32},{64,48},{80,64},{96,80},{112,96},{128,112},... | collective-permute-start | bytes 1572872 | tf_op jit(solution)/shard_map/ppermute | solution.py:10
  252.8 60.5 %all-to-all-start.4 = ((bf16[16,28,2048]{2,1,0:T(8,128)(2,1)}), bf16[16,28,2048]{2,1,0:T(8,128)(2,1)}, u32[]{:S(2)}, u32[]{:S(2)}) async-start(bf16[16,28,2048]{2,1,0:T(8,128)(2,1)} %bitcast_convert_fusion), calls=%async_computation.4 | async-start | bytes 4194304 | tf_op jit(solution)/shard_map/all_to_all | solution.py:70
  313.3 4.1 %copy-start.13 = (bf16[1,1,2048,768]{3,2,1,0:T(8,128)(2,1)S(1)}, bf16[1,1,2048,768]{3,2,1,0:T(8,128)(2,1)}, u32[]{:S(2)}) copy-start(bf16[1,1,2048,768]{3,2,1,0:T(8,128)(2,1)} %param.18) | copy-start | bytes 9437188
  313.3 4.1 %copy-start.22 = (f32[16,28,768]{2,1,0:T(8,128)S(1)}, f32[16,28,768]{2,1,0:T(8,128)}, u32[]{:S(2)}) copy-start(f32[16,28,768]{2,1,0:T(8,128)} %fusion) | copy-start | bytes 4128772
  317.5 5.0 %copy-start.17 = (bf16[16,28,768]{2,1,0:T(8,128)(2,1)}, bf16[16,28,768]{2,1,0:T(8,128)(2,1)S(1)}, u32[]{:S(2)}) copy-start(bf16[16,28,768]{2,1,0:T(8,128)(2,1)S(1)} %get-tuple-element.8) | copy-start | bytes 2064388
  317.5 3.9 copy-start.10
  321.4 1.0 copy-start.21
  324.5 32.5 %all-to-all-start.6 = ((bf16[16,28,1024]{2,1,0:T(8,128)(2,1)}), bf16[16,28,1024]{2,1,0:T(8,128)(2,1)}, u32[]{:S(2)}, u32[]{:S(2)}) async-start(bf16[16,28,1024]{2,1,0:T(8,128)(2,1)} %add_convert_fusion), calls=%async_computation.6 | async-start | bytes 2097152 | tf_op jit(solution)/shard_map/all_to_all | solution.py:70
  329.9 2.8 copy-start.14
  329.9 2.8 copy-start.18
  357.0 31.0 %all-to-all-start.5 = ((bf16[16,28,1024]{2,1,0:T(8,128)(2,1)}), bf16[16,28,1024]{2,1,0:T(8,128)(2,1)}, u32[]{:S(2)}, u32[]{:S(2)}) async-start(bf16[16,28,1024]{2,1,0:T(8,128)(2,1)} %add_convert_fusion.1), calls=%async_computation.5 | async-start | bytes 2097152 | tf_op jit(solution)/shard_map/all_to_all | solution.py:70

commit v2 on v0

--- a/solution.py
+++ b/solution.py
@@ -79,6 +79,37 @@
     return summed.astype(jnp.bfloat16)
 
 
+def back_half(d_gate, d_up, gate_mat, up_mat):
+    contract = (((2,), (1,)), ((), ()))
+    back = lax.dot_general(d_gate, gate_mat, contract, preferred_element_type=jnp.float32)
+    back = back + lax.dot_general(d_up, up_mat, contract, preferred_element_type=jnp.float32)
+    return back.astype(jnp.bfloat16)
+
+
+def hidden_grads(gate_pre, up_pre, scaled, down_mat):
+    contract = (((2,), (1,)), ((), ()))
+    d_hidden = lax.dot_general(scaled, down_mat, contract, preferred_element_type=jnp.float32)
+    gate_sig = jax.nn.sigmoid(gate_pre)
+    active = gate_pre * gate_sig
+    slope = gate_sig * (1.0 + gate_pre * (1.0 - gate_sig))
+    d_gate = (d_hidden * up_pre * slope).astype(jnp.bfloat16)
+    d_up = (d_hidden * active).astype(jnp.bfloat16)
+    return d_gate, d_up
+
+
+def pick_cols(returned, table):
+    return lax.dot_general(
+        table, returned, (((1, 2), (0, 1)), ((), ())), preferred_element_type=jnp.float32
+    )
+
+
+def beside(send, filler_input, filler):
+    send, filler_input = lax.optimization_barrier((send, filler_input))
+    arrived = exchange(send)
+    extra = filler(filler_input)
+    return lax.optimization_barrier((arrived, extra))
+
+
 def on_device(
     tokens_a, cotangent_a, tokens_b, routes_a, routes_b, probs_a, probs_b, w_gate, w_up, w_down
 ):
@@ -89,6 +120,7 @@
     gate_mat = w_gate[0, 0]
     up_mat = w_up[0, 0]
     down_mat = w_down[0, 0]
+    contract = (((2,), (0,)), ((), ()))
     first_hits = slot_hits(routes_a[0], experts, capacity)
     second_hits = slot_hits(routes_b[0], experts, capacity)
     first_cot = cotangent_a[0]
@@ -97,25 +129,49 @@
         [
             jnp.broadcast_to(tokens_a[0][:, None, :], (tok_count, 2, width)),
             scaled_rows(first_cot, probs_a[0]),
+            jnp.zeros((tok_count, 2, width), jnp.bfloat16),
         ],
         axis=2,
     )
-    first_arrived = exchange(place(first_hits, first_rows))
+    first_send = place(first_hits, first_rows)
+    second_send = place_tokens(tokens_b[0], second_hits)
+    first_send = lax.dynamic_update_slice(first_send, second_send, (0, 0, 2 * width))
+    first_arrived, first_table = beside(
+        first_send, first_hits, lambda hits: jnp.sum(hits, axis=1)
+    )
+
     gate_pre, up_pre = recompute(first_arrived[:, :, :width], gate_mat, up_mat)
     first_back = backprop(
-        gate_pre, up_pre, first_arrived[:, :, width:], gate_mat, up_mat, down_mat
+        gate_pre, up_pre, first_arrived[:, :, width:2 * width], gate_mat, up_mat, down_mat
     )
-    second_tokens = place_tokens(tokens_b[0], second_hits)
-    mixed = exchange(jnp.concatenate([first_back, second_tokens], axis=2))
-    grad_a = pick(mixed[:, :, :width], first_hits, first_cot)
+    second_tokens = first_arrived[:, :, 2 * width:]
+    returned, second_gate_pre = beside(
+        first_back,
+        second_tokens,
+        lambda rows: lax.dot_general(rows, gate_mat, contract, preferred_element_type=jnp.float32),
+    )
+    picked = lax.dot_general(
+        first_table, returned, (((1, 2), (0, 1)), ((), ())), preferred_element_type=jnp.float32
+    )
+    grad_a = (first_cot.astype(jnp.float32) + picked).astype(jnp.bfloat16)
 
     second_cot = shifted(grad_a, "pipe", -1)
-    second_gate_pre, second_up_pre = recompute(mixed[:, :, width:], gate_mat, up_mat)
-    second_scaled = exchange(place(second_hits, scaled_rows(second_cot, probs_b[0])))
+    second_scaled, second_up_pre = beside(
+        place(second_hits, scaled_rows(second_cot, probs_b[0])),
+        second_tokens,
+        lambda rows: lax.dot_general(rows, up_mat, contract, preferred_element_type=jnp.float32),
+    )
     second_back = backprop(
         second_gate_pre, second_up_pre, second_scaled, gate_mat, up_mat, down_mat
     )
-    grad_b = pick(exchange(second_back), second_hits, second_cot)
+    second_returned, second_table = beside(
+        second_back, second_hits, lambda hits: jnp.sum(hits, axis=1)
+    )
+    picked = lax.dot_general(
+        second_table, second_returned, (((1, 2), (0, 1)), ((), ())),
+        preferred_element_type=jnp.float32,
+    )
+    grad_b = (second_cot.astype(jnp.float32) + picked).astype(jnp.bfloat16)
     return (grad_a[None], grad_b[None])
 
 

time: 389 us -> 386 us (level)
  blocking collectives: 150 us -> 0 us
  waiting for transfers between devices: 144 us -> 280 us
  starting transfers between devices: 18.9 us -> 34.4 us
  matrix products: 62.6 us -> 55.3 us
  local copies, waits for them, and re-layouts: 2.5 us -> 7.21 us
    all_to_all x2 -> x0, blocking collectives: 150 us -> none  [exchange(): lax.all_to_all(block, 'expert', split_axis=0, concat_axis=0, tiled=True)]
    all_to_all x2 -> x4, waiting for transfers between devices: 133 us -> 273 us  [exchange(): lax.all_to_all(block, 'expert', split_axis=0, concat_axis=0, tiled=True)]
    all_to_all x2 -> x4, starting transfers between devices: 13.3 us -> 29.5 us  [exchange(): lax.all_to_all(block, 'expert', split_axis=0, concat_axis=0, tiled=True)]
    dot_general x2 -> x4, matrix products: 3.58 us -> 15.1 us  [the longest x1 5.48 us: on_device(): lax.dot_general(rows, gate_mat, contract, preferred_element_type=jnp.floa...]
    dot_general x2, matrix products: 18.8 us -> 11.7 us  [backprop(): lax.dot_general(d_gate, gate_mat, contract, preferred_element_type=jnp.fl...]
    dot_general x2 -> x1, matrix products: 11.1 us -> 4.77 us  [recompute(): lax.dot_general(rows, gate_mat, contract, preferred_element_type=jnp.floa...]
    ppermute x1, waiting for transfers between devices: 11.4 us -> 7.13 us  [shifted(): return lax.ppermute(block, axis, route)]
  transfers between devices with their start and end apart: 3 -> 5, of which waited for: 3 -> 5; matrix products, arithmetic and copies ran while one was open for 2% -> 3% of each run, Pallas kernels for 0% -> 0%
where the time goes in v2:
time: 386 us; the launch traced here: 385 us
  waiting for transfers between devices  280 us (73%)
  matrix products  55.3 us (14%)
  starting transfers between devices  34.4 us (9%)
  other arithmetic  7.6 us (2%)
  local copies, waits for them, and re-layouts  7.21 us (2%)
    all_to_all x4, waiting for transfers between devices, exchange(): lax.all_to_all(block, 'expert', split_axis=0, concat_axis=0, tiled=True)  273 us
    all_to_all x4, starting transfers between devices, exchange(): lax.all_to_all(block, 'expert', split_axis=0, concat_axis=0, tiled=True)  29.5 us
    dot_general x2, matrix products, backprop(): lax.dot_general(d_gate, gate_mat, contract, preferred_element_type=jnp.fl...  11.7 us
    dot_general x2, matrix products, backprop(): lax.dot_general(d_up, up_mat, contract, preferred_element_type=jnp.float32)  9.56 us
    dot_general x2, matrix products, backprop(): lax.dot_general(scaled, down_mat, contract, preferred_element_type=jnp.fl...  9.07 us
  transfers between devices with their start and end apart: 5, of which 5 were waited for; matrix products, arithmetic and copies ran while one was open for 3% of the time, Pallas kernels for 0%

profile of v2, /device:TPU:64, one launch (start us, length us, event | category | flops | bytes accessed | tf_op | source)
XLA Modules:
  0.0 385.1 jit_solution(1656376725752648199)
XLA Ops:
  0.7 0.8 convert_reduce_fusion.1
  1.5 0.8 convert_reduce_fusion
  2.7 0.7 select_reduce_fusion.1
  5.3 0.9 compare_convert_fusion
  6.1 1.1 bitcast_convert_fusion.2
  7.7 2.3 bitcast_convert_fusion
  10.7 2.6 copy-done.1
  13.4 8.0 %all-to-all-start = ((bf16[16,28,6144]{2,1,0:T(8,128)(2,1)}), bf16[16,28,6144]{2,1,0:T(8,128)(2,1)}, u32[]{:S(2)}, u32[]{:S(2)}) async-start(bf16[16,28,6144]{2,1,0:T(8,128)(2,1)} %copy-done.1), calls=%async_computation | async-start | bytes 12582912 | tf_op jit(solution)/shard_map/all_to_all | solution.py:70
  21.4 1.0 reduce_sum.77
  22.4 137.3 %all-to-all-done = bf16[16,28,6144]{2,1,0:T(8,128)(2,1)} async-done(((bf16[16,28,6144]{2,1,0:T(8,128)(2,1)}), bf16[16,28,6144]{2,1,0:T(8,128)(2,1)}, u32[]{:S(2)}, u32[]{:S(2)}) %all-to-all-start) | async-done | bytes 5505056 | tf_op jit(solution)/shard_map/all_to_all | solution.py:70
  159.7 3.3 slice.11
  162.9 4.8 %fusion.13 = f32[16,28,768]{2,1,0:T(8,128)} fusion(bf16[1,1,2048,768]{3,2,1,0:T(8,128)(2,1)S(1)} %copy-done.9, bf16[16,28,6144]{2,1,0:T(8,128)(2,1)} %all-to-all-done), kind=kOutput, calls=%fused_computation.18 | convolution fusion | flops 1409286144 | bytes 6619136 | tf_op jit(solution)/shard_map/dot_general | solution.py:51
  167.7 4.6 %fusion.5 = f32[16,28,768]{2,1,0:T(8,128)} fusion(bf16[1,1,768,2048]{3,2,1,0:T(8,128)(2,1)S(1)} %copy-done.8, bf16[16,28,6144]{2,1,0:T(8,128)(2,1)} %all-to-all-done), kind=kOutput, calls=%fused_computation.10 | convolution fusion | flops 1409286144 | bytes 6619136 | tf_op jit(solution)/shard_map/dot_general | solution.py:58
  172.3 9.5 %fusion.11 = f32[16,28,2048]{2,1,0:T(8,128)} fusion(bf16[1,1,2048,768]{3,2,1,0:T(8,128)(2,1)} %param.17, f32[16,28,768]{2,1,0:T(8,128)} %fusion.13, f32[16,28,768]{2,1,0:T(8,128)} %fusion.5, bf16[1,1,2048,768]{3,2,1,0:T(8,128)(2,1)S(1)} %copy-done, bf16[16,28,6144]{2,1,0:T(8,128)(2,1)} %all-to-all-done), kind=kOutput, calls=%fused_computation.16 | convolution fusion | flops 2822012928 | bytes 15204352 | tf_op jit(solution)/shard_map/dot_general | solution.py:64
  181.8 6.3 %add_convert_fusion.1 = bf16[16,28,2048]{2,1,0:T(8,128)(2,1)} fusion(f32[16,28,2048]{2,1,0:T(8,128)} %fusion.11, bf16[1,1,2048,768]{3,2,1,0:T(8,128)(2,1)S(1)} %copy-done, f32[16,28,768]{2,1,0:T(8,128)} %fusion.5, f32[16,28,768]{2,1,0:T(8,128)} %fusion.13), kind=kOutput, calls=%fused_computation.3 | convolution fusion | flops 1413185536 | bytes 11403264 | tf_op jit(solution)/shard_map/dot_general | solution.py:65
  188.1 5.2 %all-to-all-start.1 = ((bf16[16,28,2048]{2,1,0:T(8,128)(2,1)}), bf16[16,28,2048]{2,1,0:T(8,128)(2,1)}, u32[]{:S(2)}, u32[]{:S(2)}) async-start(bf16[16,28,2048]{2,1,0:T(8,128)(2,1)} %add_convert_fusion.1), calls=%async_computation.1 | async-start | bytes 4194304 | tf_op jit(solution)/shard_map/all_to_all | solution.py:70
  193.3 5.5 %fusion.9 = f32[16,28,768]{2,1,0:T(8,128)} fusion(bf16[16,28,2048]{2,1,0:T(8,128)(2,1)} %slice.11, bf16[1,1,2048,768]{3,2,1,0:T(8,128)(2,1)} %param.17), kind=kOutput, calls=%fused_computation.14 | convolution fusion | flops 1409286144 | bytes 6356992 | tf_op jit(solution)/shard_map/dot_general | solution.py:151
  198.8 42.2 %all-to-all-done.1 = bf16[16,28,2048]{2,1,0:T(8,128)(2,1)} async-done(((bf16[16,28,2048]{2,1,0:T(8,128)(2,1)}), bf16[16,28,2048]{2,1,0:T(8,128)(2,1)}, u32[]{:S(2)}, u32[]{:S(2)}) %all-to-all-start.1) | async-done | bytes 1835040 | tf_op jit(solution)/shard_map/all_to_all | solution.py:70
  240.9 2.1 fusion.31
  243.1 4.9 %collective-permute-start = (bf16[128,2048]{1,0:T(8,128)(2,1)S(1)}, bf16[128,2048]{1,0:T(8,128)(2,1)S(1)}, u32[]{:S(2)}, u32[]{:S(2)}) collective-permute-start(bf16[128,2048]{1,0:T(8,128)(2,1)S(1)} %fusion.31), channel_id=1, source_target_pairs={{16,0},{32,16},{48,32},{64,48},{80,64},{96,80},{112,96},{128,112},... | collective-permute-start | bytes 1572872 | tf_op jit(solution)/shard_map/ppermute | solution.py:10
  248.0 7.1 %collective-permute-done = bf16[128,2048]{1,0:T(8,128)(2,1)S(1)} collective-permute-done((bf16[128,2048]{1,0:T(8,128)(2,1)S(1)}, bf16[128,2048]{1,0:T(8,128)(2,1)S(1)}, u32[]{:S(2)}, u32[]{:S(2)}) %collective-permute-start) | collective-permute-done | bytes 524320 | tf_op jit(solution)/shard_map/ppermute | solution.py:10
  255.1 0.8 copy-done.2
  256.0 2.1 bitcast_convert_fusion.1
  258.1 10.8 %all-to-all-start.2 = ((bf16[16,28,2048]{2,1,0:T(8,128)(2,1)}), bf16[16,28,2048]{2,1,0:T(8,128)(2,1)}, u32[]{:S(2)}, u32[]{:S(2)}) async-start(bf16[16,28,2048]{2,1,0:T(8,128)(2,1)} %bitcast_convert_fusion.1), calls=%async_computation.2 | async-start | bytes 4194304 | tf_op jit(solution)/shard_map/all_to_all | solution.py:70
  268.9 4.6 %fusion.17 = f32[16,28,768]{2,1,0:T(8,128)} fusion(bf16[16,28,2048]{2,1,0:T(8,128)(2,1)} %slice.11, bf16[1,1,2048,768]{3,2,1,0:T(8,128)(2,1)S(1)} %copy-done), kind=kOutput, calls=%fused_computation.22 | convolution fusion | flops 1409286144 | bytes 6356992 | tf_op jit(solution)/shard_map/dot_general | solution.py:162
  273.5 43.7 %all-to-all-done.2 = bf16[16,28,2048]{2,1,0:T(8,128)(2,1)} async-done(((bf16[16,28,2048]{2,1,0:T(8,128)(2,1)}), bf16[16,28,2048]{2,1,0:T(8,128)(2,1)}, u32[]{:S(2)}, u32[]{:S(2)}) %all-to-all-start.2) | async-done | bytes 1835040 | tf_op jit(solution)/shard_map/all_to_all | solution.py:70
  317.2 4.5 %fusion.3 = f32[16,28,768]{2,1,0:T(8,128)S(1)} fusion(bf16[16,28,2048]{2,1,0:T(8,128)(2,1)} %all-to-all-done.2, bf16[1,1,768,2048]{3,2,1,0:T(8,128)(2,1)} %param.19), kind=kOutput, calls=%fused_computation.8 | convolution fusion | flops 1409286144 | bytes 6356992 | tf_op jit(solution)/shard_map/dot_general | solution.py:58
  321.7 2.2 fusion.7
  323.9 3.2 add_convert_fusion
  327.1 5.5 %all-to-all-start.3 = ((bf16[16,28,2048]{2,1,0:T(8,128)(2,1)}), bf16[16,28,2048]{2,1,0:T(8,128)(2,1)}, u32[]{:S(2)}, u32[]{:S(2)}) async-start(bf16[16,28,2048]{2,1,0:T(8,128)(2,1)} %add_convert_fusion), calls=%async_computation.3 | async-start | bytes 4194304 | tf_op jit(solution)/shard_map/all_to_all | solution.py:70
  332.7 49.5 %all-to-all-done.3 = bf16[16,28,2048]{2,1,0:T(8,128)(2,1)} async-done(((bf16[16,28,2048]{2,1,0:T(8,128)(2,1)}), bf16[16,28,2048]{2,1,0:T(8,128)(2,1)}, u32[]{:S(2)}, u32[]{:S(2)}) %all-to-all-start.3) | async-done | bytes 1835040 | tf_op jit(solution)/shard_map/all_to_all | solution.py:70
  382.2 2.9 fusion.32
  (43 shorter events, 3.4 us)
Async XLA Ops:
  0.6 171.7 %copy-start = (bf16[1,1,2048,768]{3,2,1,0:T(8,128)(2,1)S(1)}, bf16[1,1,2048,768]{3,2,1,0:T(8,128)(2,1)}, u32[]{:S(2)}) copy-start(bf16[1,1,2048,768]{3,2,1,0:T(8,128)(2,1)} %param.18) | copy-start | bytes 9437188
  0.6 6.7 %copy-start.6 = (f32[1,128,2]{1,2,0:T(2,128)S(1)}, f32[1,128,2]{1,2,0:T(2,128)}, u32[]{:S(2)}) copy-start(f32[1,128,2]{1,2,0:T(2,128)} %param.15) | copy-start | bytes 3076
  5.3 2.3 copy-start.3
  7.6 2.3 copy-start.5
  10.7 2.7 copy-start.1
  13.4 146.3 %all-to-all-start = ((bf16[16,28,6144]{2,1,0:T(8,128)(2,1)}), bf16[16,28,6144]{2,1,0:T(8,128)(2,1)}, u32[]{:S(2)}, u32[]{:S(2)}) async-start(bf16[16,28,6144]{2,1,0:T(8,128)(2,1)} %copy-done.1), calls=%async_computation | async-start | bytes 12582912 | tf_op jit(solution)/shard_map/all_to_all | solution.py:70
  159.6 3.3 copy-start.9
  162.9 4.8 %copy-start.8 = (bf16[1,1,768,2048]{3,2,1,0:T(8,128)(2,1)S(1)}, bf16[1,1,768,2048]{3,2,1,0:T(8,128)(2,1)}, u32[]{:S(2)}) copy-start(bf16[1,1,768,2048]{3,2,1,0:T(8,128)(2,1)} %param.19) | copy-start | bytes 9437188
  188.1 52.8 %all-to-all-start.1 = ((bf16[16,28,2048]{2,1,0:T(8,128)(2,1)}), bf16[16,28,2048]{2,1,0:T(8,128)(2,1)}, u32[]{:S(2)}, u32[]{:S(2)}) async-start(bf16[16,28,2048]{2,1,0:T(8,128)(2,1)} %add_convert_fusion.1), calls=%async_computation.1 | async-start | bytes 4194304 | tf_op jit(solution)/shard_map/all_to_all | solution.py:70
  198.8 57.3 %copy-start.7 = (f32[1,128,2]{1,2,0:T(2,128)S(1)}, f32[1,128,2]{1,2,0:T(2,128)}, u32[]{:S(2)}) copy-start(f32[1,128,2]{1,2,0:T(2,128)} %param.16) | copy-start | bytes 3076
  243.1 12.9 %copy-start.4 = (bf16[128,2048]{1,0:T(8,128)(2,1)}, bf16[128,2048]{1,0:T(8,128)(2,1)S(1)}, u32[]{:S(2)}) copy-start(bf16[128,2048]{1,0:T(8,128)(2,1)S(1)} %fusion.31) | copy-start | bytes 1572868
  243.1 12.0 %collective-permute-start = (bf16[128,2048]{1,0:T(8,128)(2,1)S(1)}, bf16[128,2048]{1,0:T(8,128)(2,1)S(1)}, u32[]{:S(2)}, u32[]{:S(2)}) collective-permute-start(bf16[128,2048]{1,0:T(8,128)(2,1)S(1)} %fusion.31), channel_id=1, source_target_pairs={{16,0},{32,16},{48,32},{64,48},{80,64},{96,80},{112,96},{128,112},... | collective-permute-start | bytes 1572872 | tf_op jit(solution)/shard_map/ppermute | solution.py:10
  255.1 0.8 copy-start.2
  258.1 59.1 %all-to-all-start.2 = ((bf16[16,28,2048]{2,1,0:T(8,128)(2,1)}), bf16[16,28,2048]{2,1,0:T(8,128)(2,1)}, u32[]{:S(2)}, u32[]{:S(2)}) async-start(bf16[16,28,2048]{2,1,0:T(8,128)(2,1)} %bitcast_convert_fusion.1), calls=%async_computation.2 | async-start | bytes 4194304 | tf_op jit(solution)/shard_map/all_to_all | solution.py:70
  317.2 4.5 %copy-start.10 = (bf16[1,1,2048,768]{3,2,1,0:T(8,128)(2,1)S(1)}, bf16[1,1,2048,768]{3,2,1,0:T(8,128)(2,1)}, u32[]{:S(2)}) copy-start(bf16[1,1,2048,768]{3,2,1,0:T(8,128)(2,1)} %param.17) | copy-start | bytes 9437188
  317.2 4.5 %copy-start.11 = (f32[16,28,768]{2,1,0:T(8,128)S(1)}, f32[16,28,768]{2,1,0:T(8,128)}, u32[]{:S(2)}) copy-start(f32[16,28,768]{2,1,0:T(8,128)} %fusion.9) | copy-start | bytes 4128772
  317.2 4.5 %copy-start.12 = (f32[16,28,768]{2,1,0:T(8,128)S(1)}, f32[16,28,768]{2,1,0:T(8,128)}, u32[]{:S(2)}) copy-start(f32[16,28,768]{2,1,0:T(8,128)} %fusion.17) | copy-start | bytes 4128772
  327.1 55.0 %all-to-all-start.3 = ((bf16[16,28,2048]{2,1,0:T(8,128)(2,1)}), bf16[16,28,2048]{2,1,0:T(8,128)(2,1)}, u32[]{:S(2)}, u32[]{:S(2)}) async-start(bf16[16,28,2048]{2,1,0:T(8,128)(2,1)} %add_convert_fusion), calls=%async_computation.3 | async-start | bytes 4194304 | tf_op jit(solution)/shard_map/all_to_all | solution.py:70

commit v3 on v2

--- a/solution.py
+++ b/solution.py
@@ -103,9 +103,9 @@
     )
 
 
-def beside(send, filler_input, filler):
+def beside(send, filler_input, filler, move=exchange):
     send, filler_input = lax.optimization_barrier((send, filler_input))
-    arrived = exchange(send)
+    arrived = move(send)
     extra = filler(filler_input)
     return lax.optimization_barrier((arrived, extra))
 
@@ -122,40 +122,42 @@
     down_mat = w_down[0, 0]
     contract = (((2,), (0,)), ((), ()))
     first_hits = slot_hits(routes_a[0], experts, capacity)
-    second_hits = slot_hits(routes_b[0], experts, capacity)
     first_cot = cotangent_a[0]
 
     first_rows = jnp.concatenate(
         [
             jnp.broadcast_to(tokens_a[0][:, None, :], (tok_count, 2, width)),
             scaled_rows(first_cot, probs_a[0]),
-            jnp.zeros((tok_count, 2, width), jnp.bfloat16),
         ],
         axis=2,
     )
-    first_send = place(first_hits, first_rows)
-    second_send = place_tokens(tokens_b[0], second_hits)
-    first_send = lax.dynamic_update_slice(first_send, second_send, (0, 0, 2 * width))
-    first_arrived, first_table = beside(
-        first_send, first_hits, lambda hits: jnp.sum(hits, axis=1)
+
+    def pack_second(pieces):
+        routes, tokens = pieces
+        hits = slot_hits(routes, experts, capacity)
+        return hits, place_tokens(tokens, hits)
+
+    first_arrived, (second_hits, second_send) = beside(
+        place(first_hits, first_rows), (routes_b[0], tokens_b[0]), pack_second
     )
 
-    gate_pre, up_pre = recompute(first_arrived[:, :, :width], gate_mat, up_mat)
-    first_back = backprop(
-        gate_pre, up_pre, first_arrived[:, :, width:2 * width], gate_mat, up_mat, down_mat
-    )
-    second_tokens = first_arrived[:, :, 2 * width:]
-    returned, second_gate_pre = beside(
-        first_back,
-        second_tokens,
-        lambda rows: lax.dot_general(rows, gate_mat, contract, preferred_element_type=jnp.float32),
-    )
+    def first_compute(arrived):
+        gate_pre, up_pre = recompute(arrived[:, :, :width], gate_mat, up_mat)
+        return backprop(gate_pre, up_pre, arrived[:, :, width:], gate_mat, up_mat, down_mat)
+
+    second_tokens, first_back = beside(second_send, first_arrived, first_compute)
+    returned, first_table = beside(first_back, first_hits, lambda hits: jnp.sum(hits, axis=1))
     picked = lax.dot_general(
         first_table, returned, (((1, 2), (0, 1)), ((), ())), preferred_element_type=jnp.float32
     )
     grad_a = (first_cot.astype(jnp.float32) + picked).astype(jnp.bfloat16)
 
-    second_cot = shifted(grad_a, "pipe", -1)
+    second_cot, second_gate_pre = beside(
+        grad_a,
+        second_tokens,
+        lambda rows: lax.dot_general(rows, gate_mat, contract, preferred_element_type=jnp.float32),
+        move=lambda block: shifted(block, "pipe", -1),
+    )
     second_scaled, second_up_pre = beside(
         place(second_hits, scaled_rows(second_cot, probs_b[0])),
         second_tokens,

time: 386 us -> 359 us (0.930)
  waiting for transfers between devices: 280 us -> 252 us
  local copies, waits for them, and re-layouts: 7.21 us -> 1.26 us
  starting transfers between devices: 34.4 us -> 38.4 us
    all_to_all x4 -> x5, waiting for transfers between devices: 273 us -> 250 us  [exchange(): lax.all_to_all(block, 'expert', split_axis=0, concat_axis=0, tiled=True)]
    ppermute x1, waiting for transfers between devices: 7.13 us -> 2.52 us  [shifted(): return lax.ppermute(block, axis, route)]
    all_to_all x4 -> x5, starting transfers between devices: 29.5 us -> 33.4 us  [exchange(): lax.all_to_all(block, 'expert', split_axis=0, concat_axis=0, tiled=True)]
  transfers between devices with their start and end apart: 5 -> 6, of which waited for: 5 -> 6; matrix products, arithmetic and copies ran while one was open for 3% -> 11% of each run, Pallas kernels for 0% -> 0%
where the time goes in v3:
time: 359 us; the launch traced here: 358 us
  waiting for transfers between devices  252 us (70%)
  matrix products  58.7 us (16%)
  starting transfers between devices  38.4 us (11%)
  other arithmetic  6.86 us (2%)
    all_to_all x5, waiting for transfers between devices, exchange(): lax.all_to_all(block, 'expert', split_axis=0, concat_axis=0, tiled=True)  250 us
    all_to_all x5, starting transfers between devices, exchange(): lax.all_to_all(block, 'expert', split_axis=0, concat_axis=0, tiled=True)  33.4 us
    dot_general x2, matrix products, backprop(): lax.dot_general(d_gate, gate_mat, contract, preferred_element_type=jnp.fl...  11.6 us
    dot_general x2, matrix products, backprop(): lax.dot_general(d_up, up_mat, contract, preferred_element_type=jnp.float32)  9.56 us
    dot_general x2, matrix products, backprop(): lax.dot_general(scaled, down_mat, contract, preferred_element_type=jnp.fl...  9.06 us
  transfers between devices with their start and end apart: 6, of which 6 were waited for; matrix products, arithmetic and copies ran while one was open for 11% of the time, Pallas kernels for 0%

profile of v3, /device:TPU:64, one launch (start us, length us, event | category | flops | bytes accessed | tf_op | source)
XLA Modules:
  0.0 358.1 jit_solution(9281517516742029613)
XLA Ops:
  0.7 0.8 convert_reduce_fusion.1
  3.3 1.1 bitcast_convert_fusion.2
  4.4 0.9 multiply_convert_fusion.1
  5.4 3.3 bitcast_convert_fusion
  8.7 8.2 %all-to-all-start = ((bf16[16,28,4096]{2,1,0:T(8,128)(2,1)}), bf16[16,28,4096]{2,1,0:T(8,128)(2,1)}, u32[]{:S(2)}, u32[]{:S(2)}) async-start(bf16[16,28,4096]{2,1,0:T(8,128)(2,1)} %bitcast_convert_fusion), calls=%async_computation | async-start | bytes 8388608 | tf_op jit(solution)/shard_map/all_to_all | solution.py:70
  17.4 0.9 compare_convert_fusion
  18.3 3.0 convolution_convert_fusion
  21.3 88.9 %all-to-all-done = bf16[16,28,4096]{2,1,0:T(8,128)(2,1)} async-done(((bf16[16,28,4096]{2,1,0:T(8,128)(2,1)}), bf16[16,28,4096]{2,1,0:T(8,128)(2,1)}, u32[]{:S(2)}, u32[]{:S(2)}) %all-to-all-start) | async-done | bytes 3670048 | tf_op jit(solution)/shard_map/all_to_all | solution.py:70
  110.2 5.2 %all-to-all-start.1 = ((bf16[16,28,2048]{2,1,0:T(8,128)(2,1)}), bf16[16,28,2048]{2,1,0:T(8,128)(2,1)}, u32[]{:S(2)}, u32[]{:S(2)}) async-start(bf16[16,28,2048]{2,1,0:T(8,128)(2,1)} %convolution_convert_fusion), calls=%async_computation.1 | async-start | bytes 4194304 | tf_op jit(solution)/shard_map/all_to_all | solution.py:70
  115.4 5.7 %fusion.10 = f32[16,28,768]{2,1,0:T(8,128)} fusion(bf16[1,1,2048,768]{3,2,1,0:T(8,128)(2,1)} %param.17, bf16[16,28,4096]{2,1,0:T(8,128)(2,1)} %all-to-all-done), kind=kOutput, calls=%fused_computation.14 | convolution fusion | flops 1409286144 | bytes 6619136 | tf_op jit(solution)/shard_map/dot_general | solution.py:51
  121.0 4.6 %fusion.2 = f32[16,28,768]{2,1,0:T(8,128)} fusion(bf16[1,1,768,2048]{3,2,1,0:T(8,128)(2,1)S(1)} %copy-done.6, bf16[16,28,4096]{2,1,0:T(8,128)(2,1)} %all-to-all-done), kind=kOutput, calls=%fused_computation.6 | convolution fusion | flops 1409286144 | bytes 6619136 | tf_op jit(solution)/shard_map/dot_general | solution.py:58
  125.6 9.4 %fusion.8 = f32[16,28,2048]{2,1,0:T(8,128)} fusion(bf16[1,1,2048,768]{3,2,1,0:T(8,128)(2,1)} %param.17, f32[16,28,768]{2,1,0:T(8,128)} %fusion.10, f32[16,28,768]{2,1,0:T(8,128)} %fusion.2, bf16[1,1,2048,768]{3,2,1,0:T(8,128)(2,1)S(1)} %copy-done, bf16[16,28,4096]{2,1,0:T(8,128)(2,1)} %all-to-all-done), kind=kOutput, calls=%fused_computation.12 | convolution fusion | flops 2822012928 | bytes 15204352 | tf_op jit(solution)/shard_map/dot_general | solution.py:64
  135.0 6.3 %add_convert_fusion.1 = bf16[16,28,2048]{2,1,0:T(8,128)(2,1)} fusion(f32[16,28,2048]{2,1,0:T(8,128)} %fusion.8, bf16[1,1,2048,768]{3,2,1,0:T(8,128)(2,1)S(1)} %copy-done, f32[16,28,768]{2,1,0:T(8,128)} %fusion.2, f32[16,28,768]{2,1,0:T(8,128)} %fusion.10), kind=kOutput, calls=%fused_computation.3 | convolution fusion | flops 1413185536 | bytes 11403264 | tf_op jit(solution)/shard_map/dot_general | solution.py:65
  141.3 21.7 %all-to-all-done.1 = bf16[16,28,2048]{2,1,0:T(8,128)(2,1)} async-done(((bf16[16,28,2048]{2,1,0:T(8,128)(2,1)}), bf16[16,28,2048]{2,1,0:T(8,128)(2,1)}, u32[]{:S(2)}, u32[]{:S(2)}) %all-to-all-start.1) | async-done | bytes 1835040 | tf_op jit(solution)/shard_map/all_to_all | solution.py:70
  163.0 5.1 %all-to-all-start.2 = ((bf16[16,28,2048]{2,1,0:T(8,128)(2,1)}), bf16[16,28,2048]{2,1,0:T(8,128)(2,1)}, u32[]{:S(2)}, u32[]{:S(2)}) async-start(bf16[16,28,2048]{2,1,0:T(8,128)(2,1)} %add_convert_fusion.1), calls=%async_computation.2 | async-start | bytes 4194304 | tf_op jit(solution)/shard_map/all_to_all | solution.py:70
  168.1 1.0 reduce_sum.77
  169.1 46.5 %all-to-all-done.2 = bf16[16,28,2048]{2,1,0:T(8,128)(2,1)} async-done(((bf16[16,28,2048]{2,1,0:T(8,128)(2,1)}), bf16[16,28,2048]{2,1,0:T(8,128)(2,1)}, u32[]{:S(2)}, u32[]{:S(2)}) %all-to-all-start.2) | async-done | bytes 1835040 | tf_op jit(solution)/shard_map/all_to_all | solution.py:70
  215.6 2.3 fusion.27
  217.9 5.0 %collective-permute-start = (bf16[128,2048]{1,0:T(8,128)(2,1)S(1)}, bf16[128,2048]{1,0:T(8,128)(2,1)S(1)}, u32[]{:S(2)}, u32[]{:S(2)}) collective-permute-start(bf16[128,2048]{1,0:T(8,128)(2,1)S(1)} %fusion.27), channel_id=1, source_target_pairs={{16,0},{32,16},{48,32},{64,48},{80,64},{96,80},{112,96},{128,112},... | collective-permute-start | bytes 1572872 | tf_op jit(solution)/shard_map/ppermute | solution.py:10
  223.0 4.6 %fusion.6 = f32[16,28,768]{2,1,0:T(8,128)} fusion(bf16[16,28,2048]{2,1,0:T(8,128)(2,1)} %all-to-all-done.1, bf16[1,1,2048,768]{3,2,1,0:T(8,128)(2,1)S(1)} %copy-done.7), kind=kOutput, calls=%fused_computation.10 | convolution fusion | flops 1409286144 | bytes 6356992 | tf_op jit(solution)/shard_map/dot_general | solution.py:158
  227.6 2.5 collective-permute-done
  230.1 0.8 copy-done.1
  231.0 2.1 bitcast_convert_fusion.1
  233.1 9.8 %all-to-all-start.3 = ((bf16[16,28,2048]{2,1,0:T(8,128)(2,1)}), bf16[16,28,2048]{2,1,0:T(8,128)(2,1)}, u32[]{:S(2)}, u32[]{:S(2)}) async-start(bf16[16,28,2048]{2,1,0:T(8,128)(2,1)} %bitcast_convert_fusion.1), calls=%async_computation.3 | async-start | bytes 4194304 | tf_op jit(solution)/shard_map/all_to_all | solution.py:70
  242.9 4.6 %fusion.14 = f32[16,28,768]{2,1,0:T(8,128)} fusion(bf16[16,28,2048]{2,1,0:T(8,128)(2,1)} %all-to-all-done.1, bf16[1,1,2048,768]{3,2,1,0:T(8,128)(2,1)S(1)} %copy-done), kind=kOutput, calls=%fused_computation.18 | convolution fusion | flops 1409286144 | bytes 6356992 | tf_op jit(solution)/shard_map/dot_general | solution.py:164
  247.5 44.6 %all-to-all-done.3 = bf16[16,28,2048]{2,1,0:T(8,128)(2,1)} async-done(((bf16[16,28,2048]{2,1,0:T(8,128)(2,1)}), bf16[16,28,2048]{2,1,0:T(8,128)(2,1)}, u32[]{:S(2)}, u32[]{:S(2)}) %all-to-all-start.3) | async-done | bytes 1835040 | tf_op jit(solution)/shard_map/all_to_all | solution.py:70
  292.0 4.5 %fusion = f32[16,28,768]{2,1,0:T(8,128)S(1)} fusion(bf16[16,28,2048]{2,1,0:T(8,128)(2,1)} %all-to-all-done.3, bf16[1,1,768,2048]{3,2,1,0:T(8,128)(2,1)} %param.19), kind=kOutput, calls=%fused_computation.4 | convolution fusion | flops 1409286144 | bytes 6356992 | tf_op jit(solution)/shard_map/dot_general | solution.py:58
  296.6 2.2 fusion.4
  298.8 3.2 add_convert_fusion
  302.0 5.1 %all-to-all-start.4 = ((bf16[16,28,2048]{2,1,0:T(8,128)(2,1)}), bf16[16,28,2048]{2,1,0:T(8,128)(2,1)}, u32[]{:S(2)}, u32[]{:S(2)}) async-start(bf16[16,28,2048]{2,1,0:T(8,128)(2,1)} %add_convert_fusion), calls=%async_computation.4 | async-start | bytes 4194304 | tf_op jit(solution)/shard_map/all_to_all | solution.py:70
  307.2 48.0 %all-to-all-done.4 = bf16[16,28,2048]{2,1,0:T(8,128)(2,1)} async-done(((bf16[16,28,2048]{2,1,0:T(8,128)(2,1)}), bf16[16,28,2048]{2,1,0:T(8,128)(2,1)}, u32[]{:S(2)}, u32[]{:S(2)}) %all-to-all-start.4) | async-done | bytes 1835040 | tf_op jit(solution)/shard_map/all_to_all | solution.py:70
  355.1 2.9 fusion.28
  (39 shorter events, 2.6 us)
Async XLA Ops:
  0.6 125.0 %copy-start = (bf16[1,1,2048,768]{3,2,1,0:T(8,128)(2,1)S(1)}, bf16[1,1,2048,768]{3,2,1,0:T(8,128)(2,1)}, u32[]{:S(2)}) copy-start(bf16[1,1,2048,768]{3,2,1,0:T(8,128)(2,1)} %param.18) | copy-start | bytes 9437188
  1.8 3.5 copy-start.2
  8.7 8.2 %copy-start.4 = (s32[1,128,2]{1,2,0:T(2,128)S(1)}, s32[1,128,2]{1,2,0:T(2,128)}, u32[]{:S(2)}) copy-start(s32[1,128,2]{1,2,0:T(2,128)} %param.14) | copy-start | bytes 3076
  8.7 101.5 %all-to-all-start = ((bf16[16,28,4096]{2,1,0:T(8,128)(2,1)}), bf16[16,28,4096]{2,1,0:T(8,128)(2,1)}, u32[]{:S(2)}, u32[]{:S(2)}) async-start(bf16[16,28,4096]{2,1,0:T(8,128)(2,1)} %bitcast_convert_fusion), calls=%async_computation | async-start | bytes 8388608 | tf_op jit(solution)/shard_map/all_to_all | solution.py:70
  110.2 52.8 %all-to-all-start.1 = ((bf16[16,28,2048]{2,1,0:T(8,128)(2,1)}), bf16[16,28,2048]{2,1,0:T(8,128)(2,1)}, u32[]{:S(2)}, u32[]{:S(2)}) async-start(bf16[16,28,2048]{2,1,0:T(8,128)(2,1)} %convolution_convert_fusion), calls=%async_computation.1 | async-start | bytes 4194304 | tf_op jit(solution)/shard_map/all_to_all | solution.py:70
  115.3 5.7 %copy-start.6 = (bf16[1,1,768,2048]{3,2,1,0:T(8,128)(2,1)S(1)}, bf16[1,1,768,2048]{3,2,1,0:T(8,128)(2,1)}, u32[]{:S(2)}) copy-start(bf16[1,1,768,2048]{3,2,1,0:T(8,128)(2,1)} %param.19) | copy-start | bytes 9437188
  163.0 52.6 %all-to-all-start.2 = ((bf16[16,28,2048]{2,1,0:T(8,128)(2,1)}), bf16[16,28,2048]{2,1,0:T(8,128)(2,1)}, u32[]{:S(2)}, u32[]{:S(2)}) async-start(bf16[16,28,2048]{2,1,0:T(8,128)(2,1)} %add_convert_fusion.1), calls=%async_computation.2 | async-start | bytes 4194304 | tf_op jit(solution)/shard_map/all_to_all | solution.py:70
  215.6 7.4 %copy-start.7 = (bf16[1,1,2048,768]{3,2,1,0:T(8,128)(2,1)S(1)}, bf16[1,1,2048,768]{3,2,1,0:T(8,128)(2,1)}, u32[]{:S(2)}) copy-start(bf16[1,1,2048,768]{3,2,1,0:T(8,128)(2,1)} %param.17) | copy-start | bytes 9437188
  217.9 9.7 %copy-start.3 = (bf16[128,2048]{1,0:T(8,128)(2,1)}, bf16[128,2048]{1,0:T(8,128)(2,1)S(1)}, u32[]{:S(2)}) copy-start(bf16[128,2048]{1,0:T(8,128)(2,1)S(1)} %fusion.27) | copy-start | bytes 1572868
  217.9 13.0 %copy-start.5 = (f32[1,128,2]{1,2,0:T(2,128)S(1)}, f32[1,128,2]{1,2,0:T(2,128)}, u32[]{:S(2)}) copy-start(f32[1,128,2]{1,2,0:T(2,128)} %param.16) | copy-start | bytes 3076
  217.9 12.1 %collective-permute-start = (bf16[128,2048]{1,0:T(8,128)(2,1)S(1)}, bf16[128,2048]{1,0:T(8,128)(2,1)S(1)}, u32[]{:S(2)}, u32[]{:S(2)}) collective-permute-start(bf16[128,2048]{1,0:T(8,128)(2,1)S(1)} %fusion.27), channel_id=1, source_target_pairs={{16,0},{32,16},{48,32},{64,48},{80,64},{96,80},{112,96},{128,112},... | collective-permute-start | bytes 1572872 | tf_op jit(solution)/shard_map/ppermute | solution.py:10
  230.1 0.8 copy-start.1
  233.1 58.9 %all-to-all-start.3 = ((bf16[16,28,2048]{2,1,0:T(8,128)(2,1)}), bf16[16,28,2048]{2,1,0:T(8,128)(2,1)}, u32[]{:S(2)}, u32[]{:S(2)}) async-start(bf16[16,28,2048]{2,1,0:T(8,128)(2,1)} %bitcast_convert_fusion.1), calls=%async_computation.3 | async-start | bytes 4194304 | tf_op jit(solution)/shard_map/all_to_all | solution.py:70
  292.0 4.5 %copy-start.8 = (bf16[1,1,2048,768]{3,2,1,0:T(8,128)(2,1)S(1)}, bf16[1,1,2048,768]{3,2,1,0:T(8,128)(2,1)}, u32[]{:S(2)}) copy-start(bf16[1,1,2048,768]{3,2,1,0:T(8,128)(2,1)} %param.17) | copy-start | bytes 9437188
  292.0 4.5 %copy-start.9 = (f32[16,28,768]{2,1,0:T(8,128)S(1)}, f32[16,28,768]{2,1,0:T(8,128)}, u32[]{:S(2)}) copy-start(f32[16,28,768]{2,1,0:T(8,128)} %fusion.6) | copy-start | bytes 4128772
  292.0 4.5 %copy-start.10 = (f32[16,28,768]{2,1,0:T(8,128)S(1)}, f32[16,28,768]{2,1,0:T(8,128)}, u32[]{:S(2)}) copy-start(f32[16,28,768]{2,1,0:T(8,128)} %fusion.14) | copy-start | bytes 4128772
  302.0 53.1 %all-to-all-start.4 = ((bf16[16,28,2048]{2,1,0:T(8,128)(2,1)}), bf16[16,28,2048]{2,1,0:T(8,128)(2,1)}, u32[]{:S(2)}, u32[]{:S(2)}) async-start(bf16[16,28,2048]{2,1,0:T(8,128)(2,1)} %add_convert_fusion), calls=%async_computation.4 | async-start | bytes 4194304 | tf_op jit(solution)/shard_map/all_to_all | solution.py:70

commit v4 on v0

--- a/solution.py
+++ b/solution.py
@@ -27,6 +27,13 @@
     return hits.reshape(routes.shape[0], 2, experts, capacity)
 
 
+LANES = 128
+
+
+def split_rows(x):
+    return x.reshape(x.shape[:-1] + (x.shape[-1] // LANES, LANES))
+
+
 def scaled_rows(cotangent, probs):
     return (probs[:, :, None] * cotangent[:, None, :].astype(jnp.float32)).astype(jnp.bfloat16)
 
@@ -46,21 +53,22 @@
     return packed.astype(jnp.bfloat16)
 
 
-def recompute(rows, gate_mat, up_mat):
-    contract = (((2,), (0,)), ((), ()))
-    gate_pre = lax.dot_general(rows, gate_mat, contract, preferred_element_type=jnp.float32)
-    up_pre = lax.dot_general(rows, up_mat, contract, preferred_element_type=jnp.float32)
-    return (gate_pre, up_pre)
+def project(rows, mat):
+    return lax.dot_general(
+        rows, mat, (((2, 3), (0, 1)), ((), ())), preferred_element_type=jnp.float32
+    )
 
 
 def backprop(gate_pre, up_pre, scaled, gate_mat, up_mat, down_mat):
-    contract = (((2,), (1,)), ((), ()))
-    d_hidden = lax.dot_general(scaled, down_mat, contract, preferred_element_type=jnp.float32)
+    d_hidden = lax.dot_general(
+        scaled, down_mat, (((2, 3), (1, 2)), ((), ())), preferred_element_type=jnp.float32
+    )
     gate_sig = jax.nn.sigmoid(gate_pre)
     active = gate_pre * gate_sig
     slope = gate_sig * (1.0 + gate_pre * (1.0 - gate_sig))
     d_gate = (d_hidden * up_pre * slope).astype(jnp.bfloat16)
     d_up = (d_hidden * active).astype(jnp.bfloat16)
+    contract = (((2,), (2,)), ((), ()))
     back = lax.dot_general(d_gate, gate_mat, contract, preferred_element_type=jnp.float32)
     back = back + lax.dot_general(d_up, up_mat, contract, preferred_element_type=jnp.float32)
     return back.astype(jnp.bfloat16)
@@ -70,13 +78,19 @@
     return lax.all_to_all(block, "expert", split_axis=0, concat_axis=0, tiled=True)
 
 
-def pick(returned, hits, cotangent):
-    table = jnp.sum(hits, axis=1)
+def beside(send, filler_input, filler, move=exchange):
+    send, filler_input = lax.optimization_barrier((send, filler_input))
+    arrived = move(send)
+    extra = filler(filler_input)
+    return lax.optimization_barrier((arrived, extra))
+
+
+def combine(cotangent, table, returned):
     picked = lax.dot_general(
         table, returned, (((1, 2), (0, 1)), ((), ())), preferred_element_type=jnp.float32
     )
-    summed = cotangent.astype(jnp.float32) + picked
-    return summed.astype(jnp.bfloat16)
+    summed = split_rows(cotangent).astype(jnp.float32) + picked
+    return summed.astype(jnp.bfloat16).reshape(cotangent.shape)
 
 
 def on_device(
@@ -85,37 +99,61 @@
     experts = lax.axis_size("expert")
     tok_count = tokens_a.shape[1]
     width = tokens_a.shape[2]
+    lanes_k = width // LANES
     capacity = 7 * tok_count // (2 * experts)
-    gate_mat = w_gate[0, 0]
-    up_mat = w_up[0, 0]
-    down_mat = w_down[0, 0]
+    gate_mat = w_gate[0, 0].reshape(lanes_k, LANES, -1)
+    up_mat = w_up[0, 0].reshape(lanes_k, LANES, -1)
     first_hits = slot_hits(routes_a[0], experts, capacity)
-    second_hits = slot_hits(routes_b[0], experts, capacity)
     first_cot = cotangent_a[0]
 
-    first_rows = jnp.concatenate(
-        [
-            jnp.broadcast_to(tokens_a[0][:, None, :], (tok_count, 2, width)),
-            scaled_rows(first_cot, probs_a[0]),
-        ],
-        axis=2,
+    first_rows = split_rows(
+        jnp.concatenate(
+            [
+                jnp.broadcast_to(tokens_a[0][:, None, :], (tok_count, 2, width)),
+                scaled_rows(first_cot, probs_a[0]),
+            ],
+            axis=2,
+        )
     )
-    first_arrived = exchange(place(first_hits, first_rows))
-    gate_pre, up_pre = recompute(first_arrived[:, :, :width], gate_mat, up_mat)
-    first_back = backprop(
-        gate_pre, up_pre, first_arrived[:, :, width:], gate_mat, up_mat, down_mat
+
+    def pack_second(pieces):
+        routes, tokens, down = pieces
+        hits = slot_hits(routes, experts, capacity)
+        return hits, place_tokens(split_rows(tokens), hits), split_rows(down)
+
+    first_arrived, (second_hits, second_send, down_mat) = beside(
+        place(first_hits, first_rows), (routes_b[0], tokens_b[0], w_down[0, 0]), pack_second
     )
-    second_tokens = place_tokens(tokens_b[0], second_hits)
-    mixed = exchange(jnp.concatenate([first_back, second_tokens], axis=2))
-    grad_a = pick(mixed[:, :, :width], first_hits, first_cot)
 
-    second_cot = shifted(grad_a, "pipe", -1)
-    second_gate_pre, second_up_pre = recompute(mixed[:, :, width:], gate_mat, up_mat)
-    second_scaled = exchange(place(second_hits, scaled_rows(second_cot, probs_b[0])))
+    def first_compute(arrived):
+        gate_pre = project(arrived[:, :, :lanes_k], gate_mat)
+        up_pre = project(arrived[:, :, :lanes_k], up_mat)
+        return backprop(
+            gate_pre, up_pre, arrived[:, :, lanes_k:], gate_mat, up_mat, down_mat
+        )
+
+    second_tokens, first_back = beside(second_send, first_arrived, first_compute)
+    returned, first_table = beside(first_back, first_hits, lambda hits: jnp.sum(hits, axis=1))
+    grad_a = combine(first_cot, first_table, returned)
+
+    second_cot, second_gate_pre = beside(
+        grad_a,
+        second_tokens,
+        lambda rows: project(rows, gate_mat),
+        move=lambda block: shifted(block, "pipe", -1),
+    )
+    second_scaled, second_up_pre = beside(
+        place(second_hits, split_rows(scaled_rows(second_cot, probs_b[0]))),
+        second_tokens,
+        lambda rows: project(rows, up_mat),
+    )
     second_back = backprop(
         second_gate_pre, second_up_pre, second_scaled, gate_mat, up_mat, down_mat
     )
-    grad_b = pick(exchange(second_back), second_hits, second_cot)
+    second_returned, second_table = beside(
+        second_back, second_hits, lambda hits: jnp.sum(hits, axis=1)
+    )
+    grad_b = combine(second_cot, second_table, second_returned)
     return (grad_a[None], grad_b[None])
 
 

time: 389 us -> 349 us (0.90)
  blocking collectives: 150 us -> 0 us
  waiting for transfers between devices: 144 us -> 213 us
  local copies, waits for them, and re-layouts: 2.5 us -> 33.8 us
  starting transfers between devices: 18.9 us -> 38.9 us
  matrix products: 62.6 us -> 54.6 us
    all_to_all x2 -> x0, blocking collectives: 150 us -> none  [exchange(): lax.all_to_all(block, 'expert', split_axis=0, concat_axis=0, tiled=True)]
    all_to_all x2 -> x5, waiting for transfers between devices: 133 us -> 211 us  [exchange(): lax.all_to_all(block, 'expert', split_axis=0, concat_axis=0, tiled=True)]
    all_to_all x2 -> x5, starting transfers between devices: 13.3 us -> 33.6 us  [exchange(): lax.all_to_all(block, 'expert', split_axis=0, concat_axis=0, tiled=True)]
    optimization_barrier x0 -> x5, local copies, waits for them, and re-layouts: none -> 14.6 us  [beside(): send, filler_input = lax.optimization_barrier((send, filler_input))]
    ppermute x1, waiting for transfers between devices: 11.4 us -> 2.31 us  [shifted(): return lax.ppermute(block, axis, route)]
    unnamed x20 -> x30, local copies, waits for them, and re-layouts: 1.97 us -> 10.7 us
    dot_general x2, matrix products: 18.8 us -> 11.6 us  [backprop(): lax.dot_general(d_gate, gate_mat, contract, preferred_element_type=jnp.fl...]
    convert_element_type x0 -> x3, local copies, waits for them, and re-layouts: none -> 7.05 us  [combine(): summed = split_rows(cotangent).astype(jnp.float32) + picked]
  transfers between devices with their start and end apart: 3 -> 6, of which waited for: 3 -> 6; matrix products, arithmetic and copies ran while one was open for 2% -> 13% of each run, Pallas kernels for 0% -> 0%
where the time goes in v4:
time: 349 us; the launch traced here: 348 us
  waiting for transfers between devices  213 us (61%)
  matrix products  54.6 us (16%)
  starting transfers between devices  38.9 us (11%)
  local copies, waits for them, and re-layouts  33.8 us (10%)
  other arithmetic  6.3 us (2%)
    all_to_all x5, waiting for transfers between devices, exchange(): lax.all_to_all(block, 'expert', split_axis=0, concat_axis=0, tiled=True)  211 us
    all_to_all x5, starting transfers between devices, exchange(): lax.all_to_all(block, 'expert', split_axis=0, concat_axis=0, tiled=True)  33.6 us
    optimization_barrier x5, local copies, waits for them, and re-layouts, beside(): send, filler_input = lax.optimization_barrier((send, filler_input))  14.6 us
    dot_general x3, matrix products, project(): lax.dot_general(rows, mat, (((2, 3), (0, 1)), ((), ())), preferred_elemen...  14.5 us
    dot_general x2, matrix products, backprop(): lax.dot_general(d_gate, gate_mat, contract, preferred_element_type=jnp.fl...  11.6 us
    unnamed x30, local copies, waits for them, and re-layouts  10.7 us
    dot_general x2, matrix products, backprop(): lax.dot_general(scaled, down_mat, (((2, 3), (1, 2)), ((), ())), preferred...  8.94 us
    dot_general x2, matrix products, backprop(): lax.dot_general(d_up, up_mat, contract, preferred_element_type=jnp.float32)  7.77 us
  transfers between devices with their start and end apart: 6, of which 6 were waited for; matrix products, arithmetic and copies ran while one was open for 13% of the time, Pallas kernels for 0%

profile of v4, /device:TPU:64, one launch (start us, length us, event | category | flops | bytes accessed | tf_op | source)
XLA Modules:
  0.0 347.6 jit_solution(708148813000590022)
XLA Ops:
  5.3 2.2 copy.48
  7.6 2.5 copy.53
  13.3 3.3 copy.54
  16.6 8.2 %all-to-all-start = ((bf16[16,28,32,128]{3,2,1,0:T(8,128)(2,1)}), bf16[16,28,32,128]{3,2,1,0:T(8,128)(2,1)}, u32[]{:S(2)}, u32[]{:S(2)}) async-start(bf16[16,28,32,128]{3,2,1,0:T(8,128)(2,1)} %copy.54), calls=%async_computation | async-start | bytes 7340032 | tf_op jit(solution)/shard_map/all_to_all | solution.py:78
  25.1 4.7 %copy.94 = bf16[96,8,16,128]{3,2,1,0:T(8,128)(2,1)} copy(bf16[96,8,16,128]{3,1,2,0:T(8,128)(2,1)} %bitcast.198) | data formatting | bytes 6291456
  30.8 2.1 convolution_convert_fusion
  32.9 73.9 %all-to-all-done = bf16[16,28,32,128]{3,2,1,0:T(8,128)(2,1)} async-done(((bf16[16,28,32,128]{3,2,1,0:T(8,128)(2,1)}), bf16[16,28,32,128]{3,2,1,0:T(8,128)(2,1)}, u32[]{:S(2)}, u32[]{:S(2)}) %all-to-all-start) | async-done | bytes 3670048 | tf_op jit(solution)/shard_map/all_to_all | solution.py:78
  106.9 3.6 %copy.59 = bf16[16,28,16,128]{3,2,1,0:T(8,128)(2,1)} copy(bf16[16,28,16,128]{3,1,2,0:T(8,128)(2,1)} %convolution_convert_fusion) | data formatting | bytes 3670016 | tf_op jit(solution)/shard_map/optimization_barrier | solution.py:82
  110.5 5.2 %all-to-all-start.1 = ((bf16[16,28,16,128]{3,2,1,0:T(8,128)(2,1)}), bf16[16,28,16,128]{3,2,1,0:T(8,128)(2,1)}, u32[]{:S(2)}, u32[]{:S(2)}) async-start(bf16[16,28,16,128]{3,2,1,0:T(8,128)(2,1)} %copy.59), calls=%async_computation.1 | async-start | bytes 3670016 | tf_op jit(solution)/shard_map/all_to_all | solution.py:78
  115.6 5.5 %fusion.2 = f32[16,28,768,1]{2,1,3,0:T(8,128)} fusion(bf16[16,128,768,1]{2,1,0,3:T(8,128)(2,1)} %bitcast.216, bf16[16,28,32,128]{3,2,1,0:T(8,128)(2,1)} %all-to-all-done), kind=kOutput, calls=%fused_computation.6 | convolution fusion | flops 1409286144 | bytes 8192000 | tf_op jit(solution)/shard_map/dot_general | solution.py:57
  121.2 4.5 %fusion.4 = f32[16,28,768,1]{2,1,3,0:T(8,128)} fusion(bf16[16,28,32,128]{3,2,1,0:T(8,128)(2,1)} %all-to-all-done, bf16[768,16,128]{2,1,0:T(8,128)(2,1)S(1)} %bitcast.200), kind=kOutput, calls=%fused_computation.8 | convolution fusion | flops 1409286144 | bytes 8192000 | tf_op jit(solution)/shard_map/dot_general | solution.py:63
  125.7 9.4 %fusion.64 = f32[16,28,16,128]{3,1,2,0:T(8,128)} fusion(bf16[16,128,768,1]{2,1,0,3:T(8,128)(2,1)} %bitcast.217, f32[16,28,768,1]{2,1,3,0:T(8,128)} %fusion.2, bf16[16,128,768,1]{2,1,0,3:T(8,128)(2,1)S(1)} %bitcast.192, bf16[16,28,32,128]{3,2,1,0:T(8,128)(2,1)} %all-to-all-done, f32[16,28,768,1]{2,1,3,0:T(8,128)} %fusion.4), kind=kOutput, calls=%fused_computation.58 | convolution fusion | flops 2822012928 | bytes 16384000 | tf_op jit(solution)/shard_map/dot_general | solution.py:72
  135.1 5.6 %add_convert_fusion.1 = bf16[16,28,16,128]{3,1,2,0:T(8,128)(2,1)} fusion(f32[16,28,16,128]{3,1,2,0:T(8,128)} %fusion.64, bf16[16,128,768,1]{2,1,0,3:T(8,128)(2,1)S(1)} %bitcast.193, f32[16,28,768,1]{2,1,3,0:T(8,128)} %fusion.2, f32[16,28,768,1]{2,1,3,0:T(8,128)} %fusion.4), kind=kOutput, calls=%fused_computation.3 | convolution fusion | flops 1413185536 | bytes 11403264 | tf_op jit(solution)/shard_map/dot_general | solution.py:73
  140.7 16.9 %all-to-all-done.1 = bf16[16,28,16,128]{3,2,1,0:T(8,128)(2,1)} async-done(((bf16[16,28,16,128]{3,2,1,0:T(8,128)(2,1)}), bf16[16,28,16,128]{3,2,1,0:T(8,128)(2,1)}, u32[]{:S(2)}, u32[]{:S(2)}) %all-to-all-start.1) | async-done | bytes 1835040 | tf_op jit(solution)/shard_map/all_to_all | solution.py:78
  157.6 3.6 %copy.63 = bf16[16,28,16,128]{3,2,1,0:T(8,128)(2,1)} copy(bf16[16,28,16,128]{3,1,2,0:T(8,128)(2,1)} %add_convert_fusion.1) | data formatting | bytes 3670016 | tf_op jit(solution)/shard_map/optimization_barrier | solution.py:82
  161.2 5.1 %all-to-all-start.2 = ((bf16[16,28,16,128]{3,2,1,0:T(8,128)(2,1)}), bf16[16,28,16,128]{3,2,1,0:T(8,128)(2,1)}, u32[]{:S(2)}, u32[]{:S(2)}) async-start(bf16[16,28,16,128]{3,2,1,0:T(8,128)(2,1)} %copy.63), calls=%async_computation.2 | async-start | bytes 3670016 | tf_op jit(solution)/shard_map/all_to_all | solution.py:78
  167.3 40.9 %all-to-all-done.2 = bf16[16,28,16,128]{3,2,1,0:T(8,128)(2,1)} async-done(((bf16[16,28,16,128]{3,2,1,0:T(8,128)(2,1)}), bf16[16,28,16,128]{3,2,1,0:T(8,128)(2,1)}, u32[]{:S(2)}, u32[]{:S(2)}) %all-to-all-start.2) | async-done | bytes 1835040 | tf_op jit(solution)/shard_map/all_to_all | solution.py:78
  208.2 3.0 fusion.54
  211.2 5.2 %collective-permute-start = (bf16[128,2048]{0,1:T(8,128)(2,1)S(1)}, bf16[128,2048]{0,1:T(8,128)(2,1)S(1)}, u32[]{:S(2)}, u32[]{:S(2)}) collective-permute-start(bf16[128,2048]{0,1:T(8,128)(2,1)S(1)} %bitcast.202), channel_id=1, source_target_pairs={{16,0},{32,16},{48,32},{64,48},{80,64},{96,80},{112,96},{128,112},... | collective-permute-start | bytes 1572872 | tf_op jit(solution)/shard_map/ppermute | solution.py:10
  216.5 4.5 %fusion.36 = f32[16,28,768]{2,1,0:T(8,128)} fusion(bf16[16,128,768,1]{2,1,0,3:T(8,128)(2,1)S(1)} %bitcast.218, bf16[16,28,16,128]{3,2,1,0:T(8,128)(2,1)} %all-to-all-done.1), kind=kOutput, calls=%fused_computation.49 | convolution fusion | flops 1409286144 | bytes 6356992 | tf_op jit(solution)/shard_map/dot_general | solution.py:57
  220.9 2.3 collective-permute-done
  224.0 2.3 copy.66
  230.3 10.0 %all-to-all-start.3 = ((bf16[16,28,16,128]{3,2,1,0:T(8,128)(2,1)}), bf16[16,28,16,128]{3,2,1,0:T(8,128)(2,1)}, u32[]{:S(2)}, u32[]{:S(2)}) async-start(bf16[16,28,16,128]{3,2,1,0:T(8,128)(2,1)} %copy.67), calls=%async_computation.3 | async-start | bytes 3670016 | tf_op jit(solution)/shard_map/all_to_all | solution.py:78
  240.4 4.5 %fusion.39 = f32[16,28,768]{2,1,0:T(8,128)} fusion(bf16[16,128,768,1]{2,1,0,3:T(8,128)(2,1)S(1)} %bitcast.194, bf16[16,28,16,128]{3,2,1,0:T(8,128)(2,1)} %all-to-all-done.1), kind=kOutput, calls=%fused_computation.50 | convolution fusion | flops 1409286144 | bytes 6356992 | tf_op jit(solution)/shard_map/dot_general | solution.py:57
  244.9 38.9 %all-to-all-done.3 = bf16[16,28,16,128]{3,2,1,0:T(8,128)(2,1)} async-done(((bf16[16,28,16,128]{3,2,1,0:T(8,128)(2,1)}), bf16[16,28,16,128]{3,2,1,0:T(8,128)(2,1)}, u32[]{:S(2)}, u32[]{:S(2)}) %all-to-all-start.3) | async-done | bytes 1835040 | tf_op jit(solution)/shard_map/all_to_all | solution.py:78
  283.8 4.4 %fusion.6 = f32[16,28,768,1]{2,1,3,0:T(8,128)S(1)} fusion(bf16[768,16,128]{2,1,0:T(8,128)(2,1)} %bitcast.199, bf16[16,28,16,128]{3,2,1,0:T(8,128)(2,1)} %all-to-all-done.3), kind=kOutput, calls=%fused_computation.10 | convolution fusion | flops 1409286144 | bytes 6356992 | tf_op jit(solution)/shard_map/dot_general | solution.py:63
  288.3 2.2 fusion.71
  290.5 2.2 add_convert_fusion
  294.7 5.2 %all-to-all-start.4 = ((bf16[16,28,16,128]{3,2,1,0:T(8,128)(2,1)}), bf16[16,28,16,128]{3,2,1,0:T(8,128)(2,1)}, u32[]{:S(2)}, u32[]{:S(2)}) async-start(bf16[16,28,16,128]{3,2,1,0:T(8,128)(2,1)} %copy.71), calls=%async_computation.4 | async-start | bytes 3670016 | tf_op jit(solution)/shard_map/all_to_all | solution.py:78
  299.8 2.0 copy.73
  301.9 40.2 %all-to-all-done.4 = bf16[16,28,16,128]{3,2,1,0:T(8,128)(2,1)} async-done(((bf16[16,28,16,128]{3,2,1,0:T(8,128)(2,1)}), bf16[16,28,16,128]{3,2,1,0:T(8,128)(2,1)}, u32[]{:S(2)}, u32[]{:S(2)}) %all-to-all-start.4) | async-done | bytes 1835040 | tf_op jit(solution)/shard_map/all_to_all | solution.py:78
  342.1 3.4 fusion.57
  (54 shorter events, 19.1 us)
Async XLA Ops:
  0.6 125.1 %copy-start = (bf16[1,1,2048,768]{3,2,1,0:T(8,128)(2,1)S(1)}, bf16[1,1,2048,768]{3,2,1,0:T(8,128)(2,1)}, u32[]{:S(2)}) copy-start(bf16[1,1,2048,768]{3,2,1,0:T(8,128)(2,1)} %param.18) | copy-start | bytes 9437188
  5.3 4.8 %copy-start.8 = (f32[1,128,2]{1,2,0:T(2,128)S(1)}, f32[1,128,2]{1,2,0:T(2,128)}, u32[]{:S(2)}) copy-start(f32[1,128,2]{1,2,0:T(2,128)} %param.15) | copy-start | bytes 3076
  10.1 1.6 copy-start.2
  16.6 8.2 %copy-start.6 = (s32[1,128,2]{1,2,0:T(2,128)S(1)}, s32[1,128,2]{1,2,0:T(2,128)}, u32[]{:S(2)}) copy-start(s32[1,128,2]{1,2,0:T(2,128)} %param.14) | copy-start | bytes 3076
  16.6 90.3 %all-to-all-start = ((bf16[16,28,32,128]{3,2,1,0:T(8,128)(2,1)}), bf16[16,28,32,128]{3,2,1,0:T(8,128)(2,1)}, u32[]{:S(2)}, u32[]{:S(2)}) async-start(bf16[16,28,32,128]{3,2,1,0:T(8,128)(2,1)} %copy.54), calls=%async_computation | async-start | bytes 7340032 | tf_op jit(solution)/shard_map/all_to_all | solution.py:78
  25.1 5.7 %copy-start.5 = (bf16[1,128,2048]{2,1,0:T(8,128)(2,1)S(1)}, bf16[1,128,2048]{2,1,0:T(8,128)(2,1)}, u32[]{:S(2)}) copy-start(bf16[1,128,2048]{2,1,0:T(8,128)(2,1)} %param.12) | copy-start | bytes 1572868
  110.5 47.1 %all-to-all-start.1 = ((bf16[16,28,16,128]{3,2,1,0:T(8,128)(2,1)}), bf16[16,28,16,128]{3,2,1,0:T(8,128)(2,1)}, u32[]{:S(2)}, u32[]{:S(2)}) async-start(bf16[16,28,16,128]{3,2,1,0:T(8,128)(2,1)} %copy.59), calls=%async_computation.1 | async-start | bytes 3670016 | tf_op jit(solution)/shard_map/all_to_all | solution.py:78
  115.6 5.5 %copy-start.1 = (bf16[96,8,16,128]{3,2,1,0:T(8,128)(2,1)S(1)}, bf16[96,8,16,128]{3,2,1,0:T(8,128)(2,1)}, u32[]{:S(2)}) copy-start(bf16[96,8,16,128]{3,2,1,0:T(8,128)(2,1)} %copy.94) | copy-start | bytes 9437188
  161.2 47.0 %all-to-all-start.2 = ((bf16[16,28,16,128]{3,2,1,0:T(8,128)(2,1)}), bf16[16,28,16,128]{3,2,1,0:T(8,128)(2,1)}, u32[]{:S(2)}, u32[]{:S(2)}) async-start(bf16[16,28,16,128]{3,2,1,0:T(8,128)(2,1)} %copy.63), calls=%async_computation.2 | async-start | bytes 3670016 | tf_op jit(solution)/shard_map/all_to_all | solution.py:78
  208.2 8.2 %copy-start.9 = (bf16[1,1,2048,768]{3,2,1,0:T(8,128)(2,1)S(1)}, bf16[1,1,2048,768]{3,2,1,0:T(8,128)(2,1)}, u32[]{:S(2)}) copy-start(bf16[1,1,2048,768]{3,2,1,0:T(8,128)(2,1)} %param.17) | copy-start | bytes 9437188
  211.2 9.7 %copy-start.3 = (bf16[128,16,128]{0,2,1:T(8,128)(2,1)}, bf16[128,16,128]{0,2,1:T(8,128)(2,1)S(1)}, u32[]{:S(2)}) copy-start(bf16[128,16,128]{0,2,1:T(8,128)(2,1)S(1)} %fusion.54) | copy-start | bytes 1572868
  211.2 15.1 %copy-start.7 = (f32[1,128,2]{1,2,0:T(2,128)S(1)}, f32[1,128,2]{1,2,0:T(2,128)}, u32[]{:S(2)}) copy-start(f32[1,128,2]{1,2,0:T(2,128)} %param.16) | copy-start | bytes 3076
  211.2 12.0 %collective-permute-start = (bf16[128,2048]{0,1:T(8,128)(2,1)S(1)}, bf16[128,2048]{0,1:T(8,128)(2,1)S(1)}, u32[]{:S(2)}, u32[]{:S(2)}) collective-permute-start(bf16[128,2048]{0,1:T(8,128)(2,1)S(1)} %bitcast.202), channel_id=1, source_target_pairs={{16,0},{32,16},{48,32},{64,48},{80,64},{96,80},{112,96},{128,112},... | collective-permute-start | bytes 1572872 | tf_op jit(solution)/shard_map/ppermute | solution.py:10
  223.2 0.8 copy-start.4
  230.3 53.5 %all-to-all-start.3 = ((bf16[16,28,16,128]{3,2,1,0:T(8,128)(2,1)}), bf16[16,28,16,128]{3,2,1,0:T(8,128)(2,1)}, u32[]{:S(2)}, u32[]{:S(2)}) async-start(bf16[16,28,16,128]{3,2,1,0:T(8,128)(2,1)} %copy.67), calls=%async_computation.3 | async-start | bytes 3670016 | tf_op jit(solution)/shard_map/all_to_all | solution.py:78
  283.8 4.4 %copy-start.10 = (bf16[1,1,2048,768]{3,2,1,0:T(8,128)(2,1)S(1)}, bf16[1,1,2048,768]{3,2,1,0:T(8,128)(2,1)}, u32[]{:S(2)}) copy-start(bf16[1,1,2048,768]{3,2,1,0:T(8,128)(2,1)} %param.17) | copy-start | bytes 9437188
  283.8 4.4 %copy-start.11 = (f32[16,28,768]{2,1,0:T(8,128)S(1)}, f32[16,28,768]{2,1,0:T(8,128)}, u32[]{:S(2)}) copy-start(f32[16,28,768]{2,1,0:T(8,128)} %fusion.36) | copy-start | bytes 4128772
  283.8 4.4 %copy-start.12 = (f32[16,28,768]{2,1,0:T(8,128)S(1)}, f32[16,28,768]{2,1,0:T(8,128)}, u32[]{:S(2)}) copy-start(f32[16,28,768]{2,1,0:T(8,128)} %fusion.39) | copy-start | bytes 4128772
  294.7 47.5 %all-to-all-start.4 = ((bf16[16,28,16,128]{3,2,1,0:T(8,128)(2,1)}), bf16[16,28,16,128]{3,2,1,0:T(8,128)(2,1)}, u32[]{:S(2)}, u32[]{:S(2)}) async-start(bf16[16,28,16,128]{3,2,1,0:T(8,128)(2,1)} %copy.71), calls=%async_computation.4 | async-start | bytes 3670016 | tf_op jit(solution)/shard_map/all_to_all | solution.py:78

commit v5 on v4

--- a/solution.py
+++ b/solution.py
@@ -35,7 +35,8 @@
 
 
 def scaled_rows(cotangent, probs):
-    return (probs[:, :, None] * cotangent[:, None, :].astype(jnp.float32)).astype(jnp.bfloat16)
+    scaled = probs[:, :, None, None] * cotangent[:, None].astype(jnp.float32)
+    return scaled.astype(jnp.bfloat16)
 
 
 def place(hits, rows):
@@ -89,8 +90,8 @@
     picked = lax.dot_general(
         table, returned, (((1, 2), (0, 1)), ((), ())), preferred_element_type=jnp.float32
     )
-    summed = split_rows(cotangent).astype(jnp.float32) + picked
-    return summed.astype(jnp.bfloat16).reshape(cotangent.shape)
+    summed = cotangent.astype(jnp.float32) + picked
+    return summed.astype(jnp.bfloat16)
 
 
 def on_device(
@@ -104,16 +105,16 @@
     gate_mat = w_gate[0, 0].reshape(lanes_k, LANES, -1)
     up_mat = w_up[0, 0].reshape(lanes_k, LANES, -1)
     first_hits = slot_hits(routes_a[0], experts, capacity)
-    first_cot = cotangent_a[0]
+    first_cot, first_tok = lax.optimization_barrier(
+        (split_rows(cotangent_a[0]), split_rows(tokens_a[0]))
+    )
 
-    first_rows = split_rows(
-        jnp.concatenate(
-            [
-                jnp.broadcast_to(tokens_a[0][:, None, :], (tok_count, 2, width)),
-                scaled_rows(first_cot, probs_a[0]),
-            ],
-            axis=2,
-        )
+    first_rows = jnp.concatenate(
+        [
+            jnp.broadcast_to(first_tok[:, None], (tok_count, 2, lanes_k, LANES)),
+            scaled_rows(first_cot, probs_a[0]),
+        ],
+        axis=2,
     )
 
     def pack_second(pieces):
@@ -136,24 +137,24 @@
     returned, first_table = beside(first_back, first_hits, lambda hits: jnp.sum(hits, axis=1))
     grad_a = combine(first_cot, first_table, returned)
 
-    second_cot, second_gate_pre = beside(
+    second_cot, (second_gate_pre, second_up_pre) = beside(
         grad_a,
         second_tokens,
-        lambda rows: project(rows, gate_mat),
+        lambda rows: (project(rows, gate_mat), project(rows, up_mat)),
         move=lambda block: shifted(block, "pipe", -1),
     )
-    second_scaled, second_up_pre = beside(
-        place(second_hits, split_rows(scaled_rows(second_cot, probs_b[0]))),
-        second_tokens,
-        lambda rows: project(rows, up_mat),
+    second_scaled, second_table = beside(
+        place(second_hits, scaled_rows(second_cot, probs_b[0])),
+        second_hits,
+        lambda hits: jnp.sum(hits, axis=1),
     )
     second_back = backprop(
         second_gate_pre, second_up_pre, second_scaled, gate_mat, up_mat, down_mat
     )
-    second_returned, second_table = beside(
-        second_back, second_hits, lambda hits: jnp.sum(hits, axis=1)
+    second_returned, grad_a = beside(
+        second_back, grad_a, lambda rows: rows.reshape(tok_count, width)
     )
-    grad_b = combine(second_cot, second_table, second_returned)
+    grad_b = combine(second_cot, second_table, second_returned).reshape(tok_count, width)
     return (grad_a[None], grad_b[None])
 
 

time: 349 us -> 349 us (level)
    convert_element_type x3 -> x1, local copies, waits for them, and re-layouts: 7.05 us -> 2.04 us  [combine(): return summed.astype(jnp.bfloat16)]
    all_to_all x5, waiting for transfers between devices: 211 us -> 215 us  [exchange(): lax.all_to_all(block, 'expert', split_axis=0, concat_axis=0, tiled=True)]
    optimization_barrier x0 -> x2, local copies, waits for them, and re-layouts: none -> 4.02 us  [on_device(): lax.optimization_barrier((split_rows(cotangent_a[0]), split_rows(tokens_a...]
    unnamed x30 -> x31, local copies, waits for them, and re-layouts: 10.7 us -> 13.5 us
    optimization_barrier x5 -> x6, local copies, waits for them, and re-layouts: 14.6 us -> 16.8 us  [beside(): send, filler_input = lax.optimization_barrier((send, filler_input))]
  transfers between devices with their start and end apart: 6 -> 6, of which waited for: 6 -> 5; matrix products, arithmetic and copies ran while one was open for 13% -> 13% of each run, Pallas kernels for 0% -> 0%
where the time goes in v5:
time: 349 us; the launch traced here: 348 us
  waiting for transfers between devices  215 us (62%)
  matrix products  51.8 us (15%)
  local copies, waits for them, and re-layouts  36.8 us (11%)
  starting transfers between devices  36.7 us (11%)
  other arithmetic  6.3 us (2%)
    all_to_all x5, waiting for transfers between devices, exchange(): lax.all_to_all(block, 'expert', split_axis=0, concat_axis=0, tiled=True)  215 us
    all_to_all x5, starting transfers between devices, exchange(): lax.all_to_all(block, 'expert', split_axis=0, concat_axis=0, tiled=True)  31.5 us
    optimization_barrier x6, local copies, waits for them, and re-layouts, beside(): send, filler_input = lax.optimization_barrier((send, filler_input))  16.8 us
    dot_general x3, matrix products, project(): lax.dot_general(rows, mat, (((2, 3), (0, 1)), ((), ())), preferred_elemen...  14.5 us
    unnamed x31, local copies, waits for them, and re-layouts  13.5 us
    dot_general x2, matrix products, backprop(): lax.dot_general(d_gate, gate_mat, contract, preferred_element_type=jnp.fl...  11.6 us
    dot_general x2, matrix products, backprop(): lax.dot_general(scaled, down_mat, (((2, 3), (1, 2)), ((), ())), preferred...  8.91 us
    dot_general x2, matrix products, backprop(): lax.dot_general(d_up, up_mat, contract, preferred_element_type=jnp.float32)  7.76 us
  transfers between devices with their start and end apart: 6, of which 5 were waited for; matrix products, arithmetic and copies ran while one was open for 13% of the time, Pallas kernels for 0%

profile of v5, /device:TPU:64, one launch (start us, length us, event | category | flops | bytes accessed | tf_op | source)
XLA Modules:
  0.0 347.9 jit_solution(1693458889682652709)
XLA Ops:
  5.2 2.0 copy.64
  9.2 2.0 copy.66
  14.3 3.4 copy.67
  17.7 8.2 %all-to-all-start = ((bf16[16,28,32,128]{3,2,1,0:T(8,128)(2,1)}), bf16[16,28,32,128]{3,2,1,0:T(8,128)(2,1)}, u32[]{:S(2)}, u32[]{:S(2)}) async-start(bf16[16,28,32,128]{3,2,1,0:T(8,128)(2,1)} %copy.67), calls=%async_computation | async-start | bytes 7340032 | tf_op jit(solution)/shard_map/all_to_all | solution.py:79
  26.2 4.7 %copy.110 = bf16[96,8,16,128]{3,2,1,0:T(8,128)(2,1)} copy(bf16[96,8,16,128]{3,1,2,0:T(8,128)(2,1)} %bitcast.193) | data formatting | bytes 6291456
  33.9 74.0 %all-to-all-done = bf16[16,28,32,128]{3,2,1,0:T(8,128)(2,1)} async-done(((bf16[16,28,32,128]{3,2,1,0:T(8,128)(2,1)}), bf16[16,28,32,128]{3,2,1,0:T(8,128)(2,1)}, u32[]{:S(2)}, u32[]{:S(2)}) %all-to-all-start) | async-done | bytes 3670048 | tf_op jit(solution)/shard_map/all_to_all | solution.py:79
  107.9 3.7 %copy.72 = bf16[16,28,16,128]{3,2,1,0:T(8,128)(2,1)} copy(bf16[16,28,16,128]{3,1,2,0:T(8,128)(2,1)} %convolution_convert_fusion) | data formatting | bytes 3670016 | tf_op jit(solution)/shard_map/optimization_barrier | solution.py:83
  111.6 5.2 %all-to-all-start.1 = ((bf16[16,28,16,128]{3,2,1,0:T(8,128)(2,1)}), bf16[16,28,16,128]{3,2,1,0:T(8,128)(2,1)}, u32[]{:S(2)}, u32[]{:S(2)}) async-start(bf16[16,28,16,128]{3,2,1,0:T(8,128)(2,1)} %copy.72), calls=%async_computation.1 | async-start | bytes 3670016 | tf_op jit(solution)/shard_map/all_to_all | solution.py:79
  116.8 5.6 %fusion.2 = f32[16,28,768,1]{2,1,3,0:T(8,128)} fusion(bf16[16,128,768,1]{2,1,0,3:T(8,128)(2,1)} %bitcast.209, bf16[16,28,32,128]{3,2,1,0:T(8,128)(2,1)} %all-to-all-done), kind=kOutput, calls=%fused_computation.6 | convolution fusion | flops 1409286144 | bytes 8192000 | tf_op jit(solution)/shard_map/dot_general | solution.py:58
  122.3 4.5 %fusion.4 = f32[16,28,768,1]{2,1,3,0:T(8,128)} fusion(bf16[16,28,32,128]{3,2,1,0:T(8,128)(2,1)} %all-to-all-done, bf16[768,16,128]{2,1,0:T(8,128)(2,1)S(1)} %bitcast.195), kind=kOutput, calls=%fused_computation.8 | convolution fusion | flops 1409286144 | bytes 8192000 | tf_op jit(solution)/shard_map/dot_general | solution.py:64
  126.8 9.4 %fusion.64 = f32[16,28,16,128]{3,1,2,0:T(8,128)} fusion(bf16[16,128,768,1]{2,1,0,3:T(8,128)(2,1)} %bitcast.210, f32[16,28,768,1]{2,1,3,0:T(8,128)} %fusion.2, bf16[16,128,768,1]{2,1,0,3:T(8,128)(2,1)S(1)} %bitcast.189, bf16[16,28,32,128]{3,2,1,0:T(8,128)(2,1)} %all-to-all-done, f32[16,28,768,1]{2,1,3,0:T(8,128)} %fusion.4), kind=kOutput, calls=%fused_computation.58 | convolution fusion | flops 2822012928 | bytes 16384000 | tf_op jit(solution)/shard_map/dot_general | solution.py:73
  136.3 5.6 %add_convert_fusion.1 = bf16[16,28,16,128]{3,1,2,0:T(8,128)(2,1)} fusion(f32[16,28,16,128]{3,1,2,0:T(8,128)} %fusion.64, bf16[16,128,768,1]{2,1,0,3:T(8,128)(2,1)S(1)} %bitcast.190, f32[16,28,768,1]{2,1,3,0:T(8,128)} %fusion.2, f32[16,28,768,1]{2,1,3,0:T(8,128)} %fusion.4), kind=kOutput, calls=%fused_computation.3 | convolution fusion | flops 1413185536 | bytes 11403264 | tf_op jit(solution)/shard_map/dot_general | solution.py:74
  141.9 16.9 %all-to-all-done.1 = bf16[16,28,16,128]{3,2,1,0:T(8,128)(2,1)} async-done(((bf16[16,28,16,128]{3,2,1,0:T(8,128)(2,1)}), bf16[16,28,16,128]{3,2,1,0:T(8,128)(2,1)}, u32[]{:S(2)}, u32[]{:S(2)}) %all-to-all-start.1) | async-done | bytes 1835040 | tf_op jit(solution)/shard_map/all_to_all | solution.py:79
  158.8 3.7 %copy.76 = bf16[16,28,16,128]{3,2,1,0:T(8,128)(2,1)} copy(bf16[16,28,16,128]{3,1,2,0:T(8,128)(2,1)} %add_convert_fusion.1) | data formatting | bytes 3670016 | tf_op jit(solution)/shard_map/optimization_barrier | solution.py:83
  162.4 5.1 %all-to-all-start.2 = ((bf16[16,28,16,128]{3,2,1,0:T(8,128)(2,1)}), bf16[16,28,16,128]{3,2,1,0:T(8,128)(2,1)}, u32[]{:S(2)}, u32[]{:S(2)}) async-start(bf16[16,28,16,128]{3,2,1,0:T(8,128)(2,1)} %copy.76), calls=%async_computation.2 | async-start | bytes 3670016 | tf_op jit(solution)/shard_map/all_to_all | solution.py:79
  168.5 40.9 %all-to-all-done.2 = bf16[16,28,16,128]{3,2,1,0:T(8,128)(2,1)} async-done(((bf16[16,28,16,128]{3,2,1,0:T(8,128)(2,1)}), bf16[16,28,16,128]{3,2,1,0:T(8,128)(2,1)}, u32[]{:S(2)}, u32[]{:S(2)}) %all-to-all-start.2) | async-done | bytes 1835040 | tf_op jit(solution)/shard_map/all_to_all | solution.py:79
  209.4 2.1 fusion.54
  211.5 5.2 %collective-permute-start = (bf16[128,16,128]{2,0,1:T(8,128)(2,1)S(1)}, bf16[128,16,128]{2,0,1:T(8,128)(2,1)S(1)}, u32[]{:S(2)}, u32[]{:S(2)}) collective-permute-start(bf16[128,16,128]{2,0,1:T(8,128)(2,1)S(1)} %fusion.54), channel_id=1, source_target_pairs={{16,0},{32,16},{48,32},{64,48},{80,64},{96,80},{112,96},{128,112},... | collective-permute-start | bytes 1572872 | tf_op jit(solution)/shard_map/ppermute | solution.py:10
  216.8 4.5 %fusion.39 = f32[16,28,768]{2,1,0:T(8,128)} fusion(bf16[16,128,768,1]{2,1,0,3:T(8,128)(2,1)S(1)} %bitcast.191, bf16[16,28,16,128]{3,2,1,0:T(8,128)(2,1)} %all-to-all-done.1), kind=kOutput, calls=%fused_computation.50 | convolution fusion | flops 1409286144 | bytes 6356992 | tf_op jit(solution)/shard_map/dot_general | solution.py:58
  221.3 4.5 %fusion.36 = f32[16,28,768]{2,1,0:T(8,128)} fusion(bf16[16,128,768,1]{2,1,0,3:T(8,128)(2,1)S(1)} %bitcast.211, bf16[16,28,16,128]{3,2,1,0:T(8,128)(2,1)} %all-to-all-done.1), kind=kOutput, calls=%fused_computation.49 | convolution fusion | flops 1409286144 | bytes 6356992 | tf_op jit(solution)/shard_map/dot_general | solution.py:58
  229.3 7.9 %all-to-all-start.3 = ((bf16[16,28,16,128]{3,2,1,0:T(8,128)(2,1)}), bf16[16,28,16,128]{3,2,1,0:T(8,128)(2,1)}, u32[]{:S(2)}, u32[]{:S(2)}) async-start(bf16[16,28,16,128]{3,2,1,0:T(8,128)(2,1)} %copy.80), calls=%async_computation.3 | async-start | bytes 3670016 | tf_op jit(solution)/shard_map/all_to_all | solution.py:79
  237.2 43.4 %all-to-all-done.3 = bf16[16,28,16,128]{3,2,1,0:T(8,128)(2,1)} async-done(((bf16[16,28,16,128]{3,2,1,0:T(8,128)(2,1)}), bf16[16,28,16,128]{3,2,1,0:T(8,128)(2,1)}, u32[]{:S(2)}, u32[]{:S(2)}) %all-to-all-start.3) | async-done | bytes 1835040 | tf_op jit(solution)/shard_map/all_to_all | solution.py:79
  280.6 4.4 %fusion.6 = f32[16,28,768,1]{2,1,3,0:T(8,128)S(1)} fusion(bf16[768,16,128]{2,1,0:T(8,128)(2,1)} %bitcast.194, bf16[16,28,16,128]{3,2,1,0:T(8,128)(2,1)} %all-to-all-done.3), kind=kOutput, calls=%fused_computation.10 | convolution fusion | flops 1409286144 | bytes 6356992 | tf_op jit(solution)/shard_map/dot_general | solution.py:64
  285.1 2.2 fusion.71
  287.3 2.2 add_convert_fusion
  291.5 5.2 %all-to-all-start.4 = ((bf16[16,28,16,128]{3,2,1,0:T(8,128)(2,1)}), bf16[16,28,16,128]{3,2,1,0:T(8,128)(2,1)}, u32[]{:S(2)}, u32[]{:S(2)}) async-start(bf16[16,28,16,128]{3,2,1,0:T(8,128)(2,1)} %copy.83), calls=%async_computation.4 | async-start | bytes 3670016 | tf_op jit(solution)/shard_map/all_to_all | solution.py:79
  296.7 2.1 copy.84
  298.7 40.2 %all-to-all-done.4 = bf16[16,28,16,128]{3,2,1,0:T(8,128)(2,1)} async-done(((bf16[16,28,16,128]{3,2,1,0:T(8,128)(2,1)}), bf16[16,28,16,128]{3,2,1,0:T(8,128)(2,1)}, u32[]{:S(2)}, u32[]{:S(2)}) %all-to-all-start.4) | async-done | bytes 1835040 | tf_op jit(solution)/shard_map/all_to_all | solution.py:79
  339.0 2.0 copy.88
  341.0 2.9 fusion.57
  343.9 2.0 copy.87
  345.9 2.0 copy.89
  (57 shorter events, 19.6 us)
Async XLA Ops:
  0.6 126.2 %copy-start = (bf16[1,1,2048,768]{3,2,1,0:T(8,128)(2,1)S(1)}, bf16[1,1,2048,768]{3,2,1,0:T(8,128)(2,1)}, u32[]{:S(2)}) copy-start(bf16[1,1,2048,768]{3,2,1,0:T(8,128)(2,1)} %param.18) | copy-start | bytes 9437188
  7.2 5.2 %copy-start.8 = (f32[1,128,2]{1,2,0:T(2,128)S(1)}, f32[1,128,2]{1,2,0:T(2,128)}, u32[]{:S(2)}) copy-start(f32[1,128,2]{1,2,0:T(2,128)} %param.15) | copy-start | bytes 3076
  11.2 1.5 copy-start.4
  17.7 8.2 %copy-start.6 = (s32[1,128,2]{1,2,0:T(2,128)S(1)}, s32[1,128,2]{1,2,0:T(2,128)}, u32[]{:S(2)}) copy-start(s32[1,128,2]{1,2,0:T(2,128)} %param.14) | copy-start | bytes 3076
  17.7 90.3 %all-to-all-start = ((bf16[16,28,32,128]{3,2,1,0:T(8,128)(2,1)}), bf16[16,28,32,128]{3,2,1,0:T(8,128)(2,1)}, u32[]{:S(2)}, u32[]{:S(2)}) async-start(bf16[16,28,32,128]{3,2,1,0:T(8,128)(2,1)} %copy.67), calls=%async_computation | async-start | bytes 7340032 | tf_op jit(solution)/shard_map/all_to_all | solution.py:79
  26.2 5.7 %copy-start.5 = (bf16[1,128,2048]{2,1,0:T(8,128)(2,1)S(1)}, bf16[1,128,2048]{2,1,0:T(8,128)(2,1)}, u32[]{:S(2)}) copy-start(bf16[1,128,2048]{2,1,0:T(8,128)(2,1)} %param.12) | copy-start | bytes 1572868
  111.6 47.1 %all-to-all-start.1 = ((bf16[16,28,16,128]{3,2,1,0:T(8,128)(2,1)}), bf16[16,28,16,128]{3,2,1,0:T(8,128)(2,1)}, u32[]{:S(2)}, u32[]{:S(2)}) async-start(bf16[16,28,16,128]{3,2,1,0:T(8,128)(2,1)} %copy.72), calls=%async_computation.1 | async-start | bytes 3670016 | tf_op jit(solution)/shard_map/all_to_all | solution.py:79
  116.8 5.6 %copy-start.1 = (bf16[96,8,16,128]{3,2,1,0:T(8,128)(2,1)S(1)}, bf16[96,8,16,128]{3,2,1,0:T(8,128)(2,1)}, u32[]{:S(2)}) copy-start(bf16[96,8,16,128]{3,2,1,0:T(8,128)(2,1)} %copy.110) | copy-start | bytes 9437188
  162.4 47.0 %all-to-all-start.2 = ((bf16[16,28,16,128]{3,2,1,0:T(8,128)(2,1)}), bf16[16,28,16,128]{3,2,1,0:T(8,128)(2,1)}, u32[]{:S(2)}, u32[]{:S(2)}) async-start(bf16[16,28,16,128]{3,2,1,0:T(8,128)(2,1)} %copy.76), calls=%async_computation.2 | async-start | bytes 3670016 | tf_op jit(solution)/shard_map/all_to_all | solution.py:79
  211.5 9.8 %copy-start.3 = (bf16[128,16,128]{2,0,1:T(8,128)(2,1)}, bf16[128,16,128]{2,0,1:T(8,128)(2,1)S(1)}, u32[]{:S(2)}) copy-start(bf16[128,16,128]{2,0,1:T(8,128)(2,1)S(1)} %fusion.54) | copy-start | bytes 1572868
  211.5 9.7 %copy-start.9 = (bf16[1,1,2048,768]{3,2,1,0:T(8,128)(2,1)S(1)}, bf16[1,1,2048,768]{3,2,1,0:T(8,128)(2,1)}, u32[]{:S(2)}) copy-start(bf16[1,1,2048,768]{3,2,1,0:T(8,128)(2,1)} %param.17) | copy-start | bytes 9437188
  211.5 14.2 %collective-permute-start = (bf16[128,16,128]{2,0,1:T(8,128)(2,1)S(1)}, bf16[128,16,128]{2,0,1:T(8,128)(2,1)S(1)}, u32[]{:S(2)}, u32[]{:S(2)}) collective-permute-start(bf16[128,16,128]{2,0,1:T(8,128)(2,1)S(1)} %fusion.54), channel_id=1, source_target_pairs={{16,0},{32,16},{48,32},{64,48},{80,64},{96,80},{112,96},{128,112},... | collective-permute-start | bytes 1572872 | tf_op jit(solution)/shard_map/ppermute | solution.py:10
  221.2 5.3 %copy-start.7 = (f32[1,128,2]{1,2,0:T(2,128)S(1)}, f32[1,128,2]{1,2,0:T(2,128)}, u32[]{:S(2)}) copy-start(f32[1,128,2]{1,2,0:T(2,128)} %param.16) | copy-start | bytes 3076
  225.7 0.8 copy-start.2
  229.3 51.3 %all-to-all-start.3 = ((bf16[16,28,16,128]{3,2,1,0:T(8,128)(2,1)}), bf16[16,28,16,128]{3,2,1,0:T(8,128)(2,1)}, u32[]{:S(2)}, u32[]{:S(2)}) async-start(bf16[16,28,16,128]{3,2,1,0:T(8,128)(2,1)} %copy.80), calls=%async_computation.3 | async-start | bytes 3670016 | tf_op jit(solution)/shard_map/all_to_all | solution.py:79
  280.6 4.4 %copy-start.10 = (bf16[1,1,2048,768]{3,2,1,0:T(8,128)(2,1)S(1)}, bf16[1,1,2048,768]{3,2,1,0:T(8,128)(2,1)}, u32[]{:S(2)}) copy-start(bf16[1,1,2048,768]{3,2,1,0:T(8,128)(2,1)} %param.17) | copy-start | bytes 9437188
  280.6 4.4 %copy-start.11 = (f32[16,28,768]{2,1,0:T(8,128)S(1)}, f32[16,28,768]{2,1,0:T(8,128)}, u32[]{:S(2)}) copy-start(f32[16,28,768]{2,1,0:T(8,128)} %fusion.36) | copy-start | bytes 4128772
  280.6 4.5 %copy-start.12 = (f32[16,28,768]{2,1,0:T(8,128)S(1)}, f32[16,28,768]{2,1,0:T(8,128)}, u32[]{:S(2)}) copy-start(f32[16,28,768]{2,1,0:T(8,128)} %fusion.39) | copy-start | bytes 4128772
  291.5 47.5 %all-to-all-start.4 = ((bf16[16,28,16,128]{3,2,1,0:T(8,128)(2,1)}), bf16[16,28,16,128]{3,2,1,0:T(8,128)(2,1)}, u32[]{:S(2)}, u32[]{:S(2)}) async-start(bf16[16,28,16,128]{3,2,1,0:T(8,128)(2,1)} %copy.83), calls=%async_computation.4 | async-start | bytes 3670016 | tf_op jit(solution)/shard_map/all_to_all | solution.py:79

commit v6 on v5

--- a/solution.py
+++ b/solution.py
@@ -2,6 +2,7 @@
 import jax.numpy as jnp
 from jax import lax
 from jax.sharding import PartitionSpec as P
+from jax.experimental.layout import Layout, with_layout_constraint
 
 
 def shifted(block, axis, distance):
@@ -51,7 +52,7 @@
     packed = lax.dot_general(
         table, tokens, (((0,), (0,)), ((), ())), preferred_element_type=jnp.float32
     )
-    return packed.astype(jnp.bfloat16)
+    return with_layout_constraint(packed.astype(jnp.bfloat16), Layout((0, 1, 2, 3)))
 
 
 def project(rows, mat):

time: 349 us -> 345 us (0.989)
    optimization_barrier x6 -> x5, local copies, waits for them, and re-layouts: 16.8 us -> 13 us  [beside(): send, filler_input = lax.optimization_barrier((send, filler_input))]
where the time goes in v6:
time: 345 us; the launch traced here: 344 us
  waiting for transfers between devices  215 us (62%)
  matrix products  51.5 us (15%)
  starting transfers between devices  36.7 us (11%)
  local copies, waits for them, and re-layouts  33.4 us (10%)
  other arithmetic  6.31 us (2%)
    all_to_all x5, waiting for transfers between devices, exchange(): lax.all_to_all(block, 'expert', split_axis=0, concat_axis=0, tiled=True)  215 us
    all_to_all x5, starting transfers between devices, exchange(): lax.all_to_all(block, 'expert', split_axis=0, concat_axis=0, tiled=True)  31.4 us
    dot_general x3, matrix products, project(): lax.dot_general(rows, mat, (((2, 3), (0, 1)), ((), ())), preferred_elemen...  14.6 us
    optimization_barrier x5, local copies, waits for them, and re-layouts, beside(): send, filler_input = lax.optimization_barrier((send, filler_input))  13 us
    unnamed x31, local copies, waits for them, and re-layouts  11.8 us
    dot_general x2, matrix products, backprop(): lax.dot_general(d_gate, gate_mat, contract, preferred_element_type=jnp.fl...  11.5 us
    dot_general x2, matrix products, backprop(): lax.dot_general(scaled, down_mat, (((2, 3), (1, 2)), ((), ())), preferred...  8.91 us
    dot_general x2, matrix products, backprop(): lax.dot_general(d_up, up_mat, contract, preferred_element_type=jnp.float32)  7.76 us
  transfers between devices with their start and end apart: 6, of which 5 were waited for; matrix products, arithmetic and copies ran while one was open for 13% of the time, Pallas kernels for 0%

profile of v6, /device:TPU:64, one launch (start us, length us, event | category | flops | bytes accessed | tf_op | source)
XLA Modules:
  0.0 344.2 jit_solution(3968338138449782622)
XLA Ops:
  5.2 2.0 copy.70
  9.2 2.0 copy.72
  14.3 3.3 copy.73
  17.6 8.2 %all-to-all-start = ((bf16[16,28,32,128]{3,2,1,0:T(8,128)(2,1)}), bf16[16,28,32,128]{3,2,1,0:T(8,128)(2,1)}, u32[]{:S(2)}, u32[]{:S(2)}) async-start(bf16[16,28,32,128]{3,2,1,0:T(8,128)(2,1)} %copy.73), calls=%async_computation | async-start | bytes 7340032 | tf_op jit(solution)/shard_map/all_to_all | solution.py:80
  28.1 2.0 copy.168
  30.4 2.8 copy.116
  34.0 73.9 %all-to-all-done = bf16[16,28,32,128]{3,2,1,0:T(8,128)(2,1)} async-done(((bf16[16,28,32,128]{3,2,1,0:T(8,128)(2,1)}), bf16[16,28,32,128]{3,2,1,0:T(8,128)(2,1)}, u32[]{:S(2)}, u32[]{:S(2)}) %all-to-all-start) | async-done | bytes 3670048 | tf_op jit(solution)/shard_map/all_to_all | solution.py:80
  107.9 5.2 %all-to-all-start.1 = ((bf16[16,28,16,128]{3,2,1,0:T(8,128)(2,1)}), bf16[16,28,16,128]{3,2,1,0:T(8,128)(2,1)}, u32[]{:S(2)}, u32[]{:S(2)}) async-start(bf16[16,28,16,128]{3,2,1,0:T(8,128)(2,1)} %copy.168), calls=%async_computation.1 | async-start | bytes 3670016 | tf_op jit(solution)/shard_map/all_to_all | solution.py:80
  113.1 5.6 %fusion.2 = f32[16,28,768,1]{2,1,3,0:T(8,128)} fusion(bf16[16,128,768,1]{2,1,0,3:T(8,128)(2,1)} %bitcast.209, bf16[16,28,32,128]{3,2,1,0:T(8,128)(2,1)} %all-to-all-done), kind=kOutput, calls=%fused_computation.6 | convolution fusion | flops 1409286144 | bytes 8192000 | tf_op jit(solution)/shard_map/dot_general | solution.py:59
  118.6 4.5 %fusion.4 = f32[16,28,768,1]{2,1,3,0:T(8,128)} fusion(bf16[16,28,32,128]{3,2,1,0:T(8,128)(2,1)} %all-to-all-done, bf16[768,16,128]{2,1,0:T(8,128)(2,1)S(1)} %bitcast.195), kind=kOutput, calls=%fused_computation.8 | convolution fusion | flops 1409286144 | bytes 8192000 | tf_op jit(solution)/shard_map/dot_general | solution.py:65
  123.1 9.3 %fusion.64 = f32[16,28,16,128]{3,1,2,0:T(8,128)} fusion(bf16[16,128,768,1]{2,1,0,3:T(8,128)(2,1)} %bitcast.210, f32[16,28,768,1]{2,1,3,0:T(8,128)} %fusion.2, bf16[16,128,768,1]{2,1,0,3:T(8,128)(2,1)S(1)} %bitcast.189, bf16[16,28,32,128]{3,2,1,0:T(8,128)(2,1)} %all-to-all-done, f32[16,28,768,1]{2,1,3,0:T(8,128)} %fusion.4), kind=kOutput, calls=%fused_computation.58 | convolution fusion | flops 2822012928 | bytes 16384000 | tf_op jit(solution)/shard_map/dot_general | solution.py:74
  132.4 5.6 %add_convert_fusion.1 = bf16[16,28,16,128]{3,1,2,0:T(8,128)(2,1)} fusion(f32[16,28,16,128]{3,1,2,0:T(8,128)} %fusion.64, bf16[16,128,768,1]{2,1,0,3:T(8,128)(2,1)S(1)} %bitcast.190, f32[16,28,768,1]{2,1,3,0:T(8,128)} %fusion.2, f32[16,28,768,1]{2,1,3,0:T(8,128)} %fusion.4), kind=kOutput, calls=%fused_computation.3 | convolution fusion | flops 1413185536 | bytes 11403264 | tf_op jit(solution)/shard_map/dot_general | solution.py:75
  138.0 17.0 %all-to-all-done.1 = bf16[16,28,16,128]{3,2,1,0:T(8,128)(2,1)} async-done(((bf16[16,28,16,128]{3,2,1,0:T(8,128)(2,1)}), bf16[16,28,16,128]{3,2,1,0:T(8,128)(2,1)}, u32[]{:S(2)}, u32[]{:S(2)}) %all-to-all-start.1) | async-done | bytes 1835040 | tf_op jit(solution)/shard_map/all_to_all | solution.py:80
  155.0 3.6 %copy.82 = bf16[16,28,16,128]{3,2,1,0:T(8,128)(2,1)} copy(bf16[16,28,16,128]{3,1,2,0:T(8,128)(2,1)} %add_convert_fusion.1) | data formatting | bytes 3670016 | tf_op jit(solution)/shard_map/optimization_barrier | solution.py:84
  158.7 5.1 %all-to-all-start.2 = ((bf16[16,28,16,128]{3,2,1,0:T(8,128)(2,1)}), bf16[16,28,16,128]{3,2,1,0:T(8,128)(2,1)}, u32[]{:S(2)}, u32[]{:S(2)}) async-start(bf16[16,28,16,128]{3,2,1,0:T(8,128)(2,1)} %copy.82), calls=%async_computation.2 | async-start | bytes 3670016 | tf_op jit(solution)/shard_map/all_to_all | solution.py:80
  164.8 40.9 %all-to-all-done.2 = bf16[16,28,16,128]{3,2,1,0:T(8,128)(2,1)} async-done(((bf16[16,28,16,128]{3,2,1,0:T(8,128)(2,1)}), bf16[16,28,16,128]{3,2,1,0:T(8,128)(2,1)}, u32[]{:S(2)}, u32[]{:S(2)}) %all-to-all-start.2) | async-done | bytes 1835040 | tf_op jit(solution)/shard_map/all_to_all | solution.py:80
  205.7 2.1 fusion.54
  207.8 5.2 %collective-permute-start = (bf16[128,16,128]{2,0,1:T(8,128)(2,1)S(1)}, bf16[128,16,128]{2,0,1:T(8,128)(2,1)S(1)}, u32[]{:S(2)}, u32[]{:S(2)}) collective-permute-start(bf16[128,16,128]{2,0,1:T(8,128)(2,1)S(1)} %fusion.54), channel_id=1, source_target_pairs={{16,0},{32,16},{48,32},{64,48},{80,64},{96,80},{112,96},{128,112},... | collective-permute-start | bytes 1572872 | tf_op jit(solution)/shard_map/ppermute | solution.py:11
  213.0 4.5 %fusion.39 = f32[16,28,768]{2,1,0:T(8,128)} fusion(bf16[16,128,768,1]{2,1,0,3:T(8,128)(2,1)S(1)} %bitcast.191, bf16[16,28,16,128]{3,2,1,0:T(8,128)(2,1)} %all-to-all-done.1), kind=kOutput, calls=%fused_computation.50 | convolution fusion | flops 1409286144 | bytes 6356992 | tf_op jit(solution)/shard_map/dot_general | solution.py:59
  217.5 4.5 %fusion.36 = f32[16,28,768]{2,1,0:T(8,128)} fusion(bf16[16,128,768,1]{2,1,0,3:T(8,128)(2,1)S(1)} %bitcast.211, bf16[16,28,16,128]{3,2,1,0:T(8,128)(2,1)} %all-to-all-done.1), kind=kOutput, calls=%fused_computation.49 | convolution fusion | flops 1409286144 | bytes 6356992 | tf_op jit(solution)/shard_map/dot_general | solution.py:59
  225.6 7.8 %all-to-all-start.3 = ((bf16[16,28,16,128]{3,2,1,0:T(8,128)(2,1)}), bf16[16,28,16,128]{3,2,1,0:T(8,128)(2,1)}, u32[]{:S(2)}, u32[]{:S(2)}) async-start(bf16[16,28,16,128]{3,2,1,0:T(8,128)(2,1)} %copy.86), calls=%async_computation.3 | async-start | bytes 3670016 | tf_op jit(solution)/shard_map/all_to_all | solution.py:80
  233.5 43.4 %all-to-all-done.3 = bf16[16,28,16,128]{3,2,1,0:T(8,128)(2,1)} async-done(((bf16[16,28,16,128]{3,2,1,0:T(8,128)(2,1)}), bf16[16,28,16,128]{3,2,1,0:T(8,128)(2,1)}, u32[]{:S(2)}, u32[]{:S(2)}) %all-to-all-start.3) | async-done | bytes 1835040 | tf_op jit(solution)/shard_map/all_to_all | solution.py:80
  276.9 4.4 %fusion.6 = f32[16,28,768,1]{2,1,3,0:T(8,128)S(1)} fusion(bf16[768,16,128]{2,1,0:T(8,128)(2,1)} %bitcast.194, bf16[16,28,16,128]{3,2,1,0:T(8,128)(2,1)} %all-to-all-done.3), kind=kOutput, calls=%fused_computation.11 | convolution fusion | flops 1409286144 | bytes 6356992 | tf_op jit(solution)/shard_map/dot_general | solution.py:65
  281.4 2.2 fusion.71
  283.6 2.2 add_convert_fusion
  287.7 5.2 %all-to-all-start.4 = ((bf16[16,28,16,128]{3,2,1,0:T(8,128)(2,1)}), bf16[16,28,16,128]{3,2,1,0:T(8,128)(2,1)}, u32[]{:S(2)}, u32[]{:S(2)}) async-start(bf16[16,28,16,128]{3,2,1,0:T(8,128)(2,1)} %copy.89), calls=%async_computation.4 | async-start | bytes 3670016 | tf_op jit(solution)/shard_map/all_to_all | solution.py:80
  292.9 2.1 copy.90
  295.0 40.2 %all-to-all-done.4 = bf16[16,28,16,128]{3,2,1,0:T(8,128)(2,1)} async-done(((bf16[16,28,16,128]{3,2,1,0:T(8,128)(2,1)}), bf16[16,28,16,128]{3,2,1,0:T(8,128)(2,1)}, u32[]{:S(2)}, u32[]{:S(2)}) %all-to-all-start.4) | async-done | bytes 1835040 | tf_op jit(solution)/shard_map/all_to_all | solution.py:80
  335.2 2.0 copy.94
  337.2 2.9 fusion.57
  340.1 2.0 copy.93
  342.2 2.0 copy.95
  (57 shorter events, 19.6 us)
Async XLA Ops:
  0.6 122.5 %copy-start = (bf16[1,1,2048,768]{3,2,1,0:T(8,128)(2,1)S(1)}, bf16[1,1,2048,768]{3,2,1,0:T(8,128)(2,1)}, u32[]{:S(2)}) copy-start(bf16[1,1,2048,768]{3,2,1,0:T(8,128)(2,1)} %param.18) | copy-start | bytes 9437188
  7.2 5.2 %copy-start.8 = (f32[1,128,2]{1,2,0:T(2,128)S(1)}, f32[1,128,2]{1,2,0:T(2,128)}, u32[]{:S(2)}) copy-start(f32[1,128,2]{1,2,0:T(2,128)} %param.15) | copy-start | bytes 3076
  11.2 1.5 copy-start.5
  17.6 8.2 %copy-start.6 = (s32[1,128,2]{1,2,0:T(2,128)S(1)}, s32[1,128,2]{1,2,0:T(2,128)}, u32[]{:S(2)}) copy-start(s32[1,128,2]{1,2,0:T(2,128)} %param.14) | copy-start | bytes 3076
  17.6 90.3 %all-to-all-start = ((bf16[16,28,32,128]{3,2,1,0:T(8,128)(2,1)}), bf16[16,28,32,128]{3,2,1,0:T(8,128)(2,1)}, u32[]{:S(2)}, u32[]{:S(2)}) async-start(bf16[16,28,32,128]{3,2,1,0:T(8,128)(2,1)} %copy.73), calls=%async_computation | async-start | bytes 7340032 | tf_op jit(solution)/shard_map/all_to_all | solution.py:80
  28.1 2.3 copy-start.1
  107.9 47.1 %all-to-all-start.1 = ((bf16[16,28,16,128]{3,2,1,0:T(8,128)(2,1)}), bf16[16,28,16,128]{3,2,1,0:T(8,128)(2,1)}, u32[]{:S(2)}, u32[]{:S(2)}) async-start(bf16[16,28,16,128]{3,2,1,0:T(8,128)(2,1)} %copy.168), calls=%async_computation.1 | async-start | bytes 3670016 | tf_op jit(solution)/shard_map/all_to_all | solution.py:80
  113.1 5.6 %copy-start.2 = (bf16[96,8,16,128]{3,2,1,0:T(8,128)(2,1)S(1)}, bf16[96,8,16,128]{3,2,1,0:T(8,128)(2,1)}, u32[]{:S(2)}) copy-start(bf16[96,8,16,128]{3,2,1,0:T(8,128)(2,1)} %copy.116) | copy-start | bytes 9437188
  158.7 47.0 %all-to-all-start.2 = ((bf16[16,28,16,128]{3,2,1,0:T(8,128)(2,1)}), bf16[16,28,16,128]{3,2,1,0:T(8,128)(2,1)}, u32[]{:S(2)}, u32[]{:S(2)}) async-start(bf16[16,28,16,128]{3,2,1,0:T(8,128)(2,1)} %copy.82), calls=%async_computation.2 | async-start | bytes 3670016 | tf_op jit(solution)/shard_map/all_to_all | solution.py:80
  207.7 9.7 %copy-start.4 = (bf16[128,16,128]{2,0,1:T(8,128)(2,1)}, bf16[128,16,128]{2,0,1:T(8,128)(2,1)S(1)}, u32[]{:S(2)}) copy-start(bf16[128,16,128]{2,0,1:T(8,128)(2,1)S(1)} %fusion.54) | copy-start | bytes 1572868
  207.8 9.7 %copy-start.9 = (bf16[1,1,2048,768]{3,2,1,0:T(8,128)(2,1)S(1)}, bf16[1,1,2048,768]{3,2,1,0:T(8,128)(2,1)}, u32[]{:S(2)}) copy-start(bf16[1,1,2048,768]{3,2,1,0:T(8,128)(2,1)} %param.17) | copy-start | bytes 9437188
  207.8 14.2 %collective-permute-start = (bf16[128,16,128]{2,0,1:T(8,128)(2,1)S(1)}, bf16[128,16,128]{2,0,1:T(8,128)(2,1)S(1)}, u32[]{:S(2)}, u32[]{:S(2)}) collective-permute-start(bf16[128,16,128]{2,0,1:T(8,128)(2,1)S(1)} %fusion.54), channel_id=1, source_target_pairs={{16,0},{32,16},{48,32},{64,48},{80,64},{96,80},{112,96},{128,112},... | collective-permute-start | bytes 1572872 | tf_op jit(solution)/shard_map/ppermute | solution.py:11
  217.5 5.3 %copy-start.7 = (f32[1,128,2]{1,2,0:T(2,128)S(1)}, f32[1,128,2]{1,2,0:T(2,128)}, u32[]{:S(2)}) copy-start(f32[1,128,2]{1,2,0:T(2,128)} %param.16) | copy-start | bytes 3076
  222.0 0.8 copy-start.3
  225.6 51.3 %all-to-all-start.3 = ((bf16[16,28,16,128]{3,2,1,0:T(8,128)(2,1)}), bf16[16,28,16,128]{3,2,1,0:T(8,128)(2,1)}, u32[]{:S(2)}, u32[]{:S(2)}) async-start(bf16[16,28,16,128]{3,2,1,0:T(8,128)(2,1)} %copy.86), calls=%async_computation.3 | async-start | bytes 3670016 | tf_op jit(solution)/shard_map/all_to_all | solution.py:80
  276.9 4.4 %copy-start.10 = (bf16[1,1,2048,768]{3,2,1,0:T(8,128)(2,1)S(1)}, bf16[1,1,2048,768]{3,2,1,0:T(8,128)(2,1)}, u32[]{:S(2)}) copy-start(bf16[1,1,2048,768]{3,2,1,0:T(8,128)(2,1)} %param.17) | copy-start | bytes 9437188
  276.9 4.4 %copy-start.11 = (f32[16,28,768]{2,1,0:T(8,128)S(1)}, f32[16,28,768]{2,1,0:T(8,128)}, u32[]{:S(2)}) copy-start(f32[16,28,768]{2,1,0:T(8,128)} %fusion.36) | copy-start | bytes 4128772
  276.9 4.4 %copy-start.12 = (f32[16,28,768]{2,1,0:T(8,128)S(1)}, f32[16,28,768]{2,1,0:T(8,128)}, u32[]{:S(2)}) copy-start(f32[16,28,768]{2,1,0:T(8,128)} %fusion.39) | copy-start | bytes 4128772
  287.7 47.5 %all-to-all-start.4 = ((bf16[16,28,16,128]{3,2,1,0:T(8,128)(2,1)}), bf16[16,28,16,128]{3,2,1,0:T(8,128)(2,1)}, u32[]{:S(2)}, u32[]{:S(2)}) async-start(bf16[16,28,16,128]{3,2,1,0:T(8,128)(2,1)} %copy.89), calls=%async_computation.4 | async-start | bytes 3670016 | tf_op jit(solution)/shard_map/all_to_all | solution.py:80

commit v7 on v6

--- a/solution.py
+++ b/solution.py
@@ -153,10 +153,12 @@
         second_gate_pre, second_up_pre, second_scaled, gate_mat, up_mat, down_mat
     )
     second_returned, grad_a = beside(
-        second_back, grad_a, lambda rows: rows.reshape(tok_count, width)
+        second_back,
+        grad_a,
+        lambda rows: with_layout_constraint(rows.reshape(1, tok_count, width), Layout((0, 1, 2))),
     )
-    grad_b = combine(second_cot, second_table, second_returned).reshape(tok_count, width)
-    return (grad_a[None], grad_b[None])
+    grad_b = combine(second_cot, second_table, second_returned).reshape(1, tok_count, width)
+    return (grad_a, with_layout_constraint(grad_b, Layout((0, 1, 2))))
 
 
 def solution(mesh):

time: 345 us -> 342 us (level)
    reshape x0 -> x2, local copies, waits for them, and re-layouts: none -> 4.11 us  [the longest x1 2.06 us: on_device(): rows.reshape(1, tok_count, width)]
    unnamed x31 -> x29, local copies, waits for them, and re-layouts: 11.8 us -> 7.76 us
  transfers between devices with their start and end apart: 6 -> 6, of which waited for: 5 -> 5; matrix products, arithmetic and copies ran while one was open for 13% -> 14% of each run, Pallas kernels for 0% -> 0%
where the time goes in v7:
time: 342 us; the launch traced here: 340 us
  waiting for transfers between devices  213 us (62%)
  matrix products  50.7 us (15%)
  starting transfers between devices  36.7 us (11%)
  local copies, waits for them, and re-layouts  32.7 us (10%)
  other arithmetic  6.31 us (2%)
    all_to_all x5, waiting for transfers between devices, exchange(): lax.all_to_all(block, 'expert', split_axis=0, concat_axis=0, tiled=True)  213 us
    all_to_all x5, starting transfers between devices, exchange(): lax.all_to_all(block, 'expert', split_axis=0, concat_axis=0, tiled=True)  31.4 us
    dot_general x3, matrix products, project(): lax.dot_general(rows, mat, (((2, 3), (0, 1)), ((), ())), preferred_elemen...  14.6 us
    optimization_barrier x5, local copies, waits for them, and re-layouts, beside(): send, filler_input = lax.optimization_barrier((send, filler_input))  13.1 us
    dot_general x2, matrix products, backprop(): lax.dot_general(d_gate, gate_mat, contract, preferred_element_type=jnp.fl...  11.5 us
    dot_general x2, matrix products, backprop(): lax.dot_general(scaled, down_mat, (((2, 3), (1, 2)), ((), ())), preferred...  8.91 us
    dot_general x2, matrix products, backprop(): lax.dot_general(d_up, up_mat, contract, preferred_element_type=jnp.float32)  7.76 us
    unnamed x29, local copies, waits for them, and re-layouts  7.76 us
  transfers between devices with their start and end apart: 6, of which 5 were waited for; matrix products, arithmetic and copies ran while one was open for 14% of the time, Pallas kernels for 0%

profile of v7, /device:TPU:64, one launch (start us, length us, event | category | flops | bytes accessed | tf_op | source)
XLA Modules:
  0.0 340.5 jit_solution(9350964116117030659)
XLA Ops:
  5.2 2.0 copy.65
  9.2 2.0 copy.67
  14.3 3.3 copy.68
  17.6 8.2 %all-to-all-start = ((bf16[16,28,32,128]{3,2,1,0:T(8,128)(2,1)}), bf16[16,28,32,128]{3,2,1,0:T(8,128)(2,1)}, u32[]{:S(2)}, u32[]{:S(2)}) async-start(bf16[16,28,32,128]{3,2,1,0:T(8,128)(2,1)} %copy.68), calls=%async_computation | async-start | bytes 7340032 | tf_op jit(solution)/shard_map/all_to_all | solution.py:80
  28.1 2.0 copy.159
  30.4 2.8 copy.107
  34.0 73.9 %all-to-all-done = bf16[16,28,32,128]{3,2,1,0:T(8,128)(2,1)} async-done(((bf16[16,28,32,128]{3,2,1,0:T(8,128)(2,1)}), bf16[16,28,32,128]{3,2,1,0:T(8,128)(2,1)}, u32[]{:S(2)}, u32[]{:S(2)}) %all-to-all-start) | async-done | bytes 3670048 | tf_op jit(solution)/shard_map/all_to_all | solution.py:80
  107.9 5.2 %all-to-all-start.1 = ((bf16[16,28,16,128]{3,2,1,0:T(8,128)(2,1)}), bf16[16,28,16,128]{3,2,1,0:T(8,128)(2,1)}, u32[]{:S(2)}, u32[]{:S(2)}) async-start(bf16[16,28,16,128]{3,2,1,0:T(8,128)(2,1)} %copy.159), calls=%async_computation.1 | async-start | bytes 3670016 | tf_op jit(solution)/shard_map/all_to_all | solution.py:80
  113.1 5.6 %fusion.2 = f32[16,28,768,1]{2,1,3,0:T(8,128)} fusion(bf16[16,128,768,1]{2,1,0,3:T(8,128)(2,1)} %bitcast.205, bf16[16,28,32,128]{3,2,1,0:T(8,128)(2,1)} %all-to-all-done), kind=kOutput, calls=%fused_computation.6 | convolution fusion | flops 1409286144 | bytes 8192000 | tf_op jit(solution)/shard_map/dot_general | solution.py:59
  118.6 4.5 %fusion.4 = f32[16,28,768,1]{2,1,3,0:T(8,128)} fusion(bf16[16,28,32,128]{3,2,1,0:T(8,128)(2,1)} %all-to-all-done, bf16[768,16,128]{2,1,0:T(8,128)(2,1)S(1)} %bitcast.193), kind=kOutput, calls=%fused_computation.8 | convolution fusion | flops 1409286144 | bytes 8192000 | tf_op jit(solution)/shard_map/dot_general | solution.py:65
  123.1 9.3 %fusion.64 = f32[16,28,16,128]{3,1,2,0:T(8,128)} fusion(bf16[16,128,768,1]{2,1,0,3:T(8,128)(2,1)} %bitcast.206, f32[16,28,768,1]{2,1,3,0:T(8,128)} %fusion.2, bf16[16,128,768,1]{2,1,0,3:T(8,128)(2,1)S(1)} %bitcast.187, bf16[16,28,32,128]{3,2,1,0:T(8,128)(2,1)} %all-to-all-done, f32[16,28,768,1]{2,1,3,0:T(8,128)} %fusion.4), kind=kOutput, calls=%fused_computation.58 | convolution fusion | flops 2822012928 | bytes 16384000 | tf_op jit(solution)/shard_map/dot_general | solution.py:74
  132.4 5.6 %add_convert_fusion.1 = bf16[16,28,16,128]{3,1,2,0:T(8,128)(2,1)} fusion(f32[16,28,16,128]{3,1,2,0:T(8,128)} %fusion.64, bf16[16,128,768,1]{2,1,0,3:T(8,128)(2,1)S(1)} %bitcast.188, f32[16,28,768,1]{2,1,3,0:T(8,128)} %fusion.2, f32[16,28,768,1]{2,1,3,0:T(8,128)} %fusion.4), kind=kOutput, calls=%fused_computation.3 | convolution fusion | flops 1413185536 | bytes 11403264 | tf_op jit(solution)/shard_map/dot_general | solution.py:75
  138.0 17.0 %all-to-all-done.1 = bf16[16,28,16,128]{3,2,1,0:T(8,128)(2,1)} async-done(((bf16[16,28,16,128]{3,2,1,0:T(8,128)(2,1)}), bf16[16,28,16,128]{3,2,1,0:T(8,128)(2,1)}, u32[]{:S(2)}, u32[]{:S(2)}) %all-to-all-start.1) | async-done | bytes 1835040 | tf_op jit(solution)/shard_map/all_to_all | solution.py:80
  155.0 3.6 %copy.77 = bf16[16,28,16,128]{3,2,1,0:T(8,128)(2,1)} copy(bf16[16,28,16,128]{3,1,2,0:T(8,128)(2,1)} %add_convert_fusion.1) | data formatting | bytes 3670016 | tf_op jit(solution)/shard_map/optimization_barrier | solution.py:84
  158.7 5.1 %all-to-all-start.2 = ((bf16[16,28,16,128]{3,2,1,0:T(8,128)(2,1)}), bf16[16,28,16,128]{3,2,1,0:T(8,128)(2,1)}, u32[]{:S(2)}, u32[]{:S(2)}) async-start(bf16[16,28,16,128]{3,2,1,0:T(8,128)(2,1)} %copy.77), calls=%async_computation.2 | async-start | bytes 3670016 | tf_op jit(solution)/shard_map/all_to_all | solution.py:80
  164.8 40.9 %all-to-all-done.2 = bf16[16,28,16,128]{3,2,1,0:T(8,128)(2,1)} async-done(((bf16[16,28,16,128]{3,2,1,0:T(8,128)(2,1)}), bf16[16,28,16,128]{3,2,1,0:T(8,128)(2,1)}, u32[]{:S(2)}, u32[]{:S(2)}) %all-to-all-start.2) | async-done | bytes 1835040 | tf_op jit(solution)/shard_map/all_to_all | solution.py:80
  205.7 2.1 fusion.54
  207.8 5.2 %collective-permute-start = (bf16[128,16,128]{2,0,1:T(8,128)(2,1)S(1)}, bf16[128,16,128]{2,0,1:T(8,128)(2,1)S(1)}, u32[]{:S(2)}, u32[]{:S(2)}) collective-permute-start(bf16[128,16,128]{2,0,1:T(8,128)(2,1)S(1)} %fusion.54), channel_id=1, source_target_pairs={{16,0},{32,16},{48,32},{64,48},{80,64},{96,80},{112,96},{128,112},... | collective-permute-start | bytes 1572872 | tf_op jit(solution)/shard_map/ppermute | solution.py:11
  213.0 4.5 %fusion.39 = f32[16,28,768]{2,1,0:T(8,128)} fusion(bf16[16,128,768,1]{2,1,0,3:T(8,128)(2,1)S(1)} %bitcast.189, bf16[16,28,16,128]{3,2,1,0:T(8,128)(2,1)} %all-to-all-done.1), kind=kOutput, calls=%fused_computation.50 | convolution fusion | flops 1409286144 | bytes 6356992 | tf_op jit(solution)/shard_map/dot_general | solution.py:59
  217.5 4.5 %fusion.36 = f32[16,28,768]{2,1,0:T(8,128)} fusion(bf16[16,128,768,1]{2,1,0,3:T(8,128)(2,1)S(1)} %bitcast.207, bf16[16,28,16,128]{3,2,1,0:T(8,128)(2,1)} %all-to-all-done.1), kind=kOutput, calls=%fused_computation.49 | convolution fusion | flops 1409286144 | bytes 6356992 | tf_op jit(solution)/shard_map/dot_general | solution.py:59
  223.6 2.0 copy.81
  225.6 7.8 %all-to-all-start.3 = ((bf16[16,28,16,128]{3,2,1,0:T(8,128)(2,1)}), bf16[16,28,16,128]{3,2,1,0:T(8,128)(2,1)}, u32[]{:S(2)}, u32[]{:S(2)}) async-start(bf16[16,28,16,128]{3,2,1,0:T(8,128)(2,1)} %copy.81), calls=%async_computation.3 | async-start | bytes 3670016 | tf_op jit(solution)/shard_map/all_to_all | solution.py:80
  233.5 43.4 %all-to-all-done.3 = bf16[16,28,16,128]{3,2,1,0:T(8,128)(2,1)} async-done(((bf16[16,28,16,128]{3,2,1,0:T(8,128)(2,1)}), bf16[16,28,16,128]{3,2,1,0:T(8,128)(2,1)}, u32[]{:S(2)}, u32[]{:S(2)}) %all-to-all-start.3) | async-done | bytes 1835040 | tf_op jit(solution)/shard_map/all_to_all | solution.py:80
  276.9 4.4 %fusion.6 = f32[16,28,768,1]{2,1,3,0:T(8,128)S(1)} fusion(bf16[768,16,128]{2,1,0:T(8,128)(2,1)} %bitcast.192, bf16[16,28,16,128]{3,2,1,0:T(8,128)(2,1)} %all-to-all-done.3), kind=kOutput, calls=%fused_computation.11 | convolution fusion | flops 1409286144 | bytes 6356992 | tf_op jit(solution)/shard_map/dot_general | solution.py:65
  281.4 2.2 fusion.71
  283.6 2.2 add_convert_fusion
  287.7 5.2 %all-to-all-start.4 = ((bf16[16,28,16,128]{3,2,1,0:T(8,128)(2,1)}), bf16[16,28,16,128]{3,2,1,0:T(8,128)(2,1)}, u32[]{:S(2)}, u32[]{:S(2)}) async-start(bf16[16,28,16,128]{3,2,1,0:T(8,128)(2,1)} %copy.84), calls=%async_computation.4 | async-start | bytes 3670016 | tf_op jit(solution)/shard_map/all_to_all | solution.py:80
  292.9 2.2 copy.85
  295.1 2.1 reshape.59
  297.2 38.0 %all-to-all-done.4 = bf16[16,28,16,128]{3,2,1,0:T(8,128)(2,1)} async-done(((bf16[16,28,16,128]{3,2,1,0:T(8,128)(2,1)}), bf16[16,28,16,128]{3,2,1,0:T(8,128)(2,1)}, u32[]{:S(2)}, u32[]{:S(2)}) %all-to-all-start.4) | async-done | bytes 1835040 | tf_op jit(solution)/shard_map/all_to_all | solution.py:80
  335.2 2.1 fusion.57
  338.4 2.1 reshape.60
  (57 shorter events, 18.7 us)
Async XLA Ops:
  0.6 122.5 %copy-start = (bf16[1,1,2048,768]{3,2,1,0:T(8,128)(2,1)S(1)}, bf16[1,1,2048,768]{3,2,1,0:T(8,128)(2,1)}, u32[]{:S(2)}) copy-start(bf16[1,1,2048,768]{3,2,1,0:T(8,128)(2,1)} %param.18) | copy-start | bytes 9437188
  7.2 5.2 %copy-start.8 = (f32[1,128,2]{1,2,0:T(2,128)S(1)}, f32[1,128,2]{1,2,0:T(2,128)}, u32[]{:S(2)}) copy-start(f32[1,128,2]{1,2,0:T(2,128)} %param.15) | copy-start | bytes 3076
  11.2 1.5 copy-start.5
  17.6 8.2 %copy-start.6 = (s32[1,128,2]{1,2,0:T(2,128)S(1)}, s32[1,128,2]{1,2,0:T(2,128)}, u32[]{:S(2)}) copy-start(s32[1,128,2]{1,2,0:T(2,128)} %param.14) | copy-start | bytes 3076
  17.6 90.3 %all-to-all-start = ((bf16[16,28,32,128]{3,2,1,0:T(8,128)(2,1)}), bf16[16,28,32,128]{3,2,1,0:T(8,128)(2,1)}, u32[]{:S(2)}, u32[]{:S(2)}) async-start(bf16[16,28,32,128]{3,2,1,0:T(8,128)(2,1)} %copy.68), calls=%async_computation | async-start | bytes 7340032 | tf_op jit(solution)/shard_map/all_to_all | solution.py:80
  28.1 2.3 copy-start.1
  107.9 47.1 %all-to-all-start.1 = ((bf16[16,28,16,128]{3,2,1,0:T(8,128)(2,1)}), bf16[16,28,16,128]{3,2,1,0:T(8,128)(2,1)}, u32[]{:S(2)}, u32[]{:S(2)}) async-start(bf16[16,28,16,128]{3,2,1,0:T(8,128)(2,1)} %copy.159), calls=%async_computation.1 | async-start | bytes 3670016 | tf_op jit(solution)/shard_map/all_to_all | solution.py:80
  113.1 5.6 %copy-start.2 = (bf16[96,8,16,128]{3,2,1,0:T(8,128)(2,1)S(1)}, bf16[96,8,16,128]{3,2,1,0:T(8,128)(2,1)}, u32[]{:S(2)}) copy-start(bf16[96,8,16,128]{3,2,1,0:T(8,128)(2,1)} %copy.107) | copy-start | bytes 9437188
  158.7 47.0 %all-to-all-start.2 = ((bf16[16,28,16,128]{3,2,1,0:T(8,128)(2,1)}), bf16[16,28,16,128]{3,2,1,0:T(8,128)(2,1)}, u32[]{:S(2)}, u32[]{:S(2)}) async-start(bf16[16,28,16,128]{3,2,1,0:T(8,128)(2,1)} %copy.77), calls=%async_computation.2 | async-start | bytes 3670016 | tf_op jit(solution)/shard_map/all_to_all | solution.py:80
  207.7 9.7 %copy-start.4 = (bf16[128,16,128]{2,0,1:T(8,128)(2,1)}, bf16[128,16,128]{2,0,1:T(8,128)(2,1)S(1)}, u32[]{:S(2)}) copy-start(bf16[128,16,128]{2,0,1:T(8,128)(2,1)S(1)} %fusion.54) | copy-start | bytes 1572868
  207.8 9.7 %copy-start.9 = (bf16[1,1,2048,768]{3,2,1,0:T(8,128)(2,1)S(1)}, bf16[1,1,2048,768]{3,2,1,0:T(8,128)(2,1)}, u32[]{:S(2)}) copy-start(bf16[1,1,2048,768]{3,2,1,0:T(8,128)(2,1)} %param.17) | copy-start | bytes 9437188
  207.8 14.2 %collective-permute-start = (bf16[128,16,128]{2,0,1:T(8,128)(2,1)S(1)}, bf16[128,16,128]{2,0,1:T(8,128)(2,1)S(1)}, u32[]{:S(2)}, u32[]{:S(2)}) collective-permute-start(bf16[128,16,128]{2,0,1:T(8,128)(2,1)S(1)} %fusion.54), channel_id=1, source_target_pairs={{16,0},{32,16},{48,32},{64,48},{80,64},{96,80},{112,96},{128,112},... | collective-permute-start | bytes 1572872 | tf_op jit(solution)/shard_map/ppermute | solution.py:11
  217.5 5.3 %copy-start.7 = (f32[1,128,2]{1,2,0:T(2,128)S(1)}, f32[1,128,2]{1,2,0:T(2,128)}, u32[]{:S(2)}) copy-start(f32[1,128,2]{1,2,0:T(2,128)} %param.16) | copy-start | bytes 3076
  222.0 0.8 copy-start.3
  225.6 51.3 %all-to-all-start.3 = ((bf16[16,28,16,128]{3,2,1,0:T(8,128)(2,1)}), bf16[16,28,16,128]{3,2,1,0:T(8,128)(2,1)}, u32[]{:S(2)}, u32[]{:S(2)}) async-start(bf16[16,28,16,128]{3,2,1,0:T(8,128)(2,1)} %copy.81), calls=%async_computation.3 | async-start | bytes 3670016 | tf_op jit(solution)/shard_map/all_to_all | solution.py:80
  276.9 4.4 %copy-start.10 = (bf16[1,1,2048,768]{3,2,1,0:T(8,128)(2,1)S(1)}, bf16[1,1,2048,768]{3,2,1,0:T(8,128)(2,1)}, u32[]{:S(2)}) copy-start(bf16[1,1,2048,768]{3,2,1,0:T(8,128)(2,1)} %param.17) | copy-start | bytes 9437188
  276.9 4.4 %copy-start.11 = (f32[16,28,768]{2,1,0:T(8,128)S(1)}, f32[16,28,768]{2,1,0:T(8,128)}, u32[]{:S(2)}) copy-start(f32[16,28,768]{2,1,0:T(8,128)} %fusion.36) | copy-start | bytes 4128772
  276.9 4.4 %copy-start.12 = (f32[16,28,768]{2,1,0:T(8,128)S(1)}, f32[16,28,768]{2,1,0:T(8,128)}, u32[]{:S(2)}) copy-start(f32[16,28,768]{2,1,0:T(8,128)} %fusion.39) | copy-start | bytes 4128772
  287.7 47.5 %all-to-all-start.4 = ((bf16[16,28,16,128]{3,2,1,0:T(8,128)(2,1)}), bf16[16,28,16,128]{3,2,1,0:T(8,128)(2,1)}, u32[]{:S(2)}, u32[]{:S(2)}) async-start(bf16[16,28,16,128]{3,2,1,0:T(8,128)(2,1)} %copy.84), calls=%async_computation.4 | async-start | bytes 3670016 | tf_op jit(solution)/shard_map/all_to_all | solution.py:80

commit v8 on v7

--- a/solution.py
+++ b/solution.py
@@ -157,7 +157,9 @@
         grad_a,
         lambda rows: with_layout_constraint(rows.reshape(1, tok_count, width), Layout((0, 1, 2))),
     )
-    grad_b = combine(second_cot, second_table, second_returned).reshape(1, tok_count, width)
+    grad_b = with_layout_constraint(
+        combine(second_cot, second_table, second_returned), Layout((0, 1, 2))
+    ).reshape(1, tok_count, width)
     return (grad_a, with_layout_constraint(grad_b, Layout((0, 1, 2))))
 
 

time: 342 us -> 336 us (0.982)
  local copies, waits for them, and re-layouts: 32.7 us -> 24.6 us
    optimization_barrier x2 -> x1, local copies, waits for them, and re-layouts: 4.02 us -> 0.14 us  [on_device(): lax.optimization_barrier((split_rows(cotangent_a[0]), split_rows(tokens_a...]
    optimization_barrier x5 -> x4, local copies, waits for them, and re-layouts: 13.1 us -> 10.9 us  [beside(): send, filler_input = lax.optimization_barrier((send, filler_input))]
    unnamed x29 -> x33, local copies, waits for them, and re-layouts: 7.76 us -> 6.7 us
  transfers between devices with their start and end apart: 6 -> 6, of which waited for: 5 -> 5; matrix products, arithmetic and copies ran while one was open for 14% -> 13% of each run, Pallas kernels for 0% -> 0%
where the time goes in v8:
time: 336 us; the launch traced here: 335 us
  waiting for transfers between devices  215 us (64%)
  matrix products  50.6 us (15%)
  starting transfers between devices  36.7 us (11%)
  local copies, waits for them, and re-layouts  24.6 us (7%)
  other arithmetic  7.1 us (2%)
    all_to_all x5, waiting for transfers between devices, exchange(): lax.all_to_all(block, 'expert', split_axis=0, concat_axis=0, tiled=True)  215 us
    all_to_all x5, starting transfers between devices, exchange(): lax.all_to_all(block, 'expert', split_axis=0, concat_axis=0, tiled=True)  31.5 us
    dot_general x3, matrix products, project(): lax.dot_general(rows, mat, (((2, 3), (0, 1)), ((), ())), preferred_elemen...  14.5 us
    dot_general x2, matrix products, backprop(): lax.dot_general(d_gate, gate_mat, contract, preferred_element_type=jnp.fl...  11.5 us
    optimization_barrier x4, local copies, waits for them, and re-layouts, beside(): send, filler_input = lax.optimization_barrier((send, filler_input))  10.9 us
    dot_general x2, matrix products, backprop(): lax.dot_general(scaled, down_mat, (((2, 3), (1, 2)), ((), ())), preferred...  8.9 us
    dot_general x2, matrix products, backprop(): lax.dot_general(d_up, up_mat, contract, preferred_element_type=jnp.float32)  7.79 us
  transfers between devices with their start and end apart: 6, of which 5 were waited for; matrix products, arithmetic and copies ran while one was open for 13% of the time, Pallas kernels for 0%

profile of v8, /device:TPU:64, one launch (start us, length us, event | category | flops | bytes accessed | tf_op | source)
XLA Modules:
  0.0 335.4 jit_solution(5343670268347356212)
XLA Ops:
  8.3 3.3 copy.54
  11.7 8.2 %all-to-all-start = ((bf16[16,28,32,128]{3,2,1,0:T(8,128)(2,1)}), bf16[16,28,32,128]{3,2,1,0:T(8,128)(2,1)}, u32[]{:S(2)}, u32[]{:S(2)}) async-start(bf16[16,28,32,128]{3,2,1,0:T(8,128)(2,1)} %copy.54), calls=%async_computation | async-start | bytes 7340032 | tf_op jit(solution)/shard_map/all_to_all | solution.py:80
  20.4 1.7 fusion.68
  22.1 2.0 copy.145
  24.4 2.8 copy.95
  28.0 73.9 %all-to-all-done = bf16[16,28,32,128]{3,2,1,0:T(8,128)(2,1)} async-done(((bf16[16,28,32,128]{3,2,1,0:T(8,128)(2,1)}), bf16[16,28,32,128]{3,2,1,0:T(8,128)(2,1)}, u32[]{:S(2)}, u32[]{:S(2)}) %all-to-all-start) | async-done | bytes 3670048 | tf_op jit(solution)/shard_map/all_to_all | solution.py:80
  101.9 5.2 %all-to-all-start.1 = ((bf16[16,28,16,128]{3,2,1,0:T(8,128)(2,1)}), bf16[16,28,16,128]{3,2,1,0:T(8,128)(2,1)}, u32[]{:S(2)}, u32[]{:S(2)}) async-start(bf16[16,28,16,128]{3,2,1,0:T(8,128)(2,1)} %copy.145), calls=%async_computation.1 | async-start | bytes 3670016 | tf_op jit(solution)/shard_map/all_to_all | solution.py:80
  107.1 5.6 %fusion.2 = f32[16,28,768,1]{2,1,3,0:T(8,128)} fusion(bf16[16,128,768,1]{2,1,0,3:T(8,128)(2,1)} %bitcast.201, bf16[16,28,32,128]{3,2,1,0:T(8,128)(2,1)} %all-to-all-done), kind=kOutput, calls=%fused_computation.6 | convolution fusion | flops 1409286144 | bytes 8192000 | tf_op jit(solution)/shard_map/dot_general | solution.py:59
  112.6 4.5 %fusion.4 = f32[16,28,768,1]{2,1,3,0:T(8,128)} fusion(bf16[16,28,32,128]{3,2,1,0:T(8,128)(2,1)} %all-to-all-done, bf16[768,16,128]{2,1,0:T(8,128)(2,1)S(1)} %bitcast.189), kind=kOutput, calls=%fused_computation.8 | convolution fusion | flops 1409286144 | bytes 8192000 | tf_op jit(solution)/shard_map/dot_general | solution.py:65
  117.1 9.3 %fusion.52 = f32[16,28,16,128]{3,1,2,0:T(8,128)} fusion(bf16[16,128,768,1]{2,1,0,3:T(8,128)(2,1)} %bitcast.202, f32[16,28,768,1]{2,1,3,0:T(8,128)} %fusion.2, bf16[16,128,768,1]{2,1,0,3:T(8,128)(2,1)S(1)} %bitcast.181, bf16[16,28,32,128]{3,2,1,0:T(8,128)(2,1)} %all-to-all-done, f32[16,28,768,1]{2,1,3,0:T(8,128)} %fusion.4), kind=kOutput, calls=%fused_computation.54 | convolution fusion | flops 2822012928 | bytes 16384000 | tf_op jit(solution)/shard_map/dot_general | solution.py:74
  126.4 5.6 %add_convert_fusion.1 = bf16[16,28,16,128]{3,1,2,0:T(8,128)(2,1)} fusion(f32[16,28,16,128]{3,1,2,0:T(8,128)} %fusion.52, bf16[16,128,768,1]{2,1,0,3:T(8,128)(2,1)S(1)} %bitcast.182, f32[16,28,768,1]{2,1,3,0:T(8,128)} %fusion.2, f32[16,28,768,1]{2,1,3,0:T(8,128)} %fusion.4), kind=kOutput, calls=%fused_computation.3 | convolution fusion | flops 1413185536 | bytes 11403264 | tf_op jit(solution)/shard_map/dot_general | solution.py:75
  132.0 17.0 %all-to-all-done.1 = bf16[16,28,16,128]{3,2,1,0:T(8,128)(2,1)} async-done(((bf16[16,28,16,128]{3,2,1,0:T(8,128)(2,1)}), bf16[16,28,16,128]{3,2,1,0:T(8,128)(2,1)}, u32[]{:S(2)}, u32[]{:S(2)}) %all-to-all-start.1) | async-done | bytes 1835040 | tf_op jit(solution)/shard_map/all_to_all | solution.py:80
  149.0 3.6 %copy.63 = bf16[16,28,16,128]{3,2,1,0:T(8,128)(2,1)} copy(bf16[16,28,16,128]{3,1,2,0:T(8,128)(2,1)} %add_convert_fusion.1) | data formatting | bytes 3670016 | tf_op jit(solution)/shard_map/optimization_barrier | solution.py:84
  152.7 5.1 %all-to-all-start.2 = ((bf16[16,28,16,128]{3,2,1,0:T(8,128)(2,1)}), bf16[16,28,16,128]{3,2,1,0:T(8,128)(2,1)}, u32[]{:S(2)}, u32[]{:S(2)}) async-start(bf16[16,28,16,128]{3,2,1,0:T(8,128)(2,1)} %copy.63), calls=%async_computation.2 | async-start | bytes 3670016 | tf_op jit(solution)/shard_map/all_to_all | solution.py:80
  158.8 40.9 %all-to-all-done.2 = bf16[16,28,16,128]{3,2,1,0:T(8,128)(2,1)} async-done(((bf16[16,28,16,128]{3,2,1,0:T(8,128)(2,1)}), bf16[16,28,16,128]{3,2,1,0:T(8,128)(2,1)}, u32[]{:S(2)}, u32[]{:S(2)}) %all-to-all-start.2) | async-done | bytes 1835040 | tf_op jit(solution)/shard_map/all_to_all | solution.py:80
  199.7 2.0 fusion.42
  202.4 5.2 %collective-permute-start = (bf16[128,16,128]{2,1,0:T(8,128)(2,1)S(1)}, bf16[128,16,128]{2,1,0:T(8,128)(2,1)S(1)}, u32[]{:S(2)}, u32[]{:S(2)}) collective-permute-start(bf16[128,16,128]{2,1,0:T(8,128)(2,1)S(1)} %fusion.57), channel_id=1, source_target_pairs={{16,0},{32,16},{48,32},{64,48},{80,64},{96,80},{112,96},{128,112},... | collective-permute-start | bytes 1572872 | tf_op jit(solution)/shard_map/ppermute | solution.py:11
  207.7 4.5 %fusion.39 = f32[16,28,768]{2,1,0:T(8,128)} fusion(bf16[16,128,768,1]{2,1,0,3:T(8,128)(2,1)S(1)} %bitcast.183, bf16[16,28,16,128]{3,2,1,0:T(8,128)(2,1)} %all-to-all-done.1), kind=kOutput, calls=%fused_computation.50 | convolution fusion | flops 1409286144 | bytes 6356992 | tf_op jit(solution)/shard_map/dot_general | solution.py:59
  212.1 4.5 %fusion.36 = f32[16,28,768]{2,1,0:T(8,128)} fusion(bf16[16,128,768,1]{2,1,0,3:T(8,128)(2,1)S(1)} %bitcast.203, bf16[16,28,16,128]{3,2,1,0:T(8,128)(2,1)} %all-to-all-done.1), kind=kOutput, calls=%fused_computation.49 | convolution fusion | flops 1409286144 | bytes 6356992 | tf_op jit(solution)/shard_map/dot_general | solution.py:59
  218.3 2.0 copy.69
  220.2 7.8 %all-to-all-start.3 = ((bf16[16,28,16,128]{3,2,1,0:T(8,128)(2,1)}), bf16[16,28,16,128]{3,2,1,0:T(8,128)(2,1)}, u32[]{:S(2)}, u32[]{:S(2)}) async-start(bf16[16,28,16,128]{3,2,1,0:T(8,128)(2,1)} %copy.69), calls=%async_computation.3 | async-start | bytes 3670016 | tf_op jit(solution)/shard_map/all_to_all | solution.py:80
  228.1 43.4 %all-to-all-done.3 = bf16[16,28,16,128]{3,2,1,0:T(8,128)(2,1)} async-done(((bf16[16,28,16,128]{3,2,1,0:T(8,128)(2,1)}), bf16[16,28,16,128]{3,2,1,0:T(8,128)(2,1)}, u32[]{:S(2)}, u32[]{:S(2)}) %all-to-all-start.3) | async-done | bytes 1835040 | tf_op jit(solution)/shard_map/all_to_all | solution.py:80
  271.6 4.4 %fusion.6 = f32[16,28,768,1]{2,1,3,0:T(8,128)S(1)} fusion(bf16[768,16,128]{2,1,0:T(8,128)(2,1)} %bitcast.188, bf16[16,28,16,128]{3,2,1,0:T(8,128)(2,1)} %all-to-all-done.3), kind=kOutput, calls=%fused_computation.11 | convolution fusion | flops 1409286144 | bytes 6356992 | tf_op jit(solution)/shard_map/dot_general | solution.py:65
  276.0 2.2 fusion.61
  278.2 2.2 add_convert_fusion
  280.4 2.0 copy.72
  282.4 5.2 %all-to-all-start.4 = ((bf16[16,28,16,128]{3,2,1,0:T(8,128)(2,1)}), bf16[16,28,16,128]{3,2,1,0:T(8,128)(2,1)}, u32[]{:S(2)}, u32[]{:S(2)}) async-start(bf16[16,28,16,128]{3,2,1,0:T(8,128)(2,1)} %copy.72), calls=%async_computation.4 | async-start | bytes 3670016 | tf_op jit(solution)/shard_map/all_to_all | solution.py:80
  287.6 2.1 reshape.59
  289.6 40.3 %all-to-all-done.4 = bf16[16,28,16,128]{3,2,1,0:T(8,128)(2,1)} async-done(((bf16[16,28,16,128]{3,2,1,0:T(8,128)(2,1)}), bf16[16,28,16,128]{3,2,1,0:T(8,128)(2,1)}, u32[]{:S(2)}, u32[]{:S(2)}) %all-to-all-start.4) | async-done | bytes 1835040 | tf_op jit(solution)/shard_map/all_to_all | solution.py:80
  329.9 2.0 fusion.45
  331.9 1.4 fusion.56
  333.4 2.1 reshape.60
  (60 shorter events, 12.6 us)
Async XLA Ops:
  0.6 116.5 %copy-start = (bf16[1,1,2048,768]{3,2,1,0:T(8,128)(2,1)S(1)}, bf16[1,1,2048,768]{3,2,1,0:T(8,128)(2,1)}, u32[]{:S(2)}) copy-start(bf16[1,1,2048,768]{3,2,1,0:T(8,128)(2,1)} %param.18) | copy-start | bytes 9437188
  4.4 2.1 copy-start.10
  5.6 0.8 copy-start.1
  11.7 8.2 %copy-start.8 = (s32[1,128,2]{1,2,0:T(2,128)S(1)}, s32[1,128,2]{1,2,0:T(2,128)}, u32[]{:S(2)}) copy-start(s32[1,128,2]{1,2,0:T(2,128)} %param.14) | copy-start | bytes 3076
  11.7 90.2 %all-to-all-start = ((bf16[16,28,32,128]{3,2,1,0:T(8,128)(2,1)}), bf16[16,28,32,128]{3,2,1,0:T(8,128)(2,1)}, u32[]{:S(2)}, u32[]{:S(2)}) async-start(bf16[16,28,32,128]{3,2,1,0:T(8,128)(2,1)} %copy.54), calls=%async_computation | async-start | bytes 7340032 | tf_op jit(solution)/shard_map/all_to_all | solution.py:80
  22.1 2.3 copy-start.3
  101.9 47.1 %all-to-all-start.1 = ((bf16[16,28,16,128]{3,2,1,0:T(8,128)(2,1)}), bf16[16,28,16,128]{3,2,1,0:T(8,128)(2,1)}, u32[]{:S(2)}, u32[]{:S(2)}) async-start(bf16[16,28,16,128]{3,2,1,0:T(8,128)(2,1)} %copy.145), calls=%async_computation.1 | async-start | bytes 3670016 | tf_op jit(solution)/shard_map/all_to_all | solution.py:80
  107.1 5.6 %copy-start.4 = (bf16[96,8,16,128]{3,2,1,0:T(8,128)(2,1)S(1)}, bf16[96,8,16,128]{3,2,1,0:T(8,128)(2,1)}, u32[]{:S(2)}) copy-start(bf16[96,8,16,128]{3,2,1,0:T(8,128)(2,1)} %copy.95) | copy-start | bytes 9437188
  152.7 47.0 %all-to-all-start.2 = ((bf16[16,28,16,128]{3,2,1,0:T(8,128)(2,1)}), bf16[16,28,16,128]{3,2,1,0:T(8,128)(2,1)}, u32[]{:S(2)}, u32[]{:S(2)}) async-start(bf16[16,28,16,128]{3,2,1,0:T(8,128)(2,1)} %copy.63), calls=%async_computation.2 | async-start | bytes 3670016 | tf_op jit(solution)/shard_map/all_to_all | solution.py:80
  199.7 2.0 copy-start.2
  202.4 9.7 %copy-start.7 = (bf16[128,16,128]{2,1,0:T(8,128)(2,1)}, bf16[128,16,128]{2,1,0:T(8,128)(2,1)S(1)}, u32[]{:S(2)}) copy-start(bf16[128,16,128]{2,1,0:T(8,128)(2,1)S(1)} %fusion.57) | copy-start | bytes 1572868
  202.4 9.7 %copy-start.11 = (bf16[1,1,2048,768]{3,2,1,0:T(8,128)(2,1)S(1)}, bf16[1,1,2048,768]{3,2,1,0:T(8,128)(2,1)}, u32[]{:S(2)}) copy-start(bf16[1,1,2048,768]{3,2,1,0:T(8,128)(2,1)} %param.17) | copy-start | bytes 9437188
  202.4 14.2 %collective-permute-start = (bf16[128,16,128]{2,1,0:T(8,128)(2,1)S(1)}, bf16[128,16,128]{2,1,0:T(8,128)(2,1)S(1)}, u32[]{:S(2)}, u32[]{:S(2)}) collective-permute-start(bf16[128,16,128]{2,1,0:T(8,128)(2,1)S(1)} %fusion.57), channel_id=1, source_target_pairs={{16,0},{32,16},{48,32},{64,48},{80,64},{96,80},{112,96},{128,112},... | collective-permute-start | bytes 1572872 | tf_op jit(solution)/shard_map/ppermute | solution.py:11
  212.1 5.3 %copy-start.9 = (f32[1,128,2]{1,2,0:T(2,128)S(1)}, f32[1,128,2]{1,2,0:T(2,128)}, u32[]{:S(2)}) copy-start(f32[1,128,2]{1,2,0:T(2,128)} %param.16) | copy-start | bytes 3076
  216.6 0.8 copy-start.5
  220.2 51.3 %all-to-all-start.3 = ((bf16[16,28,16,128]{3,2,1,0:T(8,128)(2,1)}), bf16[16,28,16,128]{3,2,1,0:T(8,128)(2,1)}, u32[]{:S(2)}, u32[]{:S(2)}) async-start(bf16[16,28,16,128]{3,2,1,0:T(8,128)(2,1)} %copy.69), calls=%async_computation.3 | async-start | bytes 3670016 | tf_op jit(solution)/shard_map/all_to_all | solution.py:80
  271.6 4.4 %copy-start.12 = (bf16[1,1,2048,768]{3,2,1,0:T(8,128)(2,1)S(1)}, bf16[1,1,2048,768]{3,2,1,0:T(8,128)(2,1)}, u32[]{:S(2)}) copy-start(bf16[1,1,2048,768]{3,2,1,0:T(8,128)(2,1)} %param.17) | copy-start | bytes 9437188
  271.6 4.4 %copy-start.13 = (f32[16,28,768]{2,1,0:T(8,128)S(1)}, f32[16,28,768]{2,1,0:T(8,128)}, u32[]{:S(2)}) copy-start(f32[16,28,768]{2,1,0:T(8,128)} %fusion.36) | copy-start | bytes 4128772
  271.6 4.4 %copy-start.14 = (f32[16,28,768]{2,1,0:T(8,128)S(1)}, f32[16,28,768]{2,1,0:T(8,128)}, u32[]{:S(2)}) copy-start(f32[16,28,768]{2,1,0:T(8,128)} %fusion.39) | copy-start | bytes 4128772
  282.4 47.5 %all-to-all-start.4 = ((bf16[16,28,16,128]{3,2,1,0:T(8,128)(2,1)}), bf16[16,28,16,128]{3,2,1,0:T(8,128)(2,1)}, u32[]{:S(2)}, u32[]{:S(2)}) async-start(bf16[16,28,16,128]{3,2,1,0:T(8,128)(2,1)} %copy.72), calls=%async_computation.4 | async-start | bytes 3670016 | tf_op jit(solution)/shard_map/all_to_all | solution.py:80
  329.9 2.0 copy-start.6
